TPU v7x, 1024 devices: a whole 4x8x16 slice. The times are simulated.
1024 devices in a mesh: group: 64 (over y, z_hi, core), blk: 16 (over x, z_lo).
Axes of the slice: x: 4, y: 8, z: 16 (z_hi: 4, z_lo: 4; z = z_hi * 4 + z_lo), core: 2. Of those that a mesh axis runs over, the one named last changes fastest.
Arguments:
- informal: bfloat16 [131072, 1024], P(('group', 'blk')), may hold values from -6 to 6
- formal: bfloat16 [131072, 1024], P(('group', 'blk')), may hold values from -6 to 6
- labels: int32 [131072], P(('group', 'blk')), may hold values from 0 to 2047
- temp: float32 [], replicated, may hold values from 2 to 4
- bias: float32 [], replicated, may hold values from -3 to -1
Outputs:
- loss: float32 [131072], P(('group', 'blk'))
- grad_informal: float32 [131072, 1024], P(('group', 'blk'))
- grad_formal: float32 [131072, 1024], P(('group', 'blk'))
- grad_temp: float32 [], replicated
- grad_bias: float32 [], replicated
All inputs are finite; a program needn't handle non-finite values.
Results may differ from a plain program's by a relative error of at most 0.0025.
Values may be sent and summed in bfloat16 or wider, within the bound.
No kernel may reach another device: no remote copies, remote signals or barrier semaphores. Data moves between devices by JAX's collectives and lax.ppermute only.
A program may use at most 32 MiB of HBM per device.

v0:
```python
import math

import jax
import jax.numpy as jnp
from jax import lax
from jax.sharding import PartitionSpec as P


def from_behind(shard, axis, by):
    count = lax.axis_size(axis)
    return lax.ppermute(shard, axis, [(i, (i + by) % count) for i in range(count)])


def block_terms(carry, informal, formal, labels, pair, pair_labels, temp, bias):
    loss_sum, grad_x, grad_y, temp_sum, bias_sum = carry
    width = informal.shape[1]
    root = math.sqrt(width)
    scale = temp / root
    other_formal = pair[0]
    other_informal = pair[1]
    raw = (
        lax.dot_general(
            informal, other_formal, (((1,), (1,)), ((), ())), preferred_element_type=jnp.float32
        )
        / root
    )
    logits = temp * raw + bias
    sign = jnp.where(labels[:, None] == pair_labels[None, :], 1.0, -1.0).astype(jnp.float32)
    loss_sum = loss_sum + jnp.sum(jax.nn.softplus(-sign * logits), axis=1)
    slope = -sign * jax.nn.sigmoid(-sign * logits)
    weights = slope.astype(jnp.bfloat16)
    grad_x = grad_x + scale * jnp.dot(weights, other_formal, preferred_element_type=jnp.float32)
    temp_sum = temp_sum + jnp.sum(slope * raw)
    bias_sum = bias_sum + jnp.sum(slope)
    raw_back = (
        lax.dot_general(
            other_informal, formal, (((1,), (1,)), ((), ())), preferred_element_type=jnp.float32
        )
        / root
    )
    logits_back = temp * raw_back + bias
    sign_back = jnp.where(pair_labels[:, None] == labels[None, :], 1.0, -1.0).astype(jnp.float32)
    weights_back = (-sign_back * jax.nn.sigmoid(-sign_back * logits_back)).astype(jnp.bfloat16)
    grad_y = grad_y + scale * lax.dot_general(
        weights_back, other_informal, (((0,), (0,)), ((), ())), preferred_element_type=jnp.float32
    )
    return (loss_sum, grad_x, grad_y, temp_sum, bias_sum)


def on_device(informal, formal, labels, temp, bias):
    rows, width = informal.shape
    ngroup = lax.axis_size("group")
    nblk = lax.axis_size("blk")
    stacked = jnp.stack([formal, informal])
    zero_grad = jnp.zeros((rows, width), jnp.float32)
    start = (
        jnp.zeros((rows,), jnp.float32),
        zero_grad,
        zero_grad,
        jnp.float32(0.0),
        jnp.float32(0.0),
    )

    def turn(step, state):
        carry, pair, pair_labels = state
        carry = block_terms(carry, informal, formal, labels, pair, pair_labels, temp, bias)
        pair, pair_labels = from_behind((pair, pair_labels), "blk", 1)
        return (carry, pair, pair_labels)

    carry, pair, pair_labels = lax.fori_loop(0, nblk - 1, turn, (start, stacked, labels))
    carry = block_terms(carry, informal, formal, labels, pair, pair_labels, temp, bias)
    loss_sum, grad_x, grad_y, temp_sum, bias_sum = carry
    temp_total, bias_total = lax.psum((temp_sum, bias_sum), ("group", "blk"))
    set_size = rows * nblk
    total = jnp.float32(rows * nblk * ngroup) * jnp.float32(set_size)
    loss = loss_sum / set_size
    return (loss, grad_x, grad_y, temp_total / total, bias_total / total)


def solution(mesh):
    in_specs = (P(("group", "blk"), None), P(("group", "blk"), None), P(("group", "blk")), P(), P())
    out_specs = (
        P(("group", "blk")),
        P(("group", "blk"), None),
        P(("group", "blk"), None),
        P(),
        P(),
    )
    return jax.shard_map(
        on_device, mesh=mesh, in_specs=in_specs, out_specs=out_specs, check_vma=False
    )
```

profile of v0, /device:TPU:1, one launch (start us, length us, event | category | flops | bytes accessed | tf_op | source)
XLA Modules:
  0.0 402.9 jit_solution(12233906862093537832)
XLA Ops:
  3.1 244.7 %while.26 = (s32[]{:T(128)}, f32[128]{0:T(128)S(1)}, f32[128,1024]{1,0:T(8,128)S(1)}, f32[128,1024]{1,0:T(8,128)S(1)}, f32[]{:T(128)}, /*index=5*/f32[]{:T(128)}...) while((s32[]{:T(128)}, f32[128]{0:T(128)S(1)}, ...), condition=%wide.region_4.5_spmd.clone, body=%wide.region_0.4_spmd.clone.sunk | while | flops 135708800 | bytes 6958353 | solution.py:70
  3.2 4.8 %collective-permute-start = (bf16[2,128,1024]{2,1,0:T(8,128)(2,1)S(1)}, bf16[2,128,1024]{2,1,0:T(8,128)(2,1)S(1)}, u32[]{:S(2)}, u32[]{:S(2)}) collective-permute-start(bf16[2,128,1024]{2,1,0:T(8,128)(2,1)S(1)} %copy.30), channel_id=1, source_target_pairs={{0,1},{1,2},{2,3},{3,4},{4,5},{5,6},{6,7},{7,8},{8,9},{9,10},{10,1... | collective-permute-start | bytes 1572872 | tf_op jit(solution)/shard_map/while/body/eval_jaxpr/ppermute | solution.py:11
  8.0 4.0 collective-permute-start.1
  12.0 1.5 fusion.83
  14.6 1.3 fusion.86
  17.2 3.3 collective-permute-done.1
  20.5 2.2 collective-permute-start
  22.7 4.1 %collective-permute-start.1 = (s32[128]{0:T(128)S(1)}, s32[128]{0:T(128)S(1)}, u32[]{:S(2)}, u32[]{:S(2)}) collective-permute-start(s32[128]{0:T(128)S(1)} %copy.31), channel_id=1, source_target_pairs={{0,1},{1,2},{2,3},{3,4},{4,5},{5,6},{6,7},{7,8},{8,9},{9,10},{10,1... | collective-permute-start | bytes 1544 | tf_op jit(solution)/shard_map/while/body/eval_jaxpr/ppermute | solution.py:11
  26.8 1.5 fusion.83
  31.9 5.4 %collective-permute-done.1 = s32[128]{0:T(128)S(1)} collective-permute-done((s32[128]{0:T(128)S(1)}, s32[128]{0:T(128)S(1)}, u32[]{:S(2)}, u32[]{:S(2)}) %collective-permute-start.1) | collective-permute-done | bytes 544 | tf_op jit(solution)/shard_map/while/body/eval_jaxpr/ppermute | solution.py:11
  37.4 1.9 collective-permute-start
  39.3 1.9 collective-permute-start.1
  41.2 1.5 fusion.83
  46.4 8.1 %collective-permute-done.1 = s32[128]{0:T(128)S(1)} collective-permute-done((s32[128]{0:T(128)S(1)}, s32[128]{0:T(128)S(1)}, u32[]{:S(2)}, u32[]{:S(2)}) %collective-permute-start.1) | collective-permute-done | bytes 544 | tf_op jit(solution)/shard_map/while/body/eval_jaxpr/ppermute | solution.py:11
  54.5 1.9 collective-permute-start
  56.5 1.9 collective-permute-start.1
  58.4 1.5 fusion.83
  63.6 9.3 %collective-permute-done.1 = s32[128]{0:T(128)S(1)} collective-permute-done((s32[128]{0:T(128)S(1)}, s32[128]{0:T(128)S(1)}, u32[]{:S(2)}, u32[]{:S(2)}) %collective-permute-start.1) | collective-permute-done | bytes 544 | tf_op jit(solution)/shard_map/while/body/eval_jaxpr/ppermute | solution.py:11
  72.9 1.9 collective-permute-start
  74.8 1.9 collective-permute-start.1
  76.8 1.5 fusion.83
  81.9 10.5 %collective-permute-done.1 = s32[128]{0:T(128)S(1)} collective-permute-done((s32[128]{0:T(128)S(1)}, s32[128]{0:T(128)S(1)}, u32[]{:S(2)}, u32[]{:S(2)}) %collective-permute-start.1) | collective-permute-done | bytes 544 | tf_op jit(solution)/shard_map/while/body/eval_jaxpr/ppermute | solution.py:11
  92.5 1.9 collective-permute-start
  94.4 1.9 collective-permute-start.1
  96.4 1.5 fusion.83
  101.5 9.8 %collective-permute-done.1 = s32[128]{0:T(128)S(1)} collective-permute-done((s32[128]{0:T(128)S(1)}, s32[128]{0:T(128)S(1)}, u32[]{:S(2)}, u32[]{:S(2)}) %collective-permute-start.1) | collective-permute-done | bytes 544 | tf_op jit(solution)/shard_map/while/body/eval_jaxpr/ppermute | solution.py:11
  111.3 1.9 collective-permute-start
  113.3 1.9 collective-permute-start.1
  115.2 1.5 fusion.83
  120.4 8.8 %collective-permute-done.1 = s32[128]{0:T(128)S(1)} collective-permute-done((s32[128]{0:T(128)S(1)}, s32[128]{0:T(128)S(1)}, u32[]{:S(2)}, u32[]{:S(2)}) %collective-permute-start.1) | collective-permute-done | bytes 544 | tf_op jit(solution)/shard_map/while/body/eval_jaxpr/ppermute | solution.py:11
  129.2 1.9 collective-permute-start
  131.2 1.9 collective-permute-start.1
  133.1 1.5 fusion.83
  138.3 7.9 %collective-permute-done.1 = s32[128]{0:T(128)S(1)} collective-permute-done((s32[128]{0:T(128)S(1)}, s32[128]{0:T(128)S(1)}, u32[]{:S(2)}, u32[]{:S(2)}) %collective-permute-start.1) | collective-permute-done | bytes 544 | tf_op jit(solution)/shard_map/while/body/eval_jaxpr/ppermute | solution.py:11
  146.2 1.9 collective-permute-start
  148.2 1.9 collective-permute-start.1
  150.1 1.5 fusion.83
  155.2 7.0 %collective-permute-done.1 = s32[128]{0:T(128)S(1)} collective-permute-done((s32[128]{0:T(128)S(1)}, s32[128]{0:T(128)S(1)}, u32[]{:S(2)}, u32[]{:S(2)}) %collective-permute-start.1) | collective-permute-done | bytes 544 | tf_op jit(solution)/shard_map/while/body/eval_jaxpr/ppermute | solution.py:11
  162.2 1.9 collective-permute-start
  164.2 1.9 collective-permute-start.1
  166.1 1.5 fusion.83
  171.3 6.0 %collective-permute-done.1 = s32[128]{0:T(128)S(1)} collective-permute-done((s32[128]{0:T(128)S(1)}, s32[128]{0:T(128)S(1)}, u32[]{:S(2)}, u32[]{:S(2)}) %collective-permute-start.1) | collective-permute-done | bytes 544 | tf_op jit(solution)/shard_map/while/body/eval_jaxpr/ppermute | solution.py:11
  177.3 1.9 collective-permute-start
  179.3 1.9 collective-permute-start.1
  181.2 1.5 fusion.83
  186.3 4.9 %collective-permute-done.1 = s32[128]{0:T(128)S(1)} collective-permute-done((s32[128]{0:T(128)S(1)}, s32[128]{0:T(128)S(1)}, u32[]{:S(2)}, u32[]{:S(2)}) %collective-permute-start.1) | collective-permute-done | bytes 544 | tf_op jit(solution)/shard_map/while/body/eval_jaxpr/ppermute | solution.py:11
  191.3 1.9 collective-permute-start
  193.2 1.9 collective-permute-start.1
  195.2 1.5 fusion.83
  200.3 4.9 %collective-permute-done.1 = s32[128]{0:T(128)S(1)} collective-permute-done((s32[128]{0:T(128)S(1)}, s32[128]{0:T(128)S(1)}, u32[]{:S(2)}, u32[]{:S(2)}) %collective-permute-start.1) | collective-permute-done | bytes 544 | tf_op jit(solution)/shard_map/while/body/eval_jaxpr/ppermute | solution.py:11
  205.3 1.9 collective-permute-start
  207.2 1.9 collective-permute-start.1
  209.1 1.5 fusion.83
  214.3 4.9 %collective-permute-done.1 = s32[128]{0:T(128)S(1)} collective-permute-done((s32[128]{0:T(128)S(1)}, s32[128]{0:T(128)S(1)}, u32[]{:S(2)}, u32[]{:S(2)}) %collective-permute-start.1) | collective-permute-done | bytes 544 | tf_op jit(solution)/shard_map/while/body/eval_jaxpr/ppermute | solution.py:11
  219.2 1.9 collective-permute-start
  221.2 1.9 collective-permute-start.1
  223.1 1.5 fusion.83
  228.2 4.9 %collective-permute-done.1 = s32[128]{0:T(128)S(1)} collective-permute-done((s32[128]{0:T(128)S(1)}, s32[128]{0:T(128)S(1)}, u32[]{:S(2)}, u32[]{:S(2)}) %collective-permute-start.1) | collective-permute-done | bytes 544 | tf_op jit(solution)/shard_map/while/body/eval_jaxpr/ppermute | solution.py:11
  233.2 1.9 collective-permute-start
  235.1 1.9 collective-permute-start.1
  237.1 1.5 fusion.83
  242.2 5.7 %collective-permute-done.1 = s32[128]{0:T(128)S(1)} collective-permute-done((s32[128]{0:T(128)S(1)}, s32[128]{0:T(128)S(1)}, u32[]{:S(2)}, u32[]{:S(2)}) %collective-permute-start.1) | collective-permute-done | bytes 544 | tf_op jit(solution)/shard_map/while/body/eval_jaxpr/ppermute | solution.py:11
  251.2 145.2 %all-reduce = (f32[]{:T(128)}, f32[]{:T(128)}) all-reduce(f32[]{:T(128)S(6)} %add.125, f32[]{:T(128)S(6)} %add.126), channel_id=1, replica_groups=mesh['group'=64,'blk'=16] {'group','blk'}, use_global_device_ids=true, to_apply=%region_7.8 | all-reduce | flops 2 | bytes 16 | tf_op jit(solution)/shard_map/psum | solution.py:73
  397.8 1.3 fusion.35
  (109 shorter events, 38.6 us)
Async XLA Ops:
  1.3 1.8 copy-start
  1.3 1.8 copy-start.1
  2.5 0.7 copy-start.2
  3.2 17.3 %collective-permute-start = (bf16[2,128,1024]{2,1,0:T(8,128)(2,1)S(1)}, bf16[2,128,1024]{2,1,0:T(8,128)(2,1)S(1)}, u32[]{:S(2)}, u32[]{:S(2)}) collective-permute-start(bf16[2,128,1024]{2,1,0:T(8,128)(2,1)S(1)} %copy.30), channel_id=1, source_target_pairs={{0,1},{1,2},{2,3},{3,4},{4,5},{5,6},{6,7},{7,8},{8,9},{9,10},{10,1... | collective-permute-start | bytes 1572872 | tf_op jit(solution)/shard_map/while/body/eval_jaxpr/ppermute | solution.py:11
  8.0 12.4 %collective-permute-start.1 = (s32[128]{0:T(128)S(1)}, s32[128]{0:T(128)S(1)}, u32[]{:S(2)}, u32[]{:S(2)}) collective-permute-start(s32[128]{0:T(128)S(1)} %copy.31), channel_id=1, source_target_pairs={{0,1},{1,2},{2,3},{3,4},{4,5},{5,6},{6,7},{7,8},{8,9},{9,10},{10,1... | collective-permute-start | bytes 1544 | tf_op jit(solution)/shard_map/while/body/eval_jaxpr/ppermute | solution.py:11
  20.5 16.8 %collective-permute-start = (bf16[2,128,1024]{2,1,0:T(8,128)(2,1)S(1)}, bf16[2,128,1024]{2,1,0:T(8,128)(2,1)S(1)}, u32[]{:S(2)}, u32[]{:S(2)}) collective-permute-start(bf16[2,128,1024]{2,1,0:T(8,128)(2,1)S(1)} %copy.30), channel_id=1, source_target_pairs={{0,1},{1,2},{2,3},{3,4},{4,5},{5,6},{6,7},{7,8},{8,9},{9,10},{10,1... | collective-permute-start | bytes 1572872 | tf_op jit(solution)/shard_map/while/body/eval_jaxpr/ppermute | solution.py:11
  22.7 14.6 %collective-permute-start.1 = (s32[128]{0:T(128)S(1)}, s32[128]{0:T(128)S(1)}, u32[]{:S(2)}, u32[]{:S(2)}) collective-permute-start(s32[128]{0:T(128)S(1)} %copy.31), channel_id=1, source_target_pairs={{0,1},{1,2},{2,3},{3,4},{4,5},{5,6},{6,7},{7,8},{8,9},{9,10},{10,1... | collective-permute-start | bytes 1544 | tf_op jit(solution)/shard_map/while/body/eval_jaxpr/ppermute | solution.py:11
  37.4 17.2 %collective-permute-start = (bf16[2,128,1024]{2,1,0:T(8,128)(2,1)S(1)}, bf16[2,128,1024]{2,1,0:T(8,128)(2,1)S(1)}, u32[]{:S(2)}, u32[]{:S(2)}) collective-permute-start(bf16[2,128,1024]{2,1,0:T(8,128)(2,1)S(1)} %copy.30), channel_id=1, source_target_pairs={{0,1},{1,2},{2,3},{3,4},{4,5},{5,6},{6,7},{7,8},{8,9},{9,10},{10,1... | collective-permute-start | bytes 1572872 | tf_op jit(solution)/shard_map/while/body/eval_jaxpr/ppermute | solution.py:11
  39.3 15.2 %collective-permute-start.1 = (s32[128]{0:T(128)S(1)}, s32[128]{0:T(128)S(1)}, u32[]{:S(2)}, u32[]{:S(2)}) collective-permute-start(s32[128]{0:T(128)S(1)} %copy.31), channel_id=1, source_target_pairs={{0,1},{1,2},{2,3},{3,4},{4,5},{5,6},{6,7},{7,8},{8,9},{9,10},{10,1... | collective-permute-start | bytes 1544 | tf_op jit(solution)/shard_map/while/body/eval_jaxpr/ppermute | solution.py:11
  54.5 18.3 %collective-permute-start = (bf16[2,128,1024]{2,1,0:T(8,128)(2,1)S(1)}, bf16[2,128,1024]{2,1,0:T(8,128)(2,1)S(1)}, u32[]{:S(2)}, u32[]{:S(2)}) collective-permute-start(bf16[2,128,1024]{2,1,0:T(8,128)(2,1)S(1)} %copy.30), channel_id=1, source_target_pairs={{0,1},{1,2},{2,3},{3,4},{4,5},{5,6},{6,7},{7,8},{8,9},{9,10},{10,1... | collective-permute-start | bytes 1572872 | tf_op jit(solution)/shard_map/while/body/eval_jaxpr/ppermute | solution.py:11
  56.5 16.4 %collective-permute-start.1 = (s32[128]{0:T(128)S(1)}, s32[128]{0:T(128)S(1)}, u32[]{:S(2)}, u32[]{:S(2)}) collective-permute-start(s32[128]{0:T(128)S(1)} %copy.31), channel_id=1, source_target_pairs={{0,1},{1,2},{2,3},{3,4},{4,5},{5,6},{6,7},{7,8},{8,9},{9,10},{10,1... | collective-permute-start | bytes 1544 | tf_op jit(solution)/shard_map/while/body/eval_jaxpr/ppermute | solution.py:11
  72.9 19.6 %collective-permute-start = (bf16[2,128,1024]{2,1,0:T(8,128)(2,1)S(1)}, bf16[2,128,1024]{2,1,0:T(8,128)(2,1)S(1)}, u32[]{:S(2)}, u32[]{:S(2)}) collective-permute-start(bf16[2,128,1024]{2,1,0:T(8,128)(2,1)S(1)} %copy.30), channel_id=1, source_target_pairs={{0,1},{1,2},{2,3},{3,4},{4,5},{5,6},{6,7},{7,8},{8,9},{9,10},{10,1... | collective-permute-start | bytes 1572872 | tf_op jit(solution)/shard_map/while/body/eval_jaxpr/ppermute | solution.py:11
  74.8 17.6 %collective-permute-start.1 = (s32[128]{0:T(128)S(1)}, s32[128]{0:T(128)S(1)}, u32[]{:S(2)}, u32[]{:S(2)}) collective-permute-start(s32[128]{0:T(128)S(1)} %copy.31), channel_id=1, source_target_pairs={{0,1},{1,2},{2,3},{3,4},{4,5},{5,6},{6,7},{7,8},{8,9},{9,10},{10,1... | collective-permute-start | bytes 1544 | tf_op jit(solution)/shard_map/while/body/eval_jaxpr/ppermute | solution.py:11
  92.5 18.8 %collective-permute-start = (bf16[2,128,1024]{2,1,0:T(8,128)(2,1)S(1)}, bf16[2,128,1024]{2,1,0:T(8,128)(2,1)S(1)}, u32[]{:S(2)}, u32[]{:S(2)}) collective-permute-start(bf16[2,128,1024]{2,1,0:T(8,128)(2,1)S(1)} %copy.30), channel_id=1, source_target_pairs={{0,1},{1,2},{2,3},{3,4},{4,5},{5,6},{6,7},{7,8},{8,9},{9,10},{10,1... | collective-permute-start | bytes 1572872 | tf_op jit(solution)/shard_map/while/body/eval_jaxpr/ppermute | solution.py:11
  94.4 16.9 %collective-permute-start.1 = (s32[128]{0:T(128)S(1)}, s32[128]{0:T(128)S(1)}, u32[]{:S(2)}, u32[]{:S(2)}) collective-permute-start(s32[128]{0:T(128)S(1)} %copy.31), channel_id=1, source_target_pairs={{0,1},{1,2},{2,3},{3,4},{4,5},{5,6},{6,7},{7,8},{8,9},{9,10},{10,1... | collective-permute-start | bytes 1544 | tf_op jit(solution)/shard_map/while/body/eval_jaxpr/ppermute | solution.py:11
  111.3 17.9 %collective-permute-start = (bf16[2,128,1024]{2,1,0:T(8,128)(2,1)S(1)}, bf16[2,128,1024]{2,1,0:T(8,128)(2,1)S(1)}, u32[]{:S(2)}, u32[]{:S(2)}) collective-permute-start(bf16[2,128,1024]{2,1,0:T(8,128)(2,1)S(1)} %copy.30), channel_id=1, source_target_pairs={{0,1},{1,2},{2,3},{3,4},{4,5},{5,6},{6,7},{7,8},{8,9},{9,10},{10,1... | collective-permute-start | bytes 1572872 | tf_op jit(solution)/shard_map/while/body/eval_jaxpr/ppermute | solution.py:11
  113.3 15.9 %collective-permute-start.1 = (s32[128]{0:T(128)S(1)}, s32[128]{0:T(128)S(1)}, u32[]{:S(2)}, u32[]{:S(2)}) collective-permute-start(s32[128]{0:T(128)S(1)} %copy.31), channel_id=1, source_target_pairs={{0,1},{1,2},{2,3},{3,4},{4,5},{5,6},{6,7},{7,8},{8,9},{9,10},{10,1... | collective-permute-start | bytes 1544 | tf_op jit(solution)/shard_map/while/body/eval_jaxpr/ppermute | solution.py:11
  129.2 16.9 %collective-permute-start = (bf16[2,128,1024]{2,1,0:T(8,128)(2,1)S(1)}, bf16[2,128,1024]{2,1,0:T(8,128)(2,1)S(1)}, u32[]{:S(2)}, u32[]{:S(2)}) collective-permute-start(bf16[2,128,1024]{2,1,0:T(8,128)(2,1)S(1)} %copy.30), channel_id=1, source_target_pairs={{0,1},{1,2},{2,3},{3,4},{4,5},{5,6},{6,7},{7,8},{8,9},{9,10},{10,1... | collective-permute-start | bytes 1572872 | tf_op jit(solution)/shard_map/while/body/eval_jaxpr/ppermute | solution.py:11
  131.2 15.0 %collective-permute-start.1 = (s32[128]{0:T(128)S(1)}, s32[128]{0:T(128)S(1)}, u32[]{:S(2)}, u32[]{:S(2)}) collective-permute-start(s32[128]{0:T(128)S(1)} %copy.31), channel_id=1, source_target_pairs={{0,1},{1,2},{2,3},{3,4},{4,5},{5,6},{6,7},{7,8},{8,9},{9,10},{10,1... | collective-permute-start | bytes 1544 | tf_op jit(solution)/shard_map/while/body/eval_jaxpr/ppermute | solution.py:11
  146.2 16.0 %collective-permute-start = (bf16[2,128,1024]{2,1,0:T(8,128)(2,1)S(1)}, bf16[2,128,1024]{2,1,0:T(8,128)(2,1)S(1)}, u32[]{:S(2)}, u32[]{:S(2)}) collective-permute-start(bf16[2,128,1024]{2,1,0:T(8,128)(2,1)S(1)} %copy.30), channel_id=1, source_target_pairs={{0,1},{1,2},{2,3},{3,4},{4,5},{5,6},{6,7},{7,8},{8,9},{9,10},{10,1... | collective-permute-start | bytes 1572872 | tf_op jit(solution)/shard_map/while/body/eval_jaxpr/ppermute | solution.py:11
  148.2 14.0 %collective-permute-start.1 = (s32[128]{0:T(128)S(1)}, s32[128]{0:T(128)S(1)}, u32[]{:S(2)}, u32[]{:S(2)}) collective-permute-start(s32[128]{0:T(128)S(1)} %copy.31), channel_id=1, source_target_pairs={{0,1},{1,2},{2,3},{3,4},{4,5},{5,6},{6,7},{7,8},{8,9},{9,10},{10,1... | collective-permute-start | bytes 1544 | tf_op jit(solution)/shard_map/while/body/eval_jaxpr/ppermute | solution.py:11
  162.2 15.0 %collective-permute-start = (bf16[2,128,1024]{2,1,0:T(8,128)(2,1)S(1)}, bf16[2,128,1024]{2,1,0:T(8,128)(2,1)S(1)}, u32[]{:S(2)}, u32[]{:S(2)}) collective-permute-start(bf16[2,128,1024]{2,1,0:T(8,128)(2,1)S(1)} %copy.30), channel_id=1, source_target_pairs={{0,1},{1,2},{2,3},{3,4},{4,5},{5,6},{6,7},{7,8},{8,9},{9,10},{10,1... | collective-permute-start | bytes 1572872 | tf_op jit(solution)/shard_map/while/body/eval_jaxpr/ppermute | solution.py:11
  164.2 13.1 %collective-permute-start.1 = (s32[128]{0:T(128)S(1)}, s32[128]{0:T(128)S(1)}, u32[]{:S(2)}, u32[]{:S(2)}) collective-permute-start(s32[128]{0:T(128)S(1)} %copy.31), channel_id=1, source_target_pairs={{0,1},{1,2},{2,3},{3,4},{4,5},{5,6},{6,7},{7,8},{8,9},{9,10},{10,1... | collective-permute-start | bytes 1544 | tf_op jit(solution)/shard_map/while/body/eval_jaxpr/ppermute | solution.py:11
  177.3 13.9 %collective-permute-start = (bf16[2,128,1024]{2,1,0:T(8,128)(2,1)S(1)}, bf16[2,128,1024]{2,1,0:T(8,128)(2,1)S(1)}, u32[]{:S(2)}, u32[]{:S(2)}) collective-permute-start(bf16[2,128,1024]{2,1,0:T(8,128)(2,1)S(1)} %copy.30), channel_id=1, source_target_pairs={{0,1},{1,2},{2,3},{3,4},{4,5},{5,6},{6,7},{7,8},{8,9},{9,10},{10,1... | collective-permute-start | bytes 1572872 | tf_op jit(solution)/shard_map/while/body/eval_jaxpr/ppermute | solution.py:11
  179.3 12.0 %collective-permute-start.1 = (s32[128]{0:T(128)S(1)}, s32[128]{0:T(128)S(1)}, u32[]{:S(2)}, u32[]{:S(2)}) collective-permute-start(s32[128]{0:T(128)S(1)} %copy.31), channel_id=1, source_target_pairs={{0,1},{1,2},{2,3},{3,4},{4,5},{5,6},{6,7},{7,8},{8,9},{9,10},{10,1... | collective-permute-start | bytes 1544 | tf_op jit(solution)/shard_map/while/body/eval_jaxpr/ppermute | solution.py:11
  191.3 13.9 %collective-permute-start = (bf16[2,128,1024]{2,1,0:T(8,128)(2,1)S(1)}, bf16[2,128,1024]{2,1,0:T(8,128)(2,1)S(1)}, u32[]{:S(2)}, u32[]{:S(2)}) collective-permute-start(bf16[2,128,1024]{2,1,0:T(8,128)(2,1)S(1)} %copy.30), channel_id=1, source_target_pairs={{0,1},{1,2},{2,3},{3,4},{4,5},{5,6},{6,7},{7,8},{8,9},{9,10},{10,1... | collective-permute-start | bytes 1572872 | tf_op jit(solution)/shard_map/while/body/eval_jaxpr/ppermute | solution.py:11
  193.2 12.0 %collective-permute-start.1 = (s32[128]{0:T(128)S(1)}, s32[128]{0:T(128)S(1)}, u32[]{:S(2)}, u32[]{:S(2)}) collective-permute-start(s32[128]{0:T(128)S(1)} %copy.31), channel_id=1, source_target_pairs={{0,1},{1,2},{2,3},{3,4},{4,5},{5,6},{6,7},{7,8},{8,9},{9,10},{10,1... | collective-permute-start | bytes 1544 | tf_op jit(solution)/shard_map/while/body/eval_jaxpr/ppermute | solution.py:11
  205.3 13.9 %collective-permute-start = (bf16[2,128,1024]{2,1,0:T(8,128)(2,1)S(1)}, bf16[2,128,1024]{2,1,0:T(8,128)(2,1)S(1)}, u32[]{:S(2)}, u32[]{:S(2)}) collective-permute-start(bf16[2,128,1024]{2,1,0:T(8,128)(2,1)S(1)} %copy.30), channel_id=1, source_target_pairs={{0,1},{1,2},{2,3},{3,4},{4,5},{5,6},{6,7},{7,8},{8,9},{9,10},{10,1... | collective-permute-start | bytes 1572872 | tf_op jit(solution)/shard_map/while/body/eval_jaxpr/ppermute | solution.py:11
  207.2 12.0 %collective-permute-start.1 = (s32[128]{0:T(128)S(1)}, s32[128]{0:T(128)S(1)}, u32[]{:S(2)}, u32[]{:S(2)}) collective-permute-start(s32[128]{0:T(128)S(1)} %copy.31), channel_id=1, source_target_pairs={{0,1},{1,2},{2,3},{3,4},{4,5},{5,6},{6,7},{7,8},{8,9},{9,10},{10,1... | collective-permute-start | bytes 1544 | tf_op jit(solution)/shard_map/while/body/eval_jaxpr/ppermute | solution.py:11
  219.2 13.9 %collective-permute-start = (bf16[2,128,1024]{2,1,0:T(8,128)(2,1)S(1)}, bf16[2,128,1024]{2,1,0:T(8,128)(2,1)S(1)}, u32[]{:S(2)}, u32[]{:S(2)}) collective-permute-start(bf16[2,128,1024]{2,1,0:T(8,128)(2,1)S(1)} %copy.30), channel_id=1, source_target_pairs={{0,1},{1,2},{2,3},{3,4},{4,5},{5,6},{6,7},{7,8},{8,9},{9,10},{10,1... | collective-permute-start | bytes 1572872 | tf_op jit(solution)/shard_map/while/body/eval_jaxpr/ppermute | solution.py:11
  221.2 12.0 %collective-permute-start.1 = (s32[128]{0:T(128)S(1)}, s32[128]{0:T(128)S(1)}, u32[]{:S(2)}, u32[]{:S(2)}) collective-permute-start(s32[128]{0:T(128)S(1)} %copy.31), channel_id=1, source_target_pairs={{0,1},{1,2},{2,3},{3,4},{4,5},{5,6},{6,7},{7,8},{8,9},{9,10},{10,1... | collective-permute-start | bytes 1544 | tf_op jit(solution)/shard_map/while/body/eval_jaxpr/ppermute | solution.py:11
  233.2 14.7 %collective-permute-start = (bf16[2,128,1024]{2,1,0:T(8,128)(2,1)S(1)}, bf16[2,128,1024]{2,1,0:T(8,128)(2,1)S(1)}, u32[]{:S(2)}, u32[]{:S(2)}) collective-permute-start(bf16[2,128,1024]{2,1,0:T(8,128)(2,1)S(1)} %copy.30), channel_id=1, source_target_pairs={{0,1},{1,2},{2,3},{3,4},{4,5},{5,6},{6,7},{7,8},{8,9},{9,10},{10,1... | collective-permute-start | bytes 1572872 | tf_op jit(solution)/shard_map/while/body/eval_jaxpr/ppermute | solution.py:11
  235.1 12.7 %collective-permute-start.1 = (s32[128]{0:T(128)S(1)}, s32[128]{0:T(128)S(1)}, u32[]{:S(2)}, u32[]{:S(2)}) collective-permute-start(s32[128]{0:T(128)S(1)} %copy.31), channel_id=1, source_target_pairs={{0,1},{1,2},{2,3},{3,4},{4,5},{5,6},{6,7},{7,8},{8,9},{9,10},{10,1... | collective-permute-start | bytes 1544 | tf_op jit(solution)/shard_map/while/body/eval_jaxpr/ppermute | solution.py:11
where the time goes:
time: 405 us; the launch traced here: 403 us
  blocking collectives  145 us (36%)
  waiting for transfers between devices  101 us (25%)
  starting transfers between devices  65 us (16%)
  matrix products  59.8 us (15%)
  loops' own time  20.3 us (5%)
  between operations  6.89 us (2%)
    psum x1, blocking collectives, on_device(): temp_total, bias_total = lax.psum((temp_sum, bias_sum), ('group', 'blk'))  145 us
    ppermute x30, waiting for transfers between devices, from_behind(): lax.ppermute(shard, axis, [(i, (i + by) % count) for i in range(count)])  101 us
    ppermute x30, starting transfers between devices, from_behind(): lax.ppermute(shard, axis, [(i, (i + by) % count) for i in range(count)])  65 us
    dot_general x16, matrix products, block_terms(): lax.dot_general(informal, other_formal, (((1,), (1,)), ((), ())), preferr...  23.1 us
    dot_general x16, matrix products, block_terms(): lax.dot_general(weights_back, other_informal, (((0,), (0,)), ((), ())), p...  20.4 us
    another operation x1, loops' own time, on_device(): lax.fori_loop(0, nblk - 1, turn, (start, stacked, labels))  20.3 us
    dot_general x16, matrix products, block_terms(): jnp.dot(weights, other_formal, preferred_element_type=jnp.float32)  16.3 us
  transfers between devices with their start and end apart: 30, of which 15 were waited for; matrix products, arithmetic and copies ran while one was open for 14% of the time, Pallas kernels for 0%

commit v1 on v0

v1 whole, which is shorter than its diff:
```python
import math

import jax
import jax.numpy as jnp
from jax import lax
from jax.sharding import Mesh
from jax.sharding import PartitionSpec as P


def shifted(value, axis, by):
    count = lax.axis_size(axis)
    return lax.ppermute(value, axis, [(i, (i + by) % count) for i in range(count)])


def gather_by_shift(value, axis):
    count = lax.axis_size(axis)
    return jnp.concatenate([value] + [shifted(value, axis, k) for k in range(1, count)], axis=0)


def reduce_by_shift(parts, axis):
    count = lax.axis_size(axis)
    total = parts[0]
    for k in range(1, count):
        total = total + shifted(parts[k], axis, -k)
    return total


def total_sums(sums, axes):
    for axis in axes:
        count = lax.axis_size(axis)
        step = 1
        while step < count:
            if step * 4 <= count:
                got = [lax.ppermute(sums, axis, [(i, i ^ (a * step)) for i in range(count)]) for a in (1, 2, 3)]
                sums = (sums + got[0]) + (got[1] + got[2])
                step *= 4
            else:
                sums = sums + lax.ppermute(sums, axis, [(i, i ^ step) for i in range(count)])
                step *= 2
    return sums


def on_device(informal, formal, labels, temp, bias):
    rows, width = informal.shape
    ngroup = lax.axis_size("group")
    nrow = lax.axis_size("bz")
    ncol = lax.axis_size("bx")
    root = math.sqrt(width)
    scale = temp / root
    row_informal = gather_by_shift(informal, "bz")
    row_labels = gather_by_shift(labels, "bz")
    col_formal = gather_by_shift(formal, "bx")
    col_labels = gather_by_shift(labels, "bx")
    raw = lax.dot_general(row_informal, col_formal, (((1,), (1,)), ((), ())), preferred_element_type=jnp.float32) / root
    logits = temp * raw + bias
    sign = jnp.where(row_labels[:, None] == col_labels[None, :], 1.0, -1.0).astype(jnp.float32)
    loss_part = jnp.sum(jax.nn.softplus(-sign * logits), axis=1)
    slope = -sign * jax.nn.sigmoid(-sign * logits)
    weights = slope.astype(jnp.bfloat16)
    grad_x_part = jnp.dot(weights, col_formal, preferred_element_type=jnp.float32)
    grad_y_part = lax.dot_general(weights, row_informal, (((0,), (0,)), ((), ())), preferred_element_type=jnp.float32)
    sums = total_sums(jnp.stack([jnp.sum(slope * raw), jnp.sum(slope)]), ("group", "bx", "bz"))
    loss_sum = reduce_by_shift(loss_part.reshape(nrow, rows), "bz")
    grad_x = scale * reduce_by_shift(grad_x_part.reshape(nrow, rows, width), "bz")
    grad_y = scale * reduce_by_shift(grad_y_part.reshape(ncol, rows, width), "bx")
    set_size = rows * nrow * ncol
    total = jnp.float32(set_size * ngroup) * jnp.float32(set_size)
    loss = loss_sum / set_size
    return (loss, grad_x, grad_y, sums[0] / total, sums[1] / total)


def split_blk(mesh):
    blk = mesh.devices[0]
    nx = len({d.coords[0] for d in blk})
    grid = mesh.devices.reshape(mesh.shape["group"], nx, blk.size // nx)
    return Mesh(grid, ("group", "bx", "bz"))


def solution(mesh):
    fine = split_blk(mesh)
    rowspec = ("group", "bx", "bz")
    in_specs = (P(rowspec, None), P(rowspec, None), P(rowspec), P(), P())
    out_specs = (P(rowspec), P(rowspec, None), P(rowspec, None), P(), P())
    return jax.shard_map(on_device, mesh=fine, in_specs=in_specs, out_specs=out_specs, check_vma=False)
```

time: 405 us -> 236 us (0.58)
  the two profiles are of different devices: /device:TPU:1 before, /device:TPU:80 now
where the time goes in v1:
time: 236 us; the launch traced here: 235 us
  starting transfers between devices  156 us (66%)
  waiting for transfers between devices  59.4 us (25%)
  between operations  6.01 us (3%)
  other arithmetic  5.85 us (2%)
  matrix products  4.5 us (2%)
  local copies, waits for them, and re-layouts  2.99 us (1%)
    ppermute x15, starting transfers between devices, total_sums(): lax.ppermute(sums, axis, [(i, i ^ a * step) for i in range(count)])  81.1 us
    ppermute x21, starting transfers between devices, shifted(): lax.ppermute(value, axis, [(i, (i + by) % count) for i in range(count)])  75.1 us
    ppermute x15, waiting for transfers between devices, total_sums(): lax.ppermute(sums, axis, [(i, i ^ a * step) for i in range(count)])  45.6 us
    ppermute x21, waiting for transfers between devices, shifted(): lax.ppermute(value, axis, [(i, (i + by) % count) for i in range(count)])  13.8 us
  transfers between devices with their start and end apart: 36, of which 14 were waited for; matrix products, arithmetic and copies ran while one was open for 4% of the time, Pallas kernels for 0%

profile of v1, /device:TPU:80, one launch (start us, length us, event | category | flops | bytes accessed | tf_op | source)
XLA Modules:
  0.0 234.9 jit_solution(9193566832416466887)
XLA Ops:
  0.6 3.4 %collective-permute-start.3 = (s32[128]{0:T(128)}, s32[128]{0:T(128)S(1)}, u32[]{:S(2)}, u32[]{:S(2)}) collective-permute-start(s32[128]{0:T(128)} %param.7), channel_id=1, source_target_pairs={{0,4},{4,8},{8,12},{12,0},{1,5},{5,9},{9,13},{13,1},{2,6},{6,10},{... | collective-permute-start | bytes 1544 | tf_op jit(solution)/shard_map/ppermute | solution.py:12
  4.0 1.9 collective-permute-start.2
  6.0 6.1 %collective-permute-start.1 = (s32[128]{0:T(128)}, s32[128]{0:T(128)S(1)}, u32[]{:S(2)}, u32[]{:S(2)}) collective-permute-start(s32[128]{0:T(128)} %param.7), channel_id=1, source_target_pairs={{0,2},{1,3},{2,0},{3,1},{4,6},{5,7},{6,4},{7,5},{8,10},{9,11},{10,... | collective-permute-start | bytes 1544 | tf_op jit(solution)/shard_map/ppermute | solution.py:12
  12.1 1.9 collective-permute-start.7
  14.0 4.8 %collective-permute-start.6 = (bf16[128,1024]{1,0:T(8,128)(2,1)}, bf16[128,1024]{1,0:T(8,128)(2,1)S(1)}, u32[]{:S(2)}, u32[]{:S(2)}) collective-permute-start(bf16[128,1024]{1,0:T(8,128)(2,1)} %param.5), channel_id=1, source_target_pairs={{0,1},{1,2},{2,3},{3,0},{4,5},{5,6},{6,7},{7,4},{8,9},{9,10},{10,1... | collective-permute-start | bytes 786440 | tf_op jit(solution)/shard_map/ppermute | solution.py:12
  18.8 1.0 constant_dynamic-update-slice_fusion.3
  19.8 1.0 constant_dynamic-update-slice_fusion.7
  20.8 2.5 %collective-permute-start = (s32[128]{0:T(128)}, s32[128]{0:T(128)S(1)}, u32[]{:S(2)}, u32[]{:S(2)}) collective-permute-start(s32[128]{0:T(128)} %param.7), channel_id=1, source_target_pairs={{0,1},{1,2},{2,3},{3,0},{4,5},{5,6},{6,7},{7,4},{8,9},{9,10},{10,1... | collective-permute-start | bytes 1544 | tf_op jit(solution)/shard_map/ppermute | solution.py:12
  23.3 4.6 %collective-permute-start.4 = (s32[128]{0:T(128)}, s32[128]{0:T(128)S(1)}, u32[]{:S(2)}, u32[]{:S(2)}) collective-permute-start(s32[128]{0:T(128)} %param.7), channel_id=1, source_target_pairs={{0,8},{4,12},{8,0},{12,4},{1,9},{5,13},{9,1},{13,5},{2,10},{6,14},... | collective-permute-start | bytes 1544 | tf_op jit(solution)/shard_map/ppermute | solution.py:12
  27.9 3.3 %collective-permute-start.5 = (s32[128]{0:T(128)}, s32[128]{0:T(128)S(1)}, u32[]{:S(2)}, u32[]{:S(2)}) collective-permute-start(s32[128]{0:T(128)} %param.7), channel_id=1, source_target_pairs={{0,12},{4,0},{8,4},{12,8},{1,13},{5,1},{9,5},{13,9},{2,14},{6,2},{... | collective-permute-start | bytes 1544 | tf_op jit(solution)/shard_map/ppermute | solution.py:12
  32.6 3.4 %collective-permute-start.8 = (bf16[128,1024]{1,0:T(8,128)(2,1)}, bf16[128,1024]{1,0:T(8,128)(2,1)S(1)}, u32[]{:S(2)}, u32[]{:S(2)}) collective-permute-start(bf16[128,1024]{1,0:T(8,128)(2,1)} %param.5), channel_id=1, source_target_pairs={{0,3},{1,0},{2,1},{3,2},{4,7},{5,4},{6,5},{7,6},{8,11},{9,8},{10,9... | collective-permute-start | bytes 786440 | tf_op jit(solution)/shard_map/ppermute | solution.py:12
  36.0 2.4 %collective-permute-start.10 = (bf16[128,1024]{1,0:T(8,128)(2,1)}, bf16[128,1024]{1,0:T(8,128)(2,1)S(1)}, u32[]{:S(2)}, u32[]{:S(2)}) collective-permute-start(bf16[128,1024]{1,0:T(8,128)(2,1)} %param.6), channel_id=1, source_target_pairs={{0,8},{4,12},{8,0},{12,4},{1,9},{5,13},{9,1},{13,5},{2,10},{6,14},... | collective-permute-start | bytes 786440 | tf_op jit(solution)/shard_map/ppermute | solution.py:12
  38.4 2.3 collective-permute-start.9
  40.7 0.7 fusion.12
  41.4 4.8 %collective-permute-start.11 = (bf16[128,1024]{1,0:T(8,128)(2,1)}, bf16[128,1024]{1,0:T(8,128)(2,1)S(1)}, u32[]{:S(2)}, u32[]{:S(2)}) collective-permute-start(bf16[128,1024]{1,0:T(8,128)(2,1)} %param.6), channel_id=1, source_target_pairs={{0,12},{4,0},{8,4},{12,8},{1,13},{5,1},{9,5},{13,9},{2,14},{6,2},{... | collective-permute-start | bytes 786440 | tf_op jit(solution)/shard_map/ppermute | solution.py:12
  46.3 4.8 %collective-permute-done.9 = bf16[128,1024]{1,0:T(8,128)(2,1)S(1)} collective-permute-done((bf16[128,1024]{1,0:T(8,128)(2,1)}, bf16[128,1024]{1,0:T(8,128)(2,1)S(1)}, u32[]{:S(2)}, u32[]{:S(2)}) %collective-permute-start.9) | collective-permute-done | bytes 262176 | tf_op jit(solution)/shard_map/ppermute | solution.py:12
  51.2 2.4 %multiply_reduce_fusion = (f32[]{:T(128)}, f32[]{:T(128)}, f32[512]{0:T(512)S(1)}, f32[512,512]{0,1:T(8,128)S(1)}) fusion(f32[]{:T(128)S(6)} %copy.17, f32[]{:T(128)S(6)} %mul.28, s32[512]{0:T(512)S(1)} %get-tuple-element.20, s32[512]{0:T(512)S(1)} %get-tuple-element.19, bf16[512,1024]{1,0:T(8,128)(2,1)S(1)} %get-tuple-element.22, ...), kind=kOutput, calls=%fused_computation.2 | convolution fusion | flops 542375424 | bytes 3151888 | tf_op jit(solution)/shard_map/dot_general | solution.py:54
  53.6 1.4 pad_maximum_fusion
  55.0 10.9 %collective-permute-start.22 = (f32[2]{0:T(128)S(1)}, f32[2]{0:T(128)S(1)}, u32[]{:S(2)}, u32[]{:S(2)}) collective-permute-start(f32[2]{0:T(128)S(1)} %pad_maximum_fusion), channel_id=1, source_target_pairs={{0,32},{16,48},{32,0},{48,16},{64,96},{80,112},{96,64},{112,80},{1... | collective-permute-start | bytes 32 | tf_op jit(solution)/shard_map/ppermute | solution.py:34
  65.9 1.9 collective-permute-start.23
  67.8 2.0 collective-permute-start.21
  69.8 1.0 fusion.7
  70.8 1.1 fusion.9
  71.9 5.2 %collective-permute-start.12 = (f32[128]{0:T(128)S(1)}, f32[128]{0:T(128)S(1)}, u32[]{:S(2)}, u32[]{:S(2)}) collective-permute-start(f32[128]{0:T(128)S(1)} %get-tuple-element.14), channel_id=1, source_target_pairs={{0,3},{1,0},{2,1},{3,2},{4,7},{5,4},{6,5},{7,6},{8,11},{9,8},{10,9... | collective-permute-start | bytes 1544 | tf_op jit(solution)/shard_map/ppermute | solution.py:12
  77.1 1.9 collective-permute-start.14
  79.0 0.2 fusion.17
  79.2 0.2 fusion.16
  79.4 6.0 %collective-permute-start.13 = (f32[128]{0:T(128)S(1)}, f32[128]{0:T(128)S(1)}, u32[]{:S(2)}, u32[]{:S(2)}) collective-permute-start(f32[128]{0:T(128)S(1)} %get-tuple-element.16), channel_id=1, source_target_pairs={{0,2},{1,3},{2,0},{3,1},{4,6},{5,7},{6,4},{7,5},{8,10},{9,11},{10,... | collective-permute-start | bytes 1544 | tf_op jit(solution)/shard_map/ppermute | solution.py:12
  85.4 1.9 collective-permute-start.15
  87.3 1.4 add_add_fusion.4
  88.7 14.6 %collective-permute-start.26 = (f32[2]{0:T(128)S(1)}, f32[2]{0:T(128)S(1)}, u32[]{:S(2)}, u32[]{:S(2)}) collective-permute-start(f32[2]{0:T(128)S(1)} %add_add_fusion.4), channel_id=1, source_target_pairs={{0,192},{16,208},{32,224},{48,240},{64,128},{80,144},{96,160},{112... | collective-permute-start | bytes 32 | tf_op jit(solution)/shard_map/ppermute | solution.py:34
  103.3 8.0 %collective-permute-done.26 = f32[2]{0:T(128)S(1)} collective-permute-done((f32[2]{0:T(128)S(1)}, f32[2]{0:T(128)S(1)}, u32[]{:S(2)}, u32[]{:S(2)}) %collective-permute-start.26) | collective-permute-done | bytes 40 | tf_op jit(solution)/shard_map/ppermute | solution.py:34
  111.3 2.3 collective-permute-start.25
  113.6 3.1 %collective-permute-done.25 = f32[2]{0:T(128)S(1)} collective-permute-done((f32[2]{0:T(128)S(1)}, f32[2]{0:T(128)S(1)}, u32[]{:S(2)}, u32[]{:S(2)}) %collective-permute-start.25) | collective-permute-done | bytes 40 | tf_op jit(solution)/shard_map/ppermute | solution.py:34
  116.7 6.1 %collective-permute-start.24 = (f32[2]{0:T(128)S(1)}, f32[2]{0:T(128)S(1)}, u32[]{:S(2)}, u32[]{:S(2)}) collective-permute-start(f32[2]{0:T(128)S(1)} %add_add_fusion.4), channel_id=1, source_target_pairs={{0,64},{16,80},{32,96},{48,112},{64,0},{80,16},{96,32},{112,48},{1... | collective-permute-start | bytes 32 | tf_op jit(solution)/shard_map/ppermute | solution.py:34
  122.8 8.1 %collective-permute-done.24 = f32[2]{0:T(128)S(1)} collective-permute-done((f32[2]{0:T(128)S(1)}, f32[2]{0:T(128)S(1)}, u32[]{:S(2)}, u32[]{:S(2)}) %collective-permute-start.24) | collective-permute-done | bytes 40 | tf_op jit(solution)/shard_map/ppermute | solution.py:34
  130.9 4.8 %collective-permute-start.29 = (f32[2]{0:T(128)S(1)}, f32[2]{0:T(128)S(1)}, u32[]{:S(2)}, u32[]{:S(2)}) collective-permute-start(f32[2]{0:T(128)S(1)} %add_add_fusion.3), channel_id=1, source_target_pairs={{0,768},{16,784},{32,800},{48,816},{64,832},{80,848},{96,864},{112... | collective-permute-start | bytes 32 | tf_op jit(solution)/shard_map/ppermute | solution.py:34
  135.7 2.8 %collective-permute-done.29 = f32[2]{0:T(128)S(1)} collective-permute-done((f32[2]{0:T(128)S(1)}, f32[2]{0:T(128)S(1)}, u32[]{:S(2)}, u32[]{:S(2)}) %collective-permute-start.29) | collective-permute-done | bytes 40 | tf_op jit(solution)/shard_map/ppermute | solution.py:34
  138.4 5.0 %collective-permute-start.28 = (f32[2]{0:T(128)S(1)}, f32[2]{0:T(128)S(1)}, u32[]{:S(2)}, u32[]{:S(2)}) collective-permute-start(f32[2]{0:T(128)S(1)} %add_add_fusion.3), channel_id=1, source_target_pairs={{0,512},{16,528},{32,544},{48,560},{64,576},{80,592},{96,608},{112... | collective-permute-start | bytes 32 | tf_op jit(solution)/shard_map/ppermute | solution.py:34
  143.5 4.3 %collective-permute-done.28 = f32[2]{0:T(128)S(1)} collective-permute-done((f32[2]{0:T(128)S(1)}, f32[2]{0:T(128)S(1)}, u32[]{:S(2)}, u32[]{:S(2)}) %collective-permute-start.28) | collective-permute-done | bytes 40 | tf_op jit(solution)/shard_map/ppermute | solution.py:34
  147.8 2.2 collective-permute-start.27
  150.0 4.1 %collective-permute-done.27 = f32[2]{0:T(128)S(1)} collective-permute-done((f32[2]{0:T(128)S(1)}, f32[2]{0:T(128)S(1)}, u32[]{:S(2)}, u32[]{:S(2)}) %collective-permute-start.27) | collective-permute-done | bytes 40 | tf_op jit(solution)/shard_map/ppermute | solution.py:34
  154.2 5.0 %collective-permute-start.32 = (f32[2]{0:T(128)S(1)}, f32[2]{0:T(128)S(1)}, u32[]{:S(2)}, u32[]{:S(2)}) collective-permute-start(f32[2]{0:T(128)S(1)} %add_add_fusion.2), channel_id=1, source_target_pairs={{0,12},{4,8},{8,4},{12,0},{1,13},{5,9},{9,5},{13,1},{2,14},{6,10},... | collective-permute-start | bytes 32 | tf_op jit(solution)/shard_map/ppermute | solution.py:34
  159.2 1.6 collective-permute-done.32
  160.8 3.6 %collective-permute-start.31 = (f32[2]{0:T(128)S(1)}, f32[2]{0:T(128)S(1)}, u32[]{:S(2)}, u32[]{:S(2)}) collective-permute-start(f32[2]{0:T(128)S(1)} %add_add_fusion.2), channel_id=1, source_target_pairs={{0,8},{4,12},{8,0},{12,4},{1,9},{5,13},{9,1},{13,5},{2,10},{6,14},... | collective-permute-start | bytes 32 | tf_op jit(solution)/shard_map/ppermute | solution.py:34
  164.4 3.4 %collective-permute-done.31 = f32[2]{0:T(128)S(1)} collective-permute-done((f32[2]{0:T(128)S(1)}, f32[2]{0:T(128)S(1)}, u32[]{:S(2)}, u32[]{:S(2)}) %collective-permute-start.31) | collective-permute-done | bytes 40 | tf_op jit(solution)/shard_map/ppermute | solution.py:34
  167.8 2.4 %collective-permute-start.30 = (f32[2]{0:T(128)S(1)}, f32[2]{0:T(128)S(1)}, u32[]{:S(2)}, u32[]{:S(2)}) collective-permute-start(f32[2]{0:T(128)S(1)} %add_add_fusion.2), channel_id=1, source_target_pairs={{0,4},{4,0},{8,12},{12,8},{1,5},{5,1},{9,13},{13,9},{2,6},{6,2},{1... | collective-permute-start | bytes 32 | tf_op jit(solution)/shard_map/ppermute | solution.py:34
  170.1 3.1 %collective-permute-done.30 = f32[2]{0:T(128)S(1)} collective-permute-done((f32[2]{0:T(128)S(1)}, f32[2]{0:T(128)S(1)}, u32[]{:S(2)}, u32[]{:S(2)}) %collective-permute-start.30) | collective-permute-done | bytes 40 | tf_op jit(solution)/shard_map/ppermute | solution.py:34
  173.2 1.9 collective-permute-start.35
  175.2 3.5 %collective-permute-done.35 = f32[2]{0:T(128)S(1)} collective-permute-done((f32[2]{0:T(128)S(1)}, f32[2]{0:T(128)S(1)}, u32[]{:S(2)}, u32[]{:S(2)}) %collective-permute-start.35) | collective-permute-done | bytes 40 | tf_op jit(solution)/shard_map/ppermute | solution.py:34
  178.7 4.3 %collective-permute-start.34 = (f32[2]{0:T(128)S(1)}, f32[2]{0:T(128)S(1)}, u32[]{:S(2)}, u32[]{:S(2)}) collective-permute-start(f32[2]{0:T(128)S(1)} %add_add_fusion.1), channel_id=1, source_target_pairs={{0,2},{1,3},{2,0},{3,1},{4,6},{5,7},{6,4},{7,5},{8,10},{9,11},{10,... | collective-permute-start | bytes 32 | tf_op jit(solution)/shard_map/ppermute | solution.py:34
  182.9 2.1 collective-permute-done.34
  185.0 14.1 %collective-permute-start.33 = (f32[2]{0:T(128)S(1)}, f32[2]{0:T(128)S(1)}, u32[]{:S(2)}, u32[]{:S(2)}) collective-permute-start(f32[2]{0:T(128)S(1)} %add_add_fusion.1), channel_id=1, source_target_pairs={{0,1},{1,0},{2,3},{3,2},{4,5},{5,4},{6,7},{7,6},{8,9},{9,8},{10,11... | collective-permute-start | bytes 32 | tf_op jit(solution)/shard_map/ppermute | solution.py:34
  199.1 1.5 collective-permute-done.33
  200.7 1.9 collective-permute-start.17
  202.6 6.3 %collective-permute-start.16 = (f32[128,1024]{1,0:T(8,128)S(1)}, f32[128,1024]{1,0:T(8,128)S(1)}, u32[]{:S(2)}, u32[]{:S(2)}) collective-permute-start(f32[128,1024]{1,0:T(8,128)S(1)} %get-tuple-element.13), channel_id=1, source_target_pairs={{0,2},{1,3},{2,0},{3,1},{4,6},{5,7},{6,4},{7,5},{8,10},{9,11},{10,... | collective-permute-start | bytes 1572872 | tf_op jit(solution)/shard_map/ppermute | solution.py:12
  208.9 4.9 %collective-permute-start.18 = (f32[128,1024]{1,0:T(8,128)S(1)}, f32[128,1024]{1,0:T(8,128)S(1)}, u32[]{:S(2)}, u32[]{:S(2)}) collective-permute-start(f32[128,1024]{1,0:T(8,128)S(1)} %get-tuple-element.8), channel_id=1, source_target_pairs={{0,12},{4,0},{8,4},{12,8},{1,13},{5,1},{9,5},{13,9},{2,14},{6,2},{... | collective-permute-start | bytes 1572872 | tf_op jit(solution)/shard_map/ppermute | solution.py:12
  213.8 1.9 collective-permute-start.20
  215.8 3.7 %collective-permute-start.19 = (f32[128,1024]{1,0:T(8,128)S(1)}, f32[128,1024]{1,0:T(8,128)S(1)}, u32[]{:S(2)}, u32[]{:S(2)}) collective-permute-start(f32[128,1024]{1,0:T(8,128)S(1)} %get-tuple-element.10), channel_id=1, source_target_pairs={{0,8},{4,12},{8,0},{12,4},{1,9},{5,13},{9,1},{13,5},{2,10},{6,14},... | collective-permute-start | bytes 1572872 | tf_op jit(solution)/shard_map/ppermute | solution.py:12
  219.4 0.6 fusion.19
  221.3 0.5 add_multiply_fusion.1
  221.8 1.0 fusion.6
  222.8 8.9 %collective-permute-done.20 = f32[128,1024]{1,0:T(8,128)S(1)} collective-permute-done((f32[128,1024]{1,0:T(8,128)S(1)}, f32[128,1024]{1,0:T(8,128)S(1)}, u32[]{:S(2)}, u32[]{:S(2)}) %collective-permute-start.20) | collective-permute-done | bytes 524320 | tf_op jit(solution)/shard_map/ppermute | solution.py:12
  231.7 1.0 fusion.3
  (32 shorter events, 0.2 us)
Async XLA Ops:
  0.6 20.2 %collective-permute-start.3 = (s32[128]{0:T(128)}, s32[128]{0:T(128)S(1)}, u32[]{:S(2)}, u32[]{:S(2)}) collective-permute-start(s32[128]{0:T(128)} %param.7), channel_id=1, source_target_pairs={{0,4},{4,8},{8,12},{12,0},{1,5},{5,9},{9,13},{13,1},{2,6},{6,10},{... | collective-permute-start | bytes 1544 | tf_op jit(solution)/shard_map/ppermute | solution.py:12
  4.0 19.2 %collective-permute-start.2 = (s32[128]{0:T(128)}, s32[128]{0:T(128)S(1)}, u32[]{:S(2)}, u32[]{:S(2)}) collective-permute-start(s32[128]{0:T(128)} %param.7), channel_id=1, source_target_pairs={{0,3},{1,0},{2,1},{3,2},{4,7},{5,4},{6,5},{7,6},{8,11},{9,8},{10,9... | collective-permute-start | bytes 1544 | tf_op jit(solution)/shard_map/ppermute | solution.py:12
  6.0 22.0 %collective-permute-start.1 = (s32[128]{0:T(128)}, s32[128]{0:T(128)S(1)}, u32[]{:S(2)}, u32[]{:S(2)}) collective-permute-start(s32[128]{0:T(128)} %param.7), channel_id=1, source_target_pairs={{0,2},{1,3},{2,0},{3,1},{4,6},{5,7},{6,4},{7,5},{8,10},{9,11},{10,... | collective-permute-start | bytes 1544 | tf_op jit(solution)/shard_map/ppermute | solution.py:12
  12.1 34.1 %collective-permute-start.7 = (bf16[128,1024]{1,0:T(8,128)(2,1)}, bf16[128,1024]{1,0:T(8,128)(2,1)S(1)}, u32[]{:S(2)}, u32[]{:S(2)}) collective-permute-start(bf16[128,1024]{1,0:T(8,128)(2,1)} %param.5), channel_id=1, source_target_pairs={{0,2},{1,3},{2,0},{3,1},{4,6},{5,7},{6,4},{7,5},{8,10},{9,11},{10,... | collective-permute-start | bytes 786440 | tf_op jit(solution)/shard_map/ppermute | solution.py:12
  14.0 27.4 %collective-permute-start.6 = (bf16[128,1024]{1,0:T(8,128)(2,1)}, bf16[128,1024]{1,0:T(8,128)(2,1)S(1)}, u32[]{:S(2)}, u32[]{:S(2)}) collective-permute-start(bf16[128,1024]{1,0:T(8,128)(2,1)} %param.5), channel_id=1, source_target_pairs={{0,1},{1,2},{2,3},{3,0},{4,5},{5,6},{6,7},{7,4},{8,9},{9,10},{10,1... | collective-permute-start | bytes 786440 | tf_op jit(solution)/shard_map/ppermute | solution.py:12
  20.8 11.8 %collective-permute-start = (s32[128]{0:T(128)}, s32[128]{0:T(128)S(1)}, u32[]{:S(2)}, u32[]{:S(2)}) collective-permute-start(s32[128]{0:T(128)} %param.7), channel_id=1, source_target_pairs={{0,1},{1,2},{2,3},{3,0},{4,5},{5,6},{6,7},{7,4},{8,9},{9,10},{10,1... | collective-permute-start | bytes 1544 | tf_op jit(solution)/shard_map/ppermute | solution.py:12
  23.3 12.7 %collective-permute-start.4 = (s32[128]{0:T(128)}, s32[128]{0:T(128)S(1)}, u32[]{:S(2)}, u32[]{:S(2)}) collective-permute-start(s32[128]{0:T(128)} %param.7), channel_id=1, source_target_pairs={{0,8},{4,12},{8,0},{12,4},{1,9},{5,13},{9,1},{13,5},{2,10},{6,14},... | collective-permute-start | bytes 1544 | tf_op jit(solution)/shard_map/ppermute | solution.py:12
  27.9 10.5 %collective-permute-start.5 = (s32[128]{0:T(128)}, s32[128]{0:T(128)S(1)}, u32[]{:S(2)}, u32[]{:S(2)}) collective-permute-start(s32[128]{0:T(128)} %param.7), channel_id=1, source_target_pairs={{0,12},{4,0},{8,4},{12,8},{1,13},{5,1},{9,5},{13,9},{2,14},{6,2},{... | collective-permute-start | bytes 1544 | tf_op jit(solution)/shard_map/ppermute | solution.py:12
  32.6 18.5 %collective-permute-start.8 = (bf16[128,1024]{1,0:T(8,128)(2,1)}, bf16[128,1024]{1,0:T(8,128)(2,1)S(1)}, u32[]{:S(2)}, u32[]{:S(2)}) collective-permute-start(bf16[128,1024]{1,0:T(8,128)(2,1)} %param.5), channel_id=1, source_target_pairs={{0,3},{1,0},{2,1},{3,2},{4,7},{5,4},{6,5},{7,6},{8,11},{9,8},{10,9... | collective-permute-start | bytes 786440 | tf_op jit(solution)/shard_map/ppermute | solution.py:12
  36.0 15.1 %collective-permute-start.10 = (bf16[128,1024]{1,0:T(8,128)(2,1)}, bf16[128,1024]{1,0:T(8,128)(2,1)S(1)}, u32[]{:S(2)}, u32[]{:S(2)}) collective-permute-start(bf16[128,1024]{1,0:T(8,128)(2,1)} %param.6), channel_id=1, source_target_pairs={{0,8},{4,12},{8,0},{12,4},{1,9},{5,13},{9,1},{13,5},{2,10},{6,14},... | collective-permute-start | bytes 786440 | tf_op jit(solution)/shard_map/ppermute | solution.py:12
  38.4 12.6 %collective-permute-start.9 = (bf16[128,1024]{1,0:T(8,128)(2,1)}, bf16[128,1024]{1,0:T(8,128)(2,1)S(1)}, u32[]{:S(2)}, u32[]{:S(2)}) collective-permute-start(bf16[128,1024]{1,0:T(8,128)(2,1)} %param.6), channel_id=1, source_target_pairs={{0,4},{4,8},{8,12},{12,0},{1,5},{5,9},{9,13},{13,1},{2,6},{6,10},{... | collective-permute-start | bytes 786440 | tf_op jit(solution)/shard_map/ppermute | solution.py:12
  41.4 9.7 %collective-permute-start.11 = (bf16[128,1024]{1,0:T(8,128)(2,1)}, bf16[128,1024]{1,0:T(8,128)(2,1)S(1)}, u32[]{:S(2)}, u32[]{:S(2)}) collective-permute-start(bf16[128,1024]{1,0:T(8,128)(2,1)} %param.6), channel_id=1, source_target_pairs={{0,12},{4,0},{8,4},{12,8},{1,13},{5,1},{9,5},{13,9},{2,14},{6,2},{... | collective-permute-start | bytes 786440 | tf_op jit(solution)/shard_map/ppermute | solution.py:12
  55.0 24.4 %collective-permute-start.22 = (f32[2]{0:T(128)S(1)}, f32[2]{0:T(128)S(1)}, u32[]{:S(2)}, u32[]{:S(2)}) collective-permute-start(f32[2]{0:T(128)S(1)} %pad_maximum_fusion), channel_id=1, source_target_pairs={{0,32},{16,48},{32,0},{48,16},{64,96},{80,112},{96,64},{112,80},{1... | collective-permute-start | bytes 32 | tf_op jit(solution)/shard_map/ppermute | solution.py:34
  65.9 19.5 %collective-permute-start.23 = (f32[2]{0:T(128)S(1)}, f32[2]{0:T(128)S(1)}, u32[]{:S(2)}, u32[]{:S(2)}) collective-permute-start(f32[2]{0:T(128)S(1)} %pad_maximum_fusion), channel_id=1, source_target_pairs={{0,48},{16,32},{32,16},{48,0},{64,112},{80,96},{96,80},{112,64},{1... | collective-permute-start | bytes 32 | tf_op jit(solution)/shard_map/ppermute | solution.py:34
  67.8 19.5 %collective-permute-start.21 = (f32[2]{0:T(128)S(1)}, f32[2]{0:T(128)S(1)}, u32[]{:S(2)}, u32[]{:S(2)}) collective-permute-start(f32[2]{0:T(128)S(1)} %pad_maximum_fusion), channel_id=1, source_target_pairs={{0,16},{16,0},{32,48},{48,32},{64,80},{80,64},{96,112},{112,96},{1... | collective-permute-start | bytes 32 | tf_op jit(solution)/shard_map/ppermute | solution.py:34
  71.9 130.7 %collective-permute-start.12 = (f32[128]{0:T(128)S(1)}, f32[128]{0:T(128)S(1)}, u32[]{:S(2)}, u32[]{:S(2)}) collective-permute-start(f32[128]{0:T(128)S(1)} %get-tuple-element.14), channel_id=1, source_target_pairs={{0,3},{1,0},{2,1},{3,2},{4,7},{5,4},{6,5},{7,6},{8,11},{9,8},{10,9... | collective-permute-start | bytes 1544 | tf_op jit(solution)/shard_map/ppermute | solution.py:12
  77.1 131.8 %collective-permute-start.14 = (f32[128]{0:T(128)S(1)}, f32[128]{0:T(128)S(1)}, u32[]{:S(2)}, u32[]{:S(2)}) collective-permute-start(f32[128]{0:T(128)S(1)} %get-tuple-element.15), channel_id=1, source_target_pairs={{0,1},{1,2},{2,3},{3,0},{4,5},{5,6},{6,7},{7,4},{8,9},{9,10},{10,1... | collective-permute-start | bytes 1544 | tf_op jit(solution)/shard_map/ppermute | solution.py:12
  79.4 134.4 %collective-permute-start.13 = (f32[128]{0:T(128)S(1)}, f32[128]{0:T(128)S(1)}, u32[]{:S(2)}, u32[]{:S(2)}) collective-permute-start(f32[128]{0:T(128)S(1)} %get-tuple-element.16), channel_id=1, source_target_pairs={{0,2},{1,3},{2,0},{3,1},{4,6},{5,7},{6,4},{7,5},{8,10},{9,11},{10,... | collective-permute-start | bytes 1544 | tf_op jit(solution)/shard_map/ppermute | solution.py:12
  85.4 130.4 %collective-permute-start.15 = (f32[128,1024]{1,0:T(8,128)S(1)}, f32[128,1024]{1,0:T(8,128)S(1)}, u32[]{:S(2)}, u32[]{:S(2)}) collective-permute-start(f32[128,1024]{1,0:T(8,128)S(1)} %get-tuple-element.11), channel_id=1, source_target_pairs={{0,3},{1,0},{2,1},{3,2},{4,7},{5,4},{6,5},{7,6},{8,11},{9,8},{10,9... | collective-permute-start | bytes 1572872 | tf_op jit(solution)/shard_map/ppermute | solution.py:12
  88.7 22.6 %collective-permute-start.26 = (f32[2]{0:T(128)S(1)}, f32[2]{0:T(128)S(1)}, u32[]{:S(2)}, u32[]{:S(2)}) collective-permute-start(f32[2]{0:T(128)S(1)} %add_add_fusion.4), channel_id=1, source_target_pairs={{0,192},{16,208},{32,224},{48,240},{64,128},{80,144},{96,160},{112... | collective-permute-start | bytes 32 | tf_op jit(solution)/shard_map/ppermute | solution.py:34
  111.3 5.5 %collective-permute-start.25 = (f32[2]{0:T(128)S(1)}, f32[2]{0:T(128)S(1)}, u32[]{:S(2)}, u32[]{:S(2)}) collective-permute-start(f32[2]{0:T(128)S(1)} %add_add_fusion.4), channel_id=1, source_target_pairs={{0,128},{16,144},{32,160},{48,176},{64,192},{80,208},{96,224},{112... | collective-permute-start | bytes 32 | tf_op jit(solution)/shard_map/ppermute | solution.py:34
  116.7 14.2 %collective-permute-start.24 = (f32[2]{0:T(128)S(1)}, f32[2]{0:T(128)S(1)}, u32[]{:S(2)}, u32[]{:S(2)}) collective-permute-start(f32[2]{0:T(128)S(1)} %add_add_fusion.4), channel_id=1, source_target_pairs={{0,64},{16,80},{32,96},{48,112},{64,0},{80,16},{96,32},{112,48},{1... | collective-permute-start | bytes 32 | tf_op jit(solution)/shard_map/ppermute | solution.py:34
  130.9 7.6 %collective-permute-start.29 = (f32[2]{0:T(128)S(1)}, f32[2]{0:T(128)S(1)}, u32[]{:S(2)}, u32[]{:S(2)}) collective-permute-start(f32[2]{0:T(128)S(1)} %add_add_fusion.3), channel_id=1, source_target_pairs={{0,768},{16,784},{32,800},{48,816},{64,832},{80,848},{96,864},{112... | collective-permute-start | bytes 32 | tf_op jit(solution)/shard_map/ppermute | solution.py:34
  138.4 9.4 %collective-permute-start.28 = (f32[2]{0:T(128)S(1)}, f32[2]{0:T(128)S(1)}, u32[]{:S(2)}, u32[]{:S(2)}) collective-permute-start(f32[2]{0:T(128)S(1)} %add_add_fusion.3), channel_id=1, source_target_pairs={{0,512},{16,528},{32,544},{48,560},{64,576},{80,592},{96,608},{112... | collective-permute-start | bytes 32 | tf_op jit(solution)/shard_map/ppermute | solution.py:34
  147.8 6.3 %collective-permute-start.27 = (f32[2]{0:T(128)S(1)}, f32[2]{0:T(128)S(1)}, u32[]{:S(2)}, u32[]{:S(2)}) collective-permute-start(f32[2]{0:T(128)S(1)} %add_add_fusion.3), channel_id=1, source_target_pairs={{0,256},{16,272},{32,288},{48,304},{64,320},{80,336},{96,352},{112... | collective-permute-start | bytes 32 | tf_op jit(solution)/shard_map/ppermute | solution.py:34
  154.2 6.7 %collective-permute-start.32 = (f32[2]{0:T(128)S(1)}, f32[2]{0:T(128)S(1)}, u32[]{:S(2)}, u32[]{:S(2)}) collective-permute-start(f32[2]{0:T(128)S(1)} %add_add_fusion.2), channel_id=1, source_target_pairs={{0,12},{4,8},{8,4},{12,0},{1,13},{5,9},{9,5},{13,1},{2,14},{6,10},... | collective-permute-start | bytes 32 | tf_op jit(solution)/shard_map/ppermute | solution.py:34
  160.8 7.0 %collective-permute-start.31 = (f32[2]{0:T(128)S(1)}, f32[2]{0:T(128)S(1)}, u32[]{:S(2)}, u32[]{:S(2)}) collective-permute-start(f32[2]{0:T(128)S(1)} %add_add_fusion.2), channel_id=1, source_target_pairs={{0,8},{4,12},{8,0},{12,4},{1,9},{5,13},{9,1},{13,5},{2,10},{6,14},... | collective-permute-start | bytes 32 | tf_op jit(solution)/shard_map/ppermute | solution.py:34
  167.8 5.5 %collective-permute-start.30 = (f32[2]{0:T(128)S(1)}, f32[2]{0:T(128)S(1)}, u32[]{:S(2)}, u32[]{:S(2)}) collective-permute-start(f32[2]{0:T(128)S(1)} %add_add_fusion.2), channel_id=1, source_target_pairs={{0,4},{4,0},{8,12},{12,8},{1,5},{5,1},{9,13},{13,9},{2,6},{6,2},{1... | collective-permute-start | bytes 32 | tf_op jit(solution)/shard_map/ppermute | solution.py:34
  173.2 5.5 %collective-permute-start.35 = (f32[2]{0:T(128)S(1)}, f32[2]{0:T(128)S(1)}, u32[]{:S(2)}, u32[]{:S(2)}) collective-permute-start(f32[2]{0:T(128)S(1)} %add_add_fusion.1), channel_id=1, source_target_pairs={{0,3},{1,2},{2,1},{3,0},{4,7},{5,6},{6,5},{7,4},{8,11},{9,10},{10,... | collective-permute-start | bytes 32 | tf_op jit(solution)/shard_map/ppermute | solution.py:34
  178.7 6.4 %collective-permute-start.34 = (f32[2]{0:T(128)S(1)}, f32[2]{0:T(128)S(1)}, u32[]{:S(2)}, u32[]{:S(2)}) collective-permute-start(f32[2]{0:T(128)S(1)} %add_add_fusion.1), channel_id=1, source_target_pairs={{0,2},{1,3},{2,0},{3,1},{4,6},{5,7},{6,4},{7,5},{8,10},{9,11},{10,... | collective-permute-start | bytes 32 | tf_op jit(solution)/shard_map/ppermute | solution.py:34
  185.0 15.6 %collective-permute-start.33 = (f32[2]{0:T(128)S(1)}, f32[2]{0:T(128)S(1)}, u32[]{:S(2)}, u32[]{:S(2)}) collective-permute-start(f32[2]{0:T(128)S(1)} %add_add_fusion.1), channel_id=1, source_target_pairs={{0,1},{1,0},{2,3},{3,2},{4,5},{5,4},{6,7},{7,6},{8,9},{9,8},{10,11... | collective-permute-start | bytes 32 | tf_op jit(solution)/shard_map/ppermute | solution.py:34
  200.7 21.2 %collective-permute-start.17 = (f32[128,1024]{1,0:T(8,128)S(1)}, f32[128,1024]{1,0:T(8,128)S(1)}, u32[]{:S(2)}, u32[]{:S(2)}) collective-permute-start(f32[128,1024]{1,0:T(8,128)S(1)} %get-tuple-element.12), channel_id=1, source_target_pairs={{0,1},{1,2},{2,3},{3,0},{4,5},{5,6},{6,7},{7,4},{8,9},{9,10},{10,1... | collective-permute-start | bytes 1572872 | tf_op jit(solution)/shard_map/ppermute | solution.py:12
  202.6 19.2 %collective-permute-start.16 = (f32[128,1024]{1,0:T(8,128)S(1)}, f32[128,1024]{1,0:T(8,128)S(1)}, u32[]{:S(2)}, u32[]{:S(2)}) collective-permute-start(f32[128,1024]{1,0:T(8,128)S(1)} %get-tuple-element.13), channel_id=1, source_target_pairs={{0,2},{1,3},{2,0},{3,1},{4,6},{5,7},{6,4},{7,5},{8,10},{9,11},{10,... | collective-permute-start | bytes 1572872 | tf_op jit(solution)/shard_map/ppermute | solution.py:12
  208.9 13.8 %collective-permute-start.18 = (f32[128,1024]{1,0:T(8,128)S(1)}, f32[128,1024]{1,0:T(8,128)S(1)}, u32[]{:S(2)}, u32[]{:S(2)}) collective-permute-start(f32[128,1024]{1,0:T(8,128)S(1)} %get-tuple-element.8), channel_id=1, source_target_pairs={{0,12},{4,0},{8,4},{12,8},{1,13},{5,1},{9,5},{13,9},{2,14},{6,2},{... | collective-permute-start | bytes 1572872 | tf_op jit(solution)/shard_map/ppermute | solution.py:12
  213.8 17.9 %collective-permute-start.20 = (f32[128,1024]{1,0:T(8,128)S(1)}, f32[128,1024]{1,0:T(8,128)S(1)}, u32[]{:S(2)}, u32[]{:S(2)}) collective-permute-start(f32[128,1024]{1,0:T(8,128)S(1)} %get-tuple-element.9), channel_id=1, source_target_pairs={{0,4},{4,8},{8,12},{12,0},{1,5},{5,9},{9,13},{13,1},{2,6},{6,10},{... | collective-permute-start | bytes 1572872 | tf_op jit(solution)/shard_map/ppermute | solution.py:12
  215.8 16.0 %collective-permute-start.19 = (f32[128,1024]{1,0:T(8,128)S(1)}, f32[128,1024]{1,0:T(8,128)S(1)}, u32[]{:S(2)}, u32[]{:S(2)}) collective-permute-start(f32[128,1024]{1,0:T(8,128)S(1)} %get-tuple-element.10), channel_id=1, source_target_pairs={{0,8},{4,12},{8,0},{12,4},{1,9},{5,13},{9,1},{13,5},{2,10},{6,14},... | collective-permute-start | bytes 1572872 | tf_op jit(solution)/shard_map/ppermute | solution.py:12

commit v2 on v1

--- a/solution.py
+++ b/solution.py
@@ -30,17 +30,12 @@
         count = lax.axis_size(axis)
         step = 1
         while step < count:
-            if step * 4 <= count:
-                got = [lax.ppermute(sums, axis, [(i, i ^ (a * step)) for i in range(count)]) for a in (1, 2, 3)]
-                sums = (sums + got[0]) + (got[1] + got[2])
-                step *= 4
-            else:
-                sums = sums + lax.ppermute(sums, axis, [(i, i ^ step) for i in range(count)])
-                step *= 2
+            sums = sums + lax.ppermute(sums, axis, [(i, i ^ step) for i in range(count)])
+            step *= 2
     return sums
 
 
-def on_device(informal, formal, labels, temp, bias):
+def device_terms(informal, formal, labels, temp, bias):
     rows, width = informal.shape
     ngroup = lax.axis_size("group")
     nrow = lax.axis_size("bz")
@@ -59,10 +54,10 @@
     weights = slope.astype(jnp.bfloat16)
     grad_x_part = jnp.dot(weights, col_formal, preferred_element_type=jnp.float32)
     grad_y_part = lax.dot_general(weights, row_informal, (((0,), (0,)), ((), ())), preferred_element_type=jnp.float32)
-    sums = total_sums(jnp.stack([jnp.sum(slope * raw), jnp.sum(slope)]), ("group", "bx", "bz"))
     loss_sum = reduce_by_shift(loss_part.reshape(nrow, rows), "bz")
     grad_x = scale * reduce_by_shift(grad_x_part.reshape(nrow, rows, width), "bz")
     grad_y = scale * reduce_by_shift(grad_y_part.reshape(ncol, rows, width), "bx")
+    sums = total_sums(jnp.stack([jnp.sum(slope * raw), jnp.sum(slope)]), ("group", "bx", "bz"))
     set_size = rows * nrow * ncol
     total = jnp.float32(set_size * ngroup) * jnp.float32(set_size)
     loss = loss_sum / set_size
@@ -81,4 +76,4 @@
     rowspec = ("group", "bx", "bz")
     in_specs = (P(rowspec, None), P(rowspec, None), P(rowspec), P(), P())
     out_specs = (P(rowspec), P(rowspec, None), P(rowspec, None), P(), P())
-    return jax.shard_map(on_device, mesh=fine, in_specs=in_specs, out_specs=out_specs, check_vma=False)
+    return jax.shard_map(device_terms, mesh=fine, in_specs=in_specs, out_specs=out_specs, check_vma=False)

time: 236 us -> 194 us (0.82)
  the two profiles are of different devices: /device:TPU:80 before, /device:TPU:1 now
where the time goes in v2:
time: 194 us; the launch traced here: 193 us
  starting transfers between devices  124 us (64%)
  waiting for transfers between devices  48.4 us (25%)
  other arithmetic  7.22 us (4%)
  between operations  5.95 us (3%)
  matrix products  4.5 us (2%)
  local copies, waits for them, and re-layouts  2.98 us (2%)
    ppermute x21, starting transfers between devices, shifted(): lax.ppermute(value, axis, [(i, (i + by) % count) for i in range(count)])  73.1 us
    ppermute x10, starting transfers between devices, total_sums(): lax.ppermute(sums, axis, [(i, i ^ step) for i in range(count)])  50.9 us
    ppermute x21, waiting for transfers between devices, shifted(): lax.ppermute(value, axis, [(i, (i + by) % count) for i in range(count)])  25 us
    ppermute x10, waiting for transfers between devices, total_sums(): lax.ppermute(sums, axis, [(i, i ^ step) for i in range(count)])  23.4 us
  transfers between devices with their start and end apart: 31, of which 12 were waited for; matrix products, arithmetic and copies ran while one was open for 5% of the time, Pallas kernels for 0%

profile of v2, /device:TPU:1, one launch (start us, length us, event | category | flops | bytes accessed | tf_op | source)
XLA Modules:
  0.0 193.1 jit_solution(15993531917070568997)
XLA Ops:
  0.6 3.9 %collective-permute-start.3 = (s32[128]{0:T(128)}, s32[128]{0:T(128)S(1)}, u32[]{:S(2)}, u32[]{:S(2)}) collective-permute-start(s32[128]{0:T(128)} %param.7), channel_id=1, source_target_pairs={{0,4},{4,8},{8,12},{12,0},{1,5},{5,9},{9,13},{13,1},{2,6},{6,10},{... | collective-permute-start | bytes 1544 | tf_op jit(solution)/shard_map/ppermute | solution.py:12
  4.6 7.6 %collective-permute-start.2 = (s32[128]{0:T(128)}, s32[128]{0:T(128)S(1)}, u32[]{:S(2)}, u32[]{:S(2)}) collective-permute-start(s32[128]{0:T(128)} %param.7), channel_id=1, source_target_pairs={{0,3},{1,0},{2,1},{3,2},{4,7},{5,4},{6,5},{7,6},{8,11},{9,8},{10,9... | collective-permute-start | bytes 1544 | tf_op jit(solution)/shard_map/ppermute | solution.py:12
  12.2 1.9 collective-permute-start.1
  14.1 4.3 %collective-permute-start.7 = (bf16[128,1024]{1,0:T(8,128)(2,1)}, bf16[128,1024]{1,0:T(8,128)(2,1)S(1)}, u32[]{:S(2)}, u32[]{:S(2)}) collective-permute-start(bf16[128,1024]{1,0:T(8,128)(2,1)} %param.5), channel_id=1, source_target_pairs={{0,2},{1,3},{2,0},{3,1},{4,6},{5,7},{6,4},{7,5},{8,10},{9,11},{10,... | collective-permute-start | bytes 786440 | tf_op jit(solution)/shard_map/ppermute | solution.py:12
  18.4 1.9 collective-permute-start.6
  20.3 1.0 constant_dynamic-update-slice_fusion.3
  21.3 1.0 constant_dynamic-update-slice_fusion.7
  22.3 2.2 %collective-permute-start = (s32[128]{0:T(128)}, s32[128]{0:T(128)S(1)}, u32[]{:S(2)}, u32[]{:S(2)}) collective-permute-start(s32[128]{0:T(128)} %param.7), channel_id=1, source_target_pairs={{0,1},{1,2},{2,3},{3,0},{4,5},{5,6},{6,7},{7,4},{8,9},{9,10},{10,1... | collective-permute-start | bytes 1544 | tf_op jit(solution)/shard_map/ppermute | solution.py:12
  24.5 0.0 collective-permute-done.2
  24.5 4.4 %collective-permute-start.4 = (s32[128]{0:T(128)}, s32[128]{0:T(128)S(1)}, u32[]{:S(2)}, u32[]{:S(2)}) collective-permute-start(s32[128]{0:T(128)} %param.7), channel_id=1, source_target_pairs={{0,8},{4,12},{8,0},{12,4},{1,9},{5,13},{9,1},{13,5},{2,10},{6,14},... | collective-permute-start | bytes 1544 | tf_op jit(solution)/shard_map/ppermute | solution.py:12
  28.9 3.1 %collective-permute-start.5 = (s32[128]{0:T(128)}, s32[128]{0:T(128)S(1)}, u32[]{:S(2)}, u32[]{:S(2)}) collective-permute-start(s32[128]{0:T(128)} %param.7), channel_id=1, source_target_pairs={{0,12},{4,0},{8,4},{12,8},{1,13},{5,1},{9,5},{13,9},{2,14},{6,2},{... | collective-permute-start | bytes 1544 | tf_op jit(solution)/shard_map/ppermute | solution.py:12
  33.3 4.9 %collective-permute-start.8 = (bf16[128,1024]{1,0:T(8,128)(2,1)}, bf16[128,1024]{1,0:T(8,128)(2,1)S(1)}, u32[]{:S(2)}, u32[]{:S(2)}) collective-permute-start(bf16[128,1024]{1,0:T(8,128)(2,1)} %param.5), channel_id=1, source_target_pairs={{0,3},{1,0},{2,1},{3,2},{4,7},{5,4},{6,5},{7,6},{8,11},{9,8},{10,9... | collective-permute-start | bytes 786440 | tf_op jit(solution)/shard_map/ppermute | solution.py:12
  38.2 0.0 collective-permute-done.4
  38.2 2.1 %collective-permute-start.10 = (bf16[128,1024]{1,0:T(8,128)(2,1)}, bf16[128,1024]{1,0:T(8,128)(2,1)S(1)}, u32[]{:S(2)}, u32[]{:S(2)}) collective-permute-start(bf16[128,1024]{1,0:T(8,128)(2,1)} %param.6), channel_id=1, source_target_pairs={{0,8},{4,12},{8,0},{12,4},{1,9},{5,13},{9,1},{13,5},{2,10},{6,14},... | collective-permute-start | bytes 786440 | tf_op jit(solution)/shard_map/ppermute | solution.py:12
  40.3 0.0 collective-permute-done.5
  40.3 2.3 %collective-permute-start.9 = (bf16[128,1024]{1,0:T(8,128)(2,1)}, bf16[128,1024]{1,0:T(8,128)(2,1)S(1)}, u32[]{:S(2)}, u32[]{:S(2)}) collective-permute-start(bf16[128,1024]{1,0:T(8,128)(2,1)} %param.6), channel_id=1, source_target_pairs={{0,4},{4,8},{8,12},{12,0},{1,5},{5,9},{9,13},{13,1},{2,6},{6,10},{... | collective-permute-start | bytes 786440 | tf_op jit(solution)/shard_map/ppermute | solution.py:12
  42.6 0.7 fusion.12
  43.3 0.0 collective-permute-done.6
  43.3 4.2 %collective-permute-start.11 = (bf16[128,1024]{1,0:T(8,128)(2,1)}, bf16[128,1024]{1,0:T(8,128)(2,1)S(1)}, u32[]{:S(2)}, u32[]{:S(2)}) collective-permute-start(bf16[128,1024]{1,0:T(8,128)(2,1)} %param.6), channel_id=1, source_target_pairs={{0,12},{4,0},{8,4},{12,8},{1,13},{5,1},{9,5},{13,9},{2,14},{6,2},{... | collective-permute-start | bytes 786440 | tf_op jit(solution)/shard_map/ppermute | solution.py:12
  47.6 2.2 %collective-permute-done.9 = bf16[128,1024]{1,0:T(8,128)(2,1)S(1)} collective-permute-done((bf16[128,1024]{1,0:T(8,128)(2,1)}, bf16[128,1024]{1,0:T(8,128)(2,1)S(1)}, u32[]{:S(2)}, u32[]{:S(2)}) %collective-permute-start.9) | collective-permute-done | bytes 262176 | tf_op jit(solution)/shard_map/ppermute | solution.py:12
  49.8 0.0 collective-permute-done.10
  49.9 1.3 collective-permute-done.11
  51.3 2.4 %multiply_reduce_fusion = (f32[]{:T(128)}, f32[]{:T(128)}, f32[512]{0:T(512)S(1)}, f32[512,512]{0,1:T(8,128)S(1)}) fusion(f32[]{:T(128)S(6)} %copy.17, f32[]{:T(128)S(6)} %mul.28, s32[512]{0:T(512)S(1)} %get-tuple-element.20, s32[512]{0:T(512)S(1)} %get-tuple-element.19, bf16[512,1024]{1,0:T(8,128)(2,1)S(1)} %get-tuple-element.22, ...), kind=kOutput, calls=%fused_computation.2 | convolution fusion | flops 542375424 | bytes 3151888 | tf_op jit(solution)/shard_map/dot_general | solution.py:49
  53.7 1.0 fusion.7
  54.7 1.1 fusion.9
  55.8 6.2 %collective-permute-start.12 = (f32[128]{0:T(128)S(1)}, f32[128]{0:T(128)S(1)}, u32[]{:S(2)}, u32[]{:S(2)}) collective-permute-start(f32[128]{0:T(128)S(1)} %get-tuple-element.14), channel_id=1, source_target_pairs={{0,3},{1,0},{2,1},{3,2},{4,7},{5,4},{6,5},{7,6},{8,11},{9,8},{10,9... | collective-permute-start | bytes 1544 | tf_op jit(solution)/shard_map/ppermute | solution.py:12
  62.0 1.9 collective-permute-start.14
  64.0 2.2 %collective-permute-start.13 = (f32[128]{0:T(128)S(1)}, f32[128]{0:T(128)S(1)}, u32[]{:S(2)}, u32[]{:S(2)}) collective-permute-start(f32[128]{0:T(128)S(1)} %get-tuple-element.16), channel_id=1, source_target_pairs={{0,2},{1,3},{2,0},{3,1},{4,6},{5,7},{6,4},{7,5},{8,10},{9,11},{10,... | collective-permute-start | bytes 1544 | tf_op jit(solution)/shard_map/ppermute | solution.py:12
  66.2 1.4 pad_maximum_fusion
  67.5 12.2 %collective-permute-start.21 = (f32[2]{0:T(128)S(1)}, f32[2]{0:T(128)S(1)}, u32[]{:S(2)}, u32[]{:S(2)}) collective-permute-start(f32[2]{0:T(128)S(1)} %pad_maximum_fusion), channel_id=1, source_target_pairs={{0,16},{16,0},{32,48},{48,32},{64,80},{80,64},{96,112},{112,96},{1... | collective-permute-start | bytes 32 | tf_op jit(solution)/shard_map/ppermute | solution.py:33
  79.7 0.2 fusion.17
  79.9 4.0 %collective-permute-start.15 = (f32[128,1024]{1,0:T(8,128)S(1)}, f32[128,1024]{1,0:T(8,128)S(1)}, u32[]{:S(2)}, u32[]{:S(2)}) collective-permute-start(f32[128,1024]{1,0:T(8,128)S(1)} %get-tuple-element.11), channel_id=1, source_target_pairs={{0,3},{1,0},{2,1},{3,2},{4,7},{5,4},{6,5},{7,6},{8,11},{9,8},{10,9... | collective-permute-start | bytes 1572872 | tf_op jit(solution)/shard_map/ppermute | solution.py:12
  83.9 1.4 fusion.24
  85.3 3.9 %collective-permute-start.22 = (f32[2]{0:T(128)S(1)}, f32[2]{0:T(128)S(1)}, u32[]{:S(2)}, u32[]{:S(2)}) collective-permute-start(f32[2]{0:T(128)S(1)} %fusion.24), channel_id=1, source_target_pairs={{0,32},{16,48},{32,0},{48,16},{64,96},{80,112},{96,64},{112,80},{1... | collective-permute-start | bytes 32 | tf_op jit(solution)/shard_map/ppermute | solution.py:33
  89.2 6.0 %collective-permute-done.22 = f32[2]{0:T(128)S(1)} collective-permute-done((f32[2]{0:T(128)S(1)}, f32[2]{0:T(128)S(1)}, u32[]{:S(2)}, u32[]{:S(2)}) %collective-permute-start.22) | collective-permute-done | bytes 40 | tf_op jit(solution)/shard_map/ppermute | solution.py:33
  95.2 1.4 fusion.25
  96.6 9.6 %collective-permute-start.23 = (f32[2]{0:T(128)S(1)}, f32[2]{0:T(128)S(1)}, u32[]{:S(2)}, u32[]{:S(2)}) collective-permute-start(f32[2]{0:T(128)S(1)} %fusion.25), channel_id=1, source_target_pairs={{0,64},{16,80},{32,96},{48,112},{64,0},{80,16},{96,32},{112,48},{1... | collective-permute-start | bytes 32 | tf_op jit(solution)/shard_map/ppermute | solution.py:33
  106.2 3.4 %collective-permute-done.23 = f32[2]{0:T(128)S(1)} collective-permute-done((f32[2]{0:T(128)S(1)}, f32[2]{0:T(128)S(1)}, u32[]{:S(2)}, u32[]{:S(2)}) %collective-permute-start.23) | collective-permute-done | bytes 40 | tf_op jit(solution)/shard_map/ppermute | solution.py:33
  109.6 1.9 collective-permute-start.24
  111.5 2.4 %collective-permute-done.24 = f32[2]{0:T(128)S(1)} collective-permute-done((f32[2]{0:T(128)S(1)}, f32[2]{0:T(128)S(1)}, u32[]{:S(2)}, u32[]{:S(2)}) %collective-permute-start.24) | collective-permute-done | bytes 40 | tf_op jit(solution)/shard_map/ppermute | solution.py:33
  113.9 1.9 collective-permute-start.25
  115.8 3.3 %collective-permute-done.25 = f32[2]{0:T(128)S(1)} collective-permute-done((f32[2]{0:T(128)S(1)}, f32[2]{0:T(128)S(1)}, u32[]{:S(2)}, u32[]{:S(2)}) %collective-permute-start.25) | collective-permute-done | bytes 40 | tf_op jit(solution)/shard_map/ppermute | solution.py:33
  119.1 5.0 %collective-permute-start.26 = (f32[2]{0:T(128)S(1)}, f32[2]{0:T(128)S(1)}, u32[]{:S(2)}, u32[]{:S(2)}) collective-permute-start(f32[2]{0:T(128)S(1)} %add.87), channel_id=1, source_target_pairs={{0,512},{16,528},{32,544},{48,560},{64,576},{80,592},{96,608},{112... | collective-permute-start | bytes 32 | tf_op jit(solution)/shard_map/ppermute | solution.py:33
  124.1 3.2 %collective-permute-done.26 = f32[2]{0:T(128)S(1)} collective-permute-done((f32[2]{0:T(128)S(1)}, f32[2]{0:T(128)S(1)}, u32[]{:S(2)}, u32[]{:S(2)}) %collective-permute-start.26) | collective-permute-done | bytes 40 | tf_op jit(solution)/shard_map/ppermute | solution.py:33
  127.3 1.9 collective-permute-start.27
  129.2 2.4 %collective-permute-done.27 = f32[2]{0:T(128)S(1)} collective-permute-done((f32[2]{0:T(128)S(1)}, f32[2]{0:T(128)S(1)}, u32[]{:S(2)}, u32[]{:S(2)}) %collective-permute-start.27) | collective-permute-done | bytes 40 | tf_op jit(solution)/shard_map/ppermute | solution.py:33
  131.6 4.9 %collective-permute-start.28 = (f32[2]{0:T(128)S(1)}, f32[2]{0:T(128)S(1)}, u32[]{:S(2)}, u32[]{:S(2)}) collective-permute-start(f32[2]{0:T(128)S(1)} %add.89), channel_id=1, source_target_pairs={{0,8},{4,12},{8,0},{12,4},{1,9},{5,13},{9,1},{13,5},{2,10},{6,14},... | collective-permute-start | bytes 32 | tf_op jit(solution)/shard_map/ppermute | solution.py:33
  136.6 0.9 collective-permute-done.28
  137.5 5.2 %collective-permute-start.29 = (f32[2]{0:T(128)S(1)}, f32[2]{0:T(128)S(1)}, u32[]{:S(2)}, u32[]{:S(2)}) collective-permute-start(f32[2]{0:T(128)S(1)} %add.90), channel_id=1, source_target_pairs={{0,1},{1,0},{2,3},{3,2},{4,5},{5,4},{6,7},{7,6},{8,9},{9,8},{10,11... | collective-permute-start | bytes 32 | tf_op jit(solution)/shard_map/ppermute | solution.py:33
  142.8 0.9 collective-permute-done.29
  143.7 4.2 %collective-permute-start.30 = (f32[2]{0:T(128)S(1)}, f32[2]{0:T(128)S(1)}, u32[]{:S(2)}, u32[]{:S(2)}) collective-permute-start(f32[2]{0:T(128)S(1)} %add.91), channel_id=1, source_target_pairs={{0,2},{1,3},{2,0},{3,1},{4,6},{5,7},{6,4},{7,5},{8,10},{9,11},{10,... | collective-permute-start | bytes 32 | tf_op jit(solution)/shard_map/ppermute | solution.py:33
  148.0 0.9 collective-permute-done.30
  148.9 3.4 %collective-permute-start.17 = (f32[128,1024]{1,0:T(8,128)S(1)}, f32[128,1024]{1,0:T(8,128)S(1)}, u32[]{:S(2)}, u32[]{:S(2)}) collective-permute-start(f32[128,1024]{1,0:T(8,128)S(1)} %get-tuple-element.12), channel_id=1, source_target_pairs={{0,1},{1,2},{2,3},{3,0},{4,5},{5,6},{6,7},{7,4},{8,9},{9,10},{10,1... | collective-permute-start | bytes 1572872 | tf_op jit(solution)/shard_map/ppermute | solution.py:12
  152.3 0.0 collective-permute-done.12
  152.3 2.8 %collective-permute-start.16 = (f32[128,1024]{1,0:T(8,128)S(1)}, f32[128,1024]{1,0:T(8,128)S(1)}, u32[]{:S(2)}, u32[]{:S(2)}) collective-permute-start(f32[128,1024]{1,0:T(8,128)S(1)} %get-tuple-element.13), channel_id=1, source_target_pairs={{0,2},{1,3},{2,0},{3,1},{4,6},{5,7},{6,4},{7,5},{8,10},{9,11},{10,... | collective-permute-start | bytes 1572872 | tf_op jit(solution)/shard_map/ppermute | solution.py:12
  155.1 0.2 fusion.16
  155.3 4.8 %collective-permute-start.18 = (f32[128,1024]{1,0:T(8,128)S(1)}, f32[128,1024]{1,0:T(8,128)S(1)}, u32[]{:S(2)}, u32[]{:S(2)}) collective-permute-start(f32[128,1024]{1,0:T(8,128)S(1)} %get-tuple-element.8), channel_id=1, source_target_pairs={{0,12},{4,0},{8,4},{12,8},{1,13},{5,1},{9,5},{13,9},{2,14},{6,2},{... | collective-permute-start | bytes 1572872 | tf_op jit(solution)/shard_map/ppermute | solution.py:12
  160.1 1.9 collective-permute-start.20
  162.0 3.1 %collective-permute-start.19 = (f32[128,1024]{1,0:T(8,128)S(1)}, f32[128,1024]{1,0:T(8,128)S(1)}, u32[]{:S(2)}, u32[]{:S(2)}) collective-permute-start(f32[128,1024]{1,0:T(8,128)S(1)} %get-tuple-element.10), channel_id=1, source_target_pairs={{0,8},{4,12},{8,0},{12,4},{1,9},{5,13},{9,1},{13,5},{2,10},{6,14},... | collective-permute-start | bytes 1572872 | tf_op jit(solution)/shard_map/ppermute | solution.py:12
  165.1 0.6 fusion.19
  167.0 0.5 add_multiply_fusion.1
  167.5 21.4 %collective-permute-done.16 = f32[128,1024]{1,0:T(8,128)S(1)} collective-permute-done((f32[128,1024]{1,0:T(8,128)S(1)}, f32[128,1024]{1,0:T(8,128)S(1)}, u32[]{:S(2)}, u32[]{:S(2)}) %collective-permute-start.16) | collective-permute-done | bytes 524320 | tf_op jit(solution)/shard_map/ppermute | solution.py:12
  188.9 0.9 fusion.6
  189.9 1.0 fusion.3
  (27 shorter events, 0.2 us)
Async XLA Ops:
  0.6 21.7 %collective-permute-start.3 = (s32[128]{0:T(128)}, s32[128]{0:T(128)S(1)}, u32[]{:S(2)}, u32[]{:S(2)}) collective-permute-start(s32[128]{0:T(128)} %param.7), channel_id=1, source_target_pairs={{0,4},{4,8},{8,12},{12,0},{1,5},{5,9},{9,13},{13,1},{2,6},{6,10},{... | collective-permute-start | bytes 1544 | tf_op jit(solution)/shard_map/ppermute | solution.py:12
  4.6 19.9 %collective-permute-start.2 = (s32[128]{0:T(128)}, s32[128]{0:T(128)S(1)}, u32[]{:S(2)}, u32[]{:S(2)}) collective-permute-start(s32[128]{0:T(128)} %param.7), channel_id=1, source_target_pairs={{0,3},{1,0},{2,1},{3,2},{4,7},{5,4},{6,5},{7,6},{8,11},{9,8},{10,9... | collective-permute-start | bytes 1544 | tf_op jit(solution)/shard_map/ppermute | solution.py:12
  12.2 16.7 %collective-permute-start.1 = (s32[128]{0:T(128)}, s32[128]{0:T(128)S(1)}, u32[]{:S(2)}, u32[]{:S(2)}) collective-permute-start(s32[128]{0:T(128)} %param.7), channel_id=1, source_target_pairs={{0,2},{1,3},{2,0},{3,1},{4,6},{5,7},{6,4},{7,5},{8,10},{9,11},{10,... | collective-permute-start | bytes 1544 | tf_op jit(solution)/shard_map/ppermute | solution.py:12
  14.1 33.4 %collective-permute-start.7 = (bf16[128,1024]{1,0:T(8,128)(2,1)}, bf16[128,1024]{1,0:T(8,128)(2,1)S(1)}, u32[]{:S(2)}, u32[]{:S(2)}) collective-permute-start(bf16[128,1024]{1,0:T(8,128)(2,1)} %param.5), channel_id=1, source_target_pairs={{0,2},{1,3},{2,0},{3,1},{4,6},{5,7},{6,4},{7,5},{8,10},{9,11},{10,... | collective-permute-start | bytes 786440 | tf_op jit(solution)/shard_map/ppermute | solution.py:12
  18.4 24.9 %collective-permute-start.6 = (bf16[128,1024]{1,0:T(8,128)(2,1)}, bf16[128,1024]{1,0:T(8,128)(2,1)S(1)}, u32[]{:S(2)}, u32[]{:S(2)}) collective-permute-start(bf16[128,1024]{1,0:T(8,128)(2,1)} %param.5), channel_id=1, source_target_pairs={{0,1},{1,2},{2,3},{3,0},{4,5},{5,6},{6,7},{7,4},{8,9},{9,10},{10,1... | collective-permute-start | bytes 786440 | tf_op jit(solution)/shard_map/ppermute | solution.py:12
  22.3 11.0 %collective-permute-start = (s32[128]{0:T(128)}, s32[128]{0:T(128)S(1)}, u32[]{:S(2)}, u32[]{:S(2)}) collective-permute-start(s32[128]{0:T(128)} %param.7), channel_id=1, source_target_pairs={{0,1},{1,2},{2,3},{3,0},{4,5},{5,6},{6,7},{7,4},{8,9},{9,10},{10,1... | collective-permute-start | bytes 1544 | tf_op jit(solution)/shard_map/ppermute | solution.py:12
  24.5 13.7 %collective-permute-start.4 = (s32[128]{0:T(128)}, s32[128]{0:T(128)S(1)}, u32[]{:S(2)}, u32[]{:S(2)}) collective-permute-start(s32[128]{0:T(128)} %param.7), channel_id=1, source_target_pairs={{0,8},{4,12},{8,0},{12,4},{1,9},{5,13},{9,1},{13,5},{2,10},{6,14},... | collective-permute-start | bytes 1544 | tf_op jit(solution)/shard_map/ppermute | solution.py:12
  28.9 11.4 %collective-permute-start.5 = (s32[128]{0:T(128)}, s32[128]{0:T(128)S(1)}, u32[]{:S(2)}, u32[]{:S(2)}) collective-permute-start(s32[128]{0:T(128)} %param.7), channel_id=1, source_target_pairs={{0,12},{4,0},{8,4},{12,8},{1,13},{5,1},{9,5},{13,9},{2,14},{6,2},{... | collective-permute-start | bytes 1544 | tf_op jit(solution)/shard_map/ppermute | solution.py:12
  33.3 16.6 %collective-permute-start.8 = (bf16[128,1024]{1,0:T(8,128)(2,1)}, bf16[128,1024]{1,0:T(8,128)(2,1)S(1)}, u32[]{:S(2)}, u32[]{:S(2)}) collective-permute-start(bf16[128,1024]{1,0:T(8,128)(2,1)} %param.5), channel_id=1, source_target_pairs={{0,3},{1,0},{2,1},{3,2},{4,7},{5,4},{6,5},{7,6},{8,11},{9,8},{10,9... | collective-permute-start | bytes 786440 | tf_op jit(solution)/shard_map/ppermute | solution.py:12
  38.2 11.7 %collective-permute-start.10 = (bf16[128,1024]{1,0:T(8,128)(2,1)}, bf16[128,1024]{1,0:T(8,128)(2,1)S(1)}, u32[]{:S(2)}, u32[]{:S(2)}) collective-permute-start(bf16[128,1024]{1,0:T(8,128)(2,1)} %param.6), channel_id=1, source_target_pairs={{0,8},{4,12},{8,0},{12,4},{1,9},{5,13},{9,1},{13,5},{2,10},{6,14},... | collective-permute-start | bytes 786440 | tf_op jit(solution)/shard_map/ppermute | solution.py:12
  40.3 9.5 %collective-permute-start.9 = (bf16[128,1024]{1,0:T(8,128)(2,1)}, bf16[128,1024]{1,0:T(8,128)(2,1)S(1)}, u32[]{:S(2)}, u32[]{:S(2)}) collective-permute-start(bf16[128,1024]{1,0:T(8,128)(2,1)} %param.6), channel_id=1, source_target_pairs={{0,4},{4,8},{8,12},{12,0},{1,5},{5,9},{9,13},{13,1},{2,6},{6,10},{... | collective-permute-start | bytes 786440 | tf_op jit(solution)/shard_map/ppermute | solution.py:12
  43.3 7.9 %collective-permute-start.11 = (bf16[128,1024]{1,0:T(8,128)(2,1)}, bf16[128,1024]{1,0:T(8,128)(2,1)S(1)}, u32[]{:S(2)}, u32[]{:S(2)}) collective-permute-start(bf16[128,1024]{1,0:T(8,128)(2,1)} %param.6), channel_id=1, source_target_pairs={{0,12},{4,0},{8,4},{12,8},{1,13},{5,1},{9,5},{13,9},{2,14},{6,2},{... | collective-permute-start | bytes 786440 | tf_op jit(solution)/shard_map/ppermute | solution.py:12
  55.8 96.5 %collective-permute-start.12 = (f32[128]{0:T(128)S(1)}, f32[128]{0:T(128)S(1)}, u32[]{:S(2)}, u32[]{:S(2)}) collective-permute-start(f32[128]{0:T(128)S(1)} %get-tuple-element.14), channel_id=1, source_target_pairs={{0,3},{1,0},{2,1},{3,2},{4,7},{5,4},{6,5},{7,6},{8,11},{9,8},{10,9... | collective-permute-start | bytes 1544 | tf_op jit(solution)/shard_map/ppermute | solution.py:12
  62.0 93.3 %collective-permute-start.14 = (f32[128]{0:T(128)S(1)}, f32[128]{0:T(128)S(1)}, u32[]{:S(2)}, u32[]{:S(2)}) collective-permute-start(f32[128]{0:T(128)S(1)} %get-tuple-element.15), channel_id=1, source_target_pairs={{0,1},{1,2},{2,3},{3,0},{4,5},{5,6},{6,7},{7,4},{8,9},{9,10},{10,1... | collective-permute-start | bytes 1544 | tf_op jit(solution)/shard_map/ppermute | solution.py:12
  64.0 96.1 %collective-permute-start.13 = (f32[128]{0:T(128)S(1)}, f32[128]{0:T(128)S(1)}, u32[]{:S(2)}, u32[]{:S(2)}) collective-permute-start(f32[128]{0:T(128)S(1)} %get-tuple-element.16), channel_id=1, source_target_pairs={{0,2},{1,3},{2,0},{3,1},{4,6},{5,7},{6,4},{7,5},{8,10},{9,11},{10,... | collective-permute-start | bytes 1544 | tf_op jit(solution)/shard_map/ppermute | solution.py:12
  67.5 16.4 %collective-permute-start.21 = (f32[2]{0:T(128)S(1)}, f32[2]{0:T(128)S(1)}, u32[]{:S(2)}, u32[]{:S(2)}) collective-permute-start(f32[2]{0:T(128)S(1)} %pad_maximum_fusion), channel_id=1, source_target_pairs={{0,16},{16,0},{32,48},{48,32},{64,80},{80,64},{96,112},{112,96},{1... | collective-permute-start | bytes 32 | tf_op jit(solution)/shard_map/ppermute | solution.py:33
  79.9 82.1 %collective-permute-start.15 = (f32[128,1024]{1,0:T(8,128)S(1)}, f32[128,1024]{1,0:T(8,128)S(1)}, u32[]{:S(2)}, u32[]{:S(2)}) collective-permute-start(f32[128,1024]{1,0:T(8,128)S(1)} %get-tuple-element.11), channel_id=1, source_target_pairs={{0,3},{1,0},{2,1},{3,2},{4,7},{5,4},{6,5},{7,6},{8,11},{9,8},{10,9... | collective-permute-start | bytes 1572872 | tf_op jit(solution)/shard_map/ppermute | solution.py:12
  85.3 9.9 %collective-permute-start.22 = (f32[2]{0:T(128)S(1)}, f32[2]{0:T(128)S(1)}, u32[]{:S(2)}, u32[]{:S(2)}) collective-permute-start(f32[2]{0:T(128)S(1)} %fusion.24), channel_id=1, source_target_pairs={{0,32},{16,48},{32,0},{48,16},{64,96},{80,112},{96,64},{112,80},{1... | collective-permute-start | bytes 32 | tf_op jit(solution)/shard_map/ppermute | solution.py:33
  96.6 13.0 %collective-permute-start.23 = (f32[2]{0:T(128)S(1)}, f32[2]{0:T(128)S(1)}, u32[]{:S(2)}, u32[]{:S(2)}) collective-permute-start(f32[2]{0:T(128)S(1)} %fusion.25), channel_id=1, source_target_pairs={{0,64},{16,80},{32,96},{48,112},{64,0},{80,16},{96,32},{112,48},{1... | collective-permute-start | bytes 32 | tf_op jit(solution)/shard_map/ppermute | solution.py:33
  109.6 4.3 %collective-permute-start.24 = (f32[2]{0:T(128)S(1)}, f32[2]{0:T(128)S(1)}, u32[]{:S(2)}, u32[]{:S(2)}) collective-permute-start(f32[2]{0:T(128)S(1)} %add.85), channel_id=1, source_target_pairs={{0,128},{16,144},{32,160},{48,176},{64,192},{80,208},{96,224},{112... | collective-permute-start | bytes 32 | tf_op jit(solution)/shard_map/ppermute | solution.py:33
  113.9 5.2 %collective-permute-start.25 = (f32[2]{0:T(128)S(1)}, f32[2]{0:T(128)S(1)}, u32[]{:S(2)}, u32[]{:S(2)}) collective-permute-start(f32[2]{0:T(128)S(1)} %add.86), channel_id=1, source_target_pairs={{0,256},{16,272},{32,288},{48,304},{64,320},{80,336},{96,352},{112... | collective-permute-start | bytes 32 | tf_op jit(solution)/shard_map/ppermute | solution.py:33
  119.1 8.2 %collective-permute-start.26 = (f32[2]{0:T(128)S(1)}, f32[2]{0:T(128)S(1)}, u32[]{:S(2)}, u32[]{:S(2)}) collective-permute-start(f32[2]{0:T(128)S(1)} %add.87), channel_id=1, source_target_pairs={{0,512},{16,528},{32,544},{48,560},{64,576},{80,592},{96,608},{112... | collective-permute-start | bytes 32 | tf_op jit(solution)/shard_map/ppermute | solution.py:33
  127.3 4.3 %collective-permute-start.27 = (f32[2]{0:T(128)S(1)}, f32[2]{0:T(128)S(1)}, u32[]{:S(2)}, u32[]{:S(2)}) collective-permute-start(f32[2]{0:T(128)S(1)} %add.88), channel_id=1, source_target_pairs={{0,4},{4,0},{8,12},{12,8},{1,5},{5,1},{9,13},{13,9},{2,6},{6,2},{1... | collective-permute-start | bytes 32 | tf_op jit(solution)/shard_map/ppermute | solution.py:33
  131.6 5.9 %collective-permute-start.28 = (f32[2]{0:T(128)S(1)}, f32[2]{0:T(128)S(1)}, u32[]{:S(2)}, u32[]{:S(2)}) collective-permute-start(f32[2]{0:T(128)S(1)} %add.89), channel_id=1, source_target_pairs={{0,8},{4,12},{8,0},{12,4},{1,9},{5,13},{9,1},{13,5},{2,10},{6,14},... | collective-permute-start | bytes 32 | tf_op jit(solution)/shard_map/ppermute | solution.py:33
  137.5 6.2 %collective-permute-start.29 = (f32[2]{0:T(128)S(1)}, f32[2]{0:T(128)S(1)}, u32[]{:S(2)}, u32[]{:S(2)}) collective-permute-start(f32[2]{0:T(128)S(1)} %add.90), channel_id=1, source_target_pairs={{0,1},{1,0},{2,3},{3,2},{4,5},{5,4},{6,7},{7,6},{8,9},{9,8},{10,11... | collective-permute-start | bytes 32 | tf_op jit(solution)/shard_map/ppermute | solution.py:33
  143.7 5.2 %collective-permute-start.30 = (f32[2]{0:T(128)S(1)}, f32[2]{0:T(128)S(1)}, u32[]{:S(2)}, u32[]{:S(2)}) collective-permute-start(f32[2]{0:T(128)S(1)} %add.91), channel_id=1, source_target_pairs={{0,2},{1,3},{2,0},{3,1},{4,6},{5,7},{6,4},{7,5},{8,10},{9,11},{10,... | collective-permute-start | bytes 32 | tf_op jit(solution)/shard_map/ppermute | solution.py:33
  148.9 18.6 %collective-permute-start.17 = (f32[128,1024]{1,0:T(8,128)S(1)}, f32[128,1024]{1,0:T(8,128)S(1)}, u32[]{:S(2)}, u32[]{:S(2)}) collective-permute-start(f32[128,1024]{1,0:T(8,128)S(1)} %get-tuple-element.12), channel_id=1, source_target_pairs={{0,1},{1,2},{2,3},{3,0},{4,5},{5,6},{6,7},{7,4},{8,9},{9,10},{10,1... | collective-permute-start | bytes 1572872 | tf_op jit(solution)/shard_map/ppermute | solution.py:12
  152.3 36.6 %collective-permute-start.16 = (f32[128,1024]{1,0:T(8,128)S(1)}, f32[128,1024]{1,0:T(8,128)S(1)}, u32[]{:S(2)}, u32[]{:S(2)}) collective-permute-start(f32[128,1024]{1,0:T(8,128)S(1)} %get-tuple-element.13), channel_id=1, source_target_pairs={{0,2},{1,3},{2,0},{3,1},{4,6},{5,7},{6,4},{7,5},{8,10},{9,11},{10,... | collective-permute-start | bytes 1572872 | tf_op jit(solution)/shard_map/ppermute | solution.py:12
  155.3 34.6 %collective-permute-start.18 = (f32[128,1024]{1,0:T(8,128)S(1)}, f32[128,1024]{1,0:T(8,128)S(1)}, u32[]{:S(2)}, u32[]{:S(2)}) collective-permute-start(f32[128,1024]{1,0:T(8,128)S(1)} %get-tuple-element.8), channel_id=1, source_target_pairs={{0,12},{4,0},{8,4},{12,8},{1,13},{5,1},{9,5},{13,9},{2,14},{6,2},{... | collective-permute-start | bytes 1572872 | tf_op jit(solution)/shard_map/ppermute | solution.py:12
  160.1 29.8 %collective-permute-start.20 = (f32[128,1024]{1,0:T(8,128)S(1)}, f32[128,1024]{1,0:T(8,128)S(1)}, u32[]{:S(2)}, u32[]{:S(2)}) collective-permute-start(f32[128,1024]{1,0:T(8,128)S(1)} %get-tuple-element.9), channel_id=1, source_target_pairs={{0,4},{4,8},{8,12},{12,0},{1,5},{5,9},{9,13},{13,1},{2,6},{6,10},{... | collective-permute-start | bytes 1572872 | tf_op jit(solution)/shard_map/ppermute | solution.py:12
  162.0 27.9 %collective-permute-start.19 = (f32[128,1024]{1,0:T(8,128)S(1)}, f32[128,1024]{1,0:T(8,128)S(1)}, u32[]{:S(2)}, u32[]{:S(2)}) collective-permute-start(f32[128,1024]{1,0:T(8,128)S(1)} %get-tuple-element.10), channel_id=1, source_target_pairs={{0,8},{4,12},{8,0},{12,4},{1,9},{5,13},{9,1},{13,5},{2,10},{6,14},... | collective-permute-start | bytes 1572872 | tf_op jit(solution)/shard_map/ppermute | solution.py:12

commit v3 on v2

--- a/solution.py
+++ b/solution.py
@@ -25,6 +25,30 @@
     return total
 
 
+def with_labels(block, labels):
+    rows, width = block.shape
+    assert rows <= width
+    shifts = 8 * jnp.arange(4, dtype=jnp.int32)
+    digits = (labels[None, :] >> shifts[:, None]) & 255
+    tail = jnp.zeros((16, width), block.dtype).at[:4, :rows].set(digits.astype(block.dtype))
+    return jnp.concatenate([block, tail], axis=0)
+
+
+def split_labels(gathered, rows):
+    width = gathered.shape[1]
+    pieces = gathered.reshape(-1, rows + 16, width)
+    data = pieces[:, :rows].reshape(-1, width)
+    digits = pieces[:, rows : rows + 4, :rows].astype(jnp.int32)
+    labels = digits[:, 0] | (digits[:, 1] << 8) | (digits[:, 2] << 16) | (digits[:, 3] << 24)
+    return data, labels.reshape(-1)
+
+
+def with_loss(grad_part, loss_part):
+    count, rows, width = grad_part.shape
+    tail = jnp.zeros((count, 8, width), grad_part.dtype).at[:, 0, :rows].set(loss_part)
+    return jnp.concatenate([grad_part, tail], axis=1)
+
+
 def total_sums(sums, axes):
     for axis in axes:
         count = lax.axis_size(axis)
@@ -42,10 +66,8 @@
     ncol = lax.axis_size("bx")
     root = math.sqrt(width)
     scale = temp / root
-    row_informal = gather_by_shift(informal, "bz")
-    row_labels = gather_by_shift(labels, "bz")
-    col_formal = gather_by_shift(formal, "bx")
-    col_labels = gather_by_shift(labels, "bx")
+    row_informal, row_labels = split_labels(gather_by_shift(with_labels(informal, labels), "bz"), rows)
+    col_formal, col_labels = split_labels(gather_by_shift(with_labels(formal, labels), "bx"), rows)
     raw = lax.dot_general(row_informal, col_formal, (((1,), (1,)), ((), ())), preferred_element_type=jnp.float32) / root
     logits = temp * raw + bias
     sign = jnp.where(row_labels[:, None] == col_labels[None, :], 1.0, -1.0).astype(jnp.float32)
@@ -54,8 +76,9 @@
     weights = slope.astype(jnp.bfloat16)
     grad_x_part = jnp.dot(weights, col_formal, preferred_element_type=jnp.float32)
     grad_y_part = lax.dot_general(weights, row_informal, (((0,), (0,)), ((), ())), preferred_element_type=jnp.float32)
-    loss_sum = reduce_by_shift(loss_part.reshape(nrow, rows), "bz")
-    grad_x = scale * reduce_by_shift(grad_x_part.reshape(nrow, rows, width), "bz")
+    packed = reduce_by_shift(with_loss(grad_x_part.reshape(nrow, rows, width), loss_part.reshape(nrow, rows)), "bz")
+    loss_sum = packed[rows, :rows]
+    grad_x = scale * packed[:rows]
     grad_y = scale * reduce_by_shift(grad_y_part.reshape(ncol, rows, width), "bx")
     sums = total_sums(jnp.stack([jnp.sum(slope * raw), jnp.sum(slope)]), ("group", "bx", "bz"))
     set_size = rows * nrow * ncol

time: 194 us -> 178 us (0.918)
  starting transfers between devices: 124 us -> 109 us
  waiting for transfers between devices: 48.4 us -> 44.4 us
  local copies, waits for them, and re-layouts: 2.98 us -> 5.23 us
  other arithmetic: 7.22 us -> 9.35 us
  matrix products: 4.5 us -> 2.44 us
    ppermute x21 -> x12, starting transfers between devices: 73.1 us -> 42.7 us  [shifted(): lax.ppermute(value, axis, [(i, (i + by) % count) for i in range(count)])]
    ppermute x10, starting transfers between devices: 50.9 us -> 66.5 us  [total_sums(): lax.ppermute(sums, axis, [(i, i ^ step) for i in range(count)])]
    ppermute x10, waiting for transfers between devices: 23.4 us -> 13.1 us  [total_sums(): lax.ppermute(sums, axis, [(i, i ^ step) for i in range(count)])]
    ppermute x21 -> x12, waiting for transfers between devices: 25 us -> 31.4 us  [shifted(): lax.ppermute(value, axis, [(i, (i + by) % count) for i in range(count)])]
  transfers between devices with their start and end apart: 31 -> 22, of which waited for: 12 -> 12; matrix products, arithmetic and copies ran while one was open for 5% -> 5% of each run, Pallas kernels for 0% -> 0%
where the time goes in v3:
time: 178 us; the launch traced here: 177 us
  starting transfers between devices  109 us (61%)
  waiting for transfers between devices  44.4 us (25%)
  other arithmetic  9.35 us (5%)
  between operations  5.9 us (3%)
  local copies, waits for them, and re-layouts  5.23 us (3%)
  matrix products  2.44 us (1%)
    ppermute x10, starting transfers between devices, total_sums(): lax.ppermute(sums, axis, [(i, i ^ step) for i in range(count)])  66.5 us
    ppermute x12, starting transfers between devices, shifted(): lax.ppermute(value, axis, [(i, (i + by) % count) for i in range(count)])  42.7 us
    ppermute x12, waiting for transfers between devices, shifted(): lax.ppermute(value, axis, [(i, (i + by) % count) for i in range(count)])  31.4 us
    ppermute x10, waiting for transfers between devices, total_sums(): lax.ppermute(sums, axis, [(i, i ^ step) for i in range(count)])  13.1 us
  transfers between devices with their start and end apart: 22, of which 12 were waited for; matrix products, arithmetic and copies ran while one was open for 5% of the time, Pallas kernels for 0%

profile of v3, /device:TPU:1, one launch (start us, length us, event | category | flops | bytes accessed | tf_op | source)
XLA Modules:
  0.0 176.6 jit_solution(1465858504259997469)
XLA Ops:
  0.6 0.0 copy-start
  0.6 0.0 copy-start.1
  0.7 1.1 constant_dynamic-update-slice_fusion.3
  1.8 0.7 and_convert_fusion
  2.6 4.8 %collective-permute-start = (bf16[144,1024]{1,0:T(8,128)(2,1)S(1)}, bf16[144,1024]{1,0:T(8,128)(2,1)}, u32[]{:S(2)}, u32[]{:S(2)}) collective-permute-start(bf16[144,1024]{1,0:T(8,128)(2,1)S(1)} %get-tuple-element.49), channel_id=1, source_target_pairs={{0,1},{1,2},{2,3},{3,0},{4,5},{5,6},{6,7},{7,4},{8,9},{9,10},{10,1... | collective-permute-start | bytes 884744 | tf_op jit(solution)/shard_map/ppermute | solution.py:12
  7.4 5.8 %collective-permute-start.1 = (bf16[144,1024]{1,0:T(8,128)(2,1)S(1)}, bf16[144,1024]{1,0:T(8,128)(2,1)}, u32[]{:S(2)}, u32[]{:S(2)}) collective-permute-start(bf16[144,1024]{1,0:T(8,128)(2,1)S(1)} %get-tuple-element.49), channel_id=1, source_target_pairs={{0,2},{1,3},{2,0},{3,1},{4,6},{5,7},{6,4},{7,5},{8,10},{9,11},{10,... | collective-permute-start | bytes 884744 | tf_op jit(solution)/shard_map/ppermute | solution.py:12
  13.2 2.2 %collective-permute-start.2 = (bf16[144,1024]{1,0:T(8,128)(2,1)S(1)}, bf16[144,1024]{1,0:T(8,128)(2,1)}, u32[]{:S(2)}, u32[]{:S(2)}) collective-permute-start(bf16[144,1024]{1,0:T(8,128)(2,1)S(1)} %get-tuple-element.49), channel_id=1, source_target_pairs={{0,3},{1,0},{2,1},{3,2},{4,7},{5,4},{6,5},{7,6},{8,11},{9,8},{10,9... | collective-permute-start | bytes 884744 | tf_op jit(solution)/shard_map/ppermute | solution.py:12
  15.4 3.1 %collective-permute-start.3 = (bf16[144,1024]{1,0:T(8,128)(2,1)S(1)}, bf16[144,1024]{1,0:T(8,128)(2,1)S(1)}, u32[]{:S(2)}, u32[]{:S(2)}) collective-permute-start(bf16[144,1024]{1,0:T(8,128)(2,1)S(1)} %get-tuple-element.48), channel_id=1, source_target_pairs={{0,4},{4,8},{8,12},{12,0},{1,5},{5,9},{9,13},{13,1},{2,6},{6,10},{... | collective-permute-start | bytes 884744 | tf_op jit(solution)/shard_map/ppermute | solution.py:12
  18.6 4.4 %collective-permute-start.4 = (bf16[144,1024]{1,0:T(8,128)(2,1)S(1)}, bf16[144,1024]{1,0:T(8,128)(2,1)S(1)}, u32[]{:S(2)}, u32[]{:S(2)}) collective-permute-start(bf16[144,1024]{1,0:T(8,128)(2,1)S(1)} %get-tuple-element.48), channel_id=1, source_target_pairs={{0,8},{4,12},{8,0},{12,4},{1,9},{5,13},{9,1},{13,5},{2,10},{6,14},... | collective-permute-start | bytes 884744 | tf_op jit(solution)/shard_map/ppermute | solution.py:12
  24.2 3.1 %collective-permute-start.5 = (bf16[144,1024]{1,0:T(8,128)(2,1)S(1)}, bf16[144,1024]{1,0:T(8,128)(2,1)S(1)}, u32[]{:S(2)}, u32[]{:S(2)}) collective-permute-start(bf16[144,1024]{1,0:T(8,128)(2,1)S(1)} %get-tuple-element.48), channel_id=1, source_target_pairs={{0,12},{4,0},{8,4},{12,8},{1,13},{5,1},{9,5},{13,9},{2,14},{6,2},{... | collective-permute-start | bytes 884744 | tf_op jit(solution)/shard_map/ppermute | solution.py:12
  27.3 1.0 constant_dynamic-update-slice_fusion.2
  28.3 1.0 constant_dynamic-update-slice_fusion.1
  29.3 0.0 collective-permute-done.2
  29.3 1.0 constant_dynamic-update-slice_fusion
  30.3 0.1 slice.164
  30.4 1.0 collective-permute-done.4
  31.5 0.6 collective-permute-done.5
  32.1 0.1 slice.165
  32.3 1.0 fusion.14
  33.3 1.6 multiply_reduce_fusion
  34.9 1.4 pad_maximum_fusion.2
  36.3 11.9 %collective-permute-start.12 = (f32[2]{0:T(128)S(1)}, f32[2]{0:T(128)S(1)}, u32[]{:S(2)}, u32[]{:S(2)}) collective-permute-start(f32[2]{0:T(128)S(1)} %pad_maximum_fusion.2), channel_id=1, source_target_pairs={{0,16},{16,0},{32,48},{48,32},{64,80},{80,64},{96,112},{112,96},{1... | collective-permute-start | bytes 32 | tf_op jit(solution)/shard_map/ppermute | solution.py:57
  48.2 0.7 fusion.18
  48.9 0.2 fusion.15
  49.1 3.2 %collective-permute-start.10 = (f32[128,1024]{1,0:T(8,128)S(1)}, f32[128,1024]{1,0:T(8,128)S(1)}, u32[]{:S(2)}, u32[]{:S(2)}) collective-permute-start(f32[128,1024]{1,0:T(8,128)S(1)} %get-tuple-element.47), channel_id=1, source_target_pairs={{0,8},{4,12},{8,0},{12,4},{1,9},{5,13},{9,1},{13,5},{2,10},{6,14},... | collective-permute-start | bytes 1572872 | tf_op jit(solution)/shard_map/ppermute | solution.py:12
  52.4 3.5 %collective-permute-start.11 = (f32[128,1024]{1,0:T(8,128)S(1)}, f32[128,1024]{1,0:T(8,128)S(1)}, u32[]{:S(2)}, u32[]{:S(2)}) collective-permute-start(f32[128,1024]{1,0:T(8,128)S(1)} %get-tuple-element.46), channel_id=1, source_target_pairs={{0,4},{4,8},{8,12},{12,0},{1,5},{5,9},{9,13},{13,1},{2,6},{6,10},{... | collective-permute-start | bytes 1572872 | tf_op jit(solution)/shard_map/ppermute | solution.py:12
  55.8 3.1 %collective-permute-start.9 = (f32[128,1024]{1,0:T(8,128)S(1)}, f32[128,1024]{1,0:T(8,128)S(1)}, u32[]{:S(2)}, u32[]{:S(2)}) collective-permute-start(f32[128,1024]{1,0:T(8,128)S(1)} %get-tuple-element.45), channel_id=1, source_target_pairs={{0,12},{4,0},{8,4},{12,8},{1,13},{5,1},{9,5},{13,9},{2,14},{6,2},{... | collective-permute-start | bytes 1572872 | tf_op jit(solution)/shard_map/ppermute | solution.py:12
  59.0 0.7 fusion.17
  59.7 0.3 select_maximum_fusion
  60.0 0.1 slice_bitcast_fusion.2
  60.2 2.2 %collective-permute-start.6 = (f32[136,1024]{1,0:T(8,128)S(1)}, f32[136,1024]{1,0:T(8,128)S(1)}, u32[]{:S(2)}, u32[]{:S(2)}) collective-permute-start(f32[136,1024]{1,0:T(8,128)S(1)} %get-tuple-element.42), channel_id=1, source_target_pairs={{0,3},{1,0},{2,1},{3,2},{4,7},{5,4},{6,5},{7,6},{8,11},{9,8},{10,9... | collective-permute-start | bytes 1671176 | tf_op jit(solution)/shard_map/ppermute | solution.py:12
  62.4 0.0 collective-permute-done.12
  62.4 1.4 fusion.25
  63.7 10.3 %collective-permute-start.13 = (f32[2]{0:T(128)S(1)}, f32[2]{0:T(128)S(1)}, u32[]{:S(2)}, u32[]{:S(2)}) collective-permute-start(f32[2]{0:T(128)S(1)} %fusion.25), channel_id=1, source_target_pairs={{0,32},{16,48},{32,0},{48,16},{64,96},{80,112},{96,64},{112,80},{1... | collective-permute-start | bytes 32 | tf_op jit(solution)/shard_map/ppermute | solution.py:57
  74.0 1.0 collective-permute-done.13
  75.0 1.4 fusion.26
  76.4 15.5 %collective-permute-start.14 = (f32[2]{0:T(128)S(1)}, f32[2]{0:T(128)S(1)}, u32[]{:S(2)}, u32[]{:S(2)}) collective-permute-start(f32[2]{0:T(128)S(1)} %fusion.26), channel_id=1, source_target_pairs={{0,64},{16,80},{32,96},{48,112},{64,0},{80,16},{96,32},{112,48},{1... | collective-permute-start | bytes 32 | tf_op jit(solution)/shard_map/ppermute | solution.py:57
  91.8 0.9 collective-permute-done.14
  92.8 3.2 %collective-permute-start.15 = (f32[2]{0:T(128)S(1)}, f32[2]{0:T(128)S(1)}, u32[]{:S(2)}, u32[]{:S(2)}) collective-permute-start(f32[2]{0:T(128)S(1)} %add.82), channel_id=1, source_target_pairs={{0,128},{16,144},{32,160},{48,176},{64,192},{80,208},{96,224},{112... | collective-permute-start | bytes 32 | tf_op jit(solution)/shard_map/ppermute | solution.py:57
  96.0 1.1 collective-permute-done.15
  97.1 4.2 %collective-permute-start.16 = (f32[2]{0:T(128)S(1)}, f32[2]{0:T(128)S(1)}, u32[]{:S(2)}, u32[]{:S(2)}) collective-permute-start(f32[2]{0:T(128)S(1)} %add.83), channel_id=1, source_target_pairs={{0,256},{16,272},{32,288},{48,304},{64,320},{80,336},{96,352},{112... | collective-permute-start | bytes 32 | tf_op jit(solution)/shard_map/ppermute | solution.py:57
  101.3 1.0 collective-permute-done.16
  102.3 7.4 %collective-permute-start.17 = (f32[2]{0:T(128)S(1)}, f32[2]{0:T(128)S(1)}, u32[]{:S(2)}, u32[]{:S(2)}) collective-permute-start(f32[2]{0:T(128)S(1)} %add.84), channel_id=1, source_target_pairs={{0,512},{16,528},{32,544},{48,560},{64,576},{80,592},{96,608},{112... | collective-permute-start | bytes 32 | tf_op jit(solution)/shard_map/ppermute | solution.py:57
  109.7 0.9 collective-permute-done.17
  110.7 1.9 %collective-permute-start.18 = (f32[2]{0:T(128)S(1)}, f32[2]{0:T(128)S(1)}, u32[]{:S(2)}, u32[]{:S(2)}) collective-permute-start(f32[2]{0:T(128)S(1)} %add.85), channel_id=1, source_target_pairs={{0,4},{4,0},{8,12},{12,8},{1,5},{5,1},{9,13},{13,9},{2,6},{6,2},{1... | collective-permute-start | bytes 32 | tf_op jit(solution)/shard_map/ppermute | solution.py:57
  112.6 2.4 %collective-permute-done.18 = f32[2]{0:T(128)S(1)} collective-permute-done((f32[2]{0:T(128)S(1)}, f32[2]{0:T(128)S(1)}, u32[]{:S(2)}, u32[]{:S(2)}) %collective-permute-start.18) | collective-permute-done | bytes 40 | tf_op jit(solution)/shard_map/ppermute | solution.py:57
  115.0 1.9 %collective-permute-start.19 = (f32[2]{0:T(128)S(1)}, f32[2]{0:T(128)S(1)}, u32[]{:S(2)}, u32[]{:S(2)}) collective-permute-start(f32[2]{0:T(128)S(1)} %add.86), channel_id=1, source_target_pairs={{0,8},{4,12},{8,0},{12,4},{1,9},{5,13},{9,1},{13,5},{2,10},{6,14},... | collective-permute-start | bytes 32 | tf_op jit(solution)/shard_map/ppermute | solution.py:57
  116.9 3.9 %collective-permute-done.19 = f32[2]{0:T(128)S(1)} collective-permute-done((f32[2]{0:T(128)S(1)}, f32[2]{0:T(128)S(1)}, u32[]{:S(2)}, u32[]{:S(2)}) %collective-permute-start.19) | collective-permute-done | bytes 40 | tf_op jit(solution)/shard_map/ppermute | solution.py:57
  120.8 4.9 %collective-permute-start.20 = (f32[2]{0:T(128)S(1)}, f32[2]{0:T(128)S(1)}, u32[]{:S(2)}, u32[]{:S(2)}) collective-permute-start(f32[2]{0:T(128)S(1)} %add.87), channel_id=1, source_target_pairs={{0,1},{1,0},{2,3},{3,2},{4,5},{5,4},{6,7},{7,6},{8,9},{9,8},{10,11... | collective-permute-start | bytes 32 | tf_op jit(solution)/shard_map/ppermute | solution.py:57
  125.6 0.9 collective-permute-done.20
  126.6 5.3 %collective-permute-start.21 = (f32[2]{0:T(128)S(1)}, f32[2]{0:T(128)S(1)}, u32[]{:S(2)}, u32[]{:S(2)}) collective-permute-start(f32[2]{0:T(128)S(1)} %add.88), channel_id=1, source_target_pairs={{0,2},{1,3},{2,0},{3,1},{4,6},{5,7},{6,4},{7,5},{8,10},{9,11},{10,... | collective-permute-start | bytes 32 | tf_op jit(solution)/shard_map/ppermute | solution.py:57
  131.9 0.9 collective-permute-done.21
  132.9 4.2 %collective-permute-start.7 = (f32[136,1024]{1,0:T(8,128)S(1)}, f32[136,1024]{1,0:T(8,128)S(1)}, u32[]{:S(2)}, u32[]{:S(2)}) collective-permute-start(f32[136,1024]{1,0:T(8,128)S(1)} %get-tuple-element.44), channel_id=1, source_target_pairs={{0,2},{1,3},{2,0},{3,1},{4,6},{5,7},{6,4},{7,5},{8,10},{9,11},{10,... | collective-permute-start | bytes 1671176 | tf_op jit(solution)/shard_map/ppermute | solution.py:12
  137.1 0.0 collective-permute-done.10
  137.2 3.1 %collective-permute-start.8 = (f32[136,1024]{1,0:T(8,128)S(1)}, f32[136,1024]{1,0:T(8,128)S(1)}, u32[]{:S(2)}, u32[]{:S(2)}) collective-permute-start(f32[136,1024]{1,0:T(8,128)S(1)} %get-tuple-element.43), channel_id=1, source_target_pairs={{0,1},{1,2},{2,3},{3,0},{4,5},{5,6},{6,7},{7,4},{8,9},{9,10},{10,1... | collective-permute-start | bytes 1671176 | tf_op jit(solution)/shard_map/ppermute | solution.py:12
  140.3 0.6 fusion.16
  142.1 0.0 collective-permute-done.11
  142.2 0.0 collective-permute-done.9
  142.2 1.0 fusion.6
  143.1 0.0 collective-permute-done.6
  143.1 29.7 %collective-permute-done.7 = f32[136,1024]{1,0:T(8,128)S(1)} collective-permute-done((f32[136,1024]{1,0:T(8,128)S(1)}, f32[136,1024]{1,0:T(8,128)S(1)}, u32[]{:S(2)}, u32[]{:S(2)}) %collective-permute-start.7) | collective-permute-done | bytes 557088 | tf_op jit(solution)/shard_map/ppermute | solution.py:12
  172.8 0.2 fusion.3
  173.0 0.8 slice_multiply_fusion
  173.9 0.5 fusion.13
  (24 shorter events, 0.2 us)
Async XLA Ops:
  0.6 1.9 %copy-start = (bf16[128,1024]{1,0:T(8,128)(2,1)S(1)}, bf16[128,1024]{1,0:T(8,128)(2,1)}, u32[]{:S(2)}) copy-start(bf16[128,1024]{1,0:T(8,128)(2,1)} %param.11) | copy-start | bytes 786436
  0.6 1.9 %copy-start.1 = (bf16[128,1024]{1,0:T(8,128)(2,1)S(1)}, bf16[128,1024]{1,0:T(8,128)(2,1)}, u32[]{:S(2)}) copy-start(bf16[128,1024]{1,0:T(8,128)(2,1)} %param.12) | copy-start | bytes 786436
  2.6 21.6 %collective-permute-start = (bf16[144,1024]{1,0:T(8,128)(2,1)S(1)}, bf16[144,1024]{1,0:T(8,128)(2,1)}, u32[]{:S(2)}, u32[]{:S(2)}) collective-permute-start(bf16[144,1024]{1,0:T(8,128)(2,1)S(1)} %get-tuple-element.49), channel_id=1, source_target_pairs={{0,1},{1,2},{2,3},{3,0},{4,5},{5,6},{6,7},{7,4},{8,9},{9,10},{10,1... | collective-permute-start | bytes 884744 | tf_op jit(solution)/shard_map/ppermute | solution.py:12
  7.4 20.9 %collective-permute-start.1 = (bf16[144,1024]{1,0:T(8,128)(2,1)S(1)}, bf16[144,1024]{1,0:T(8,128)(2,1)}, u32[]{:S(2)}, u32[]{:S(2)}) collective-permute-start(bf16[144,1024]{1,0:T(8,128)(2,1)S(1)} %get-tuple-element.49), channel_id=1, source_target_pairs={{0,2},{1,3},{2,0},{3,1},{4,6},{5,7},{6,4},{7,5},{8,10},{9,11},{10,... | collective-permute-start | bytes 884744 | tf_op jit(solution)/shard_map/ppermute | solution.py:12
  13.2 16.0 %collective-permute-start.2 = (bf16[144,1024]{1,0:T(8,128)(2,1)S(1)}, bf16[144,1024]{1,0:T(8,128)(2,1)}, u32[]{:S(2)}, u32[]{:S(2)}) collective-permute-start(bf16[144,1024]{1,0:T(8,128)(2,1)S(1)} %get-tuple-element.49), channel_id=1, source_target_pairs={{0,3},{1,0},{2,1},{3,2},{4,7},{5,4},{6,5},{7,6},{8,11},{9,8},{10,9... | collective-permute-start | bytes 884744 | tf_op jit(solution)/shard_map/ppermute | solution.py:12
  15.4 15.0 %collective-permute-start.3 = (bf16[144,1024]{1,0:T(8,128)(2,1)S(1)}, bf16[144,1024]{1,0:T(8,128)(2,1)S(1)}, u32[]{:S(2)}, u32[]{:S(2)}) collective-permute-start(bf16[144,1024]{1,0:T(8,128)(2,1)S(1)} %get-tuple-element.48), channel_id=1, source_target_pairs={{0,4},{4,8},{8,12},{12,0},{1,5},{5,9},{9,13},{13,1},{2,6},{6,10},{... | collective-permute-start | bytes 884744 | tf_op jit(solution)/shard_map/ppermute | solution.py:12
  18.6 12.9 %collective-permute-start.4 = (bf16[144,1024]{1,0:T(8,128)(2,1)S(1)}, bf16[144,1024]{1,0:T(8,128)(2,1)S(1)}, u32[]{:S(2)}, u32[]{:S(2)}) collective-permute-start(bf16[144,1024]{1,0:T(8,128)(2,1)S(1)} %get-tuple-element.48), channel_id=1, source_target_pairs={{0,8},{4,12},{8,0},{12,4},{1,9},{5,13},{9,1},{13,5},{2,10},{6,14},... | collective-permute-start | bytes 884744 | tf_op jit(solution)/shard_map/ppermute | solution.py:12
  24.2 7.9 %collective-permute-start.5 = (bf16[144,1024]{1,0:T(8,128)(2,1)S(1)}, bf16[144,1024]{1,0:T(8,128)(2,1)S(1)}, u32[]{:S(2)}, u32[]{:S(2)}) collective-permute-start(bf16[144,1024]{1,0:T(8,128)(2,1)S(1)} %get-tuple-element.48), channel_id=1, source_target_pairs={{0,12},{4,0},{8,4},{12,8},{1,13},{5,1},{9,5},{13,9},{2,14},{6,2},{... | collective-permute-start | bytes 884744 | tf_op jit(solution)/shard_map/ppermute | solution.py:12
  36.3 26.1 %collective-permute-start.12 = (f32[2]{0:T(128)S(1)}, f32[2]{0:T(128)S(1)}, u32[]{:S(2)}, u32[]{:S(2)}) collective-permute-start(f32[2]{0:T(128)S(1)} %pad_maximum_fusion.2), channel_id=1, source_target_pairs={{0,16},{16,0},{32,48},{48,32},{64,80},{80,64},{96,112},{112,96},{1... | collective-permute-start | bytes 32 | tf_op jit(solution)/shard_map/ppermute | solution.py:57
  49.1 88.0 %collective-permute-start.10 = (f32[128,1024]{1,0:T(8,128)S(1)}, f32[128,1024]{1,0:T(8,128)S(1)}, u32[]{:S(2)}, u32[]{:S(2)}) collective-permute-start(f32[128,1024]{1,0:T(8,128)S(1)} %get-tuple-element.47), channel_id=1, source_target_pairs={{0,8},{4,12},{8,0},{12,4},{1,9},{5,13},{9,1},{13,5},{2,10},{6,14},... | collective-permute-start | bytes 1572872 | tf_op jit(solution)/shard_map/ppermute | solution.py:12
  52.4 89.8 %collective-permute-start.11 = (f32[128,1024]{1,0:T(8,128)S(1)}, f32[128,1024]{1,0:T(8,128)S(1)}, u32[]{:S(2)}, u32[]{:S(2)}) collective-permute-start(f32[128,1024]{1,0:T(8,128)S(1)} %get-tuple-element.46), channel_id=1, source_target_pairs={{0,4},{4,8},{8,12},{12,0},{1,5},{5,9},{9,13},{13,1},{2,6},{6,10},{... | collective-permute-start | bytes 1572872 | tf_op jit(solution)/shard_map/ppermute | solution.py:12
  55.8 86.3 %collective-permute-start.9 = (f32[128,1024]{1,0:T(8,128)S(1)}, f32[128,1024]{1,0:T(8,128)S(1)}, u32[]{:S(2)}, u32[]{:S(2)}) collective-permute-start(f32[128,1024]{1,0:T(8,128)S(1)} %get-tuple-element.45), channel_id=1, source_target_pairs={{0,12},{4,0},{8,4},{12,8},{1,13},{5,1},{9,5},{13,9},{2,14},{6,2},{... | collective-permute-start | bytes 1572872 | tf_op jit(solution)/shard_map/ppermute | solution.py:12
  60.2 83.0 %collective-permute-start.6 = (f32[136,1024]{1,0:T(8,128)S(1)}, f32[136,1024]{1,0:T(8,128)S(1)}, u32[]{:S(2)}, u32[]{:S(2)}) collective-permute-start(f32[136,1024]{1,0:T(8,128)S(1)} %get-tuple-element.42), channel_id=1, source_target_pairs={{0,3},{1,0},{2,1},{3,2},{4,7},{5,4},{6,5},{7,6},{8,11},{9,8},{10,9... | collective-permute-start | bytes 1671176 | tf_op jit(solution)/shard_map/ppermute | solution.py:12
  63.7 11.2 %collective-permute-start.13 = (f32[2]{0:T(128)S(1)}, f32[2]{0:T(128)S(1)}, u32[]{:S(2)}, u32[]{:S(2)}) collective-permute-start(f32[2]{0:T(128)S(1)} %fusion.25), channel_id=1, source_target_pairs={{0,32},{16,48},{32,0},{48,16},{64,96},{80,112},{96,64},{112,80},{1... | collective-permute-start | bytes 32 | tf_op jit(solution)/shard_map/ppermute | solution.py:57
  76.4 16.4 %collective-permute-start.14 = (f32[2]{0:T(128)S(1)}, f32[2]{0:T(128)S(1)}, u32[]{:S(2)}, u32[]{:S(2)}) collective-permute-start(f32[2]{0:T(128)S(1)} %fusion.26), channel_id=1, source_target_pairs={{0,64},{16,80},{32,96},{48,112},{64,0},{80,16},{96,32},{112,48},{1... | collective-permute-start | bytes 32 | tf_op jit(solution)/shard_map/ppermute | solution.py:57
  92.8 4.3 %collective-permute-start.15 = (f32[2]{0:T(128)S(1)}, f32[2]{0:T(128)S(1)}, u32[]{:S(2)}, u32[]{:S(2)}) collective-permute-start(f32[2]{0:T(128)S(1)} %add.82), channel_id=1, source_target_pairs={{0,128},{16,144},{32,160},{48,176},{64,192},{80,208},{96,224},{112... | collective-permute-start | bytes 32 | tf_op jit(solution)/shard_map/ppermute | solution.py:57
  97.1 5.2 %collective-permute-start.16 = (f32[2]{0:T(128)S(1)}, f32[2]{0:T(128)S(1)}, u32[]{:S(2)}, u32[]{:S(2)}) collective-permute-start(f32[2]{0:T(128)S(1)} %add.83), channel_id=1, source_target_pairs={{0,256},{16,272},{32,288},{48,304},{64,320},{80,336},{96,352},{112... | collective-permute-start | bytes 32 | tf_op jit(solution)/shard_map/ppermute | solution.py:57
  102.3 8.4 %collective-permute-start.17 = (f32[2]{0:T(128)S(1)}, f32[2]{0:T(128)S(1)}, u32[]{:S(2)}, u32[]{:S(2)}) collective-permute-start(f32[2]{0:T(128)S(1)} %add.84), channel_id=1, source_target_pairs={{0,512},{16,528},{32,544},{48,560},{64,576},{80,592},{96,608},{112... | collective-permute-start | bytes 32 | tf_op jit(solution)/shard_map/ppermute | solution.py:57
  110.7 4.3 %collective-permute-start.18 = (f32[2]{0:T(128)S(1)}, f32[2]{0:T(128)S(1)}, u32[]{:S(2)}, u32[]{:S(2)}) collective-permute-start(f32[2]{0:T(128)S(1)} %add.85), channel_id=1, source_target_pairs={{0,4},{4,0},{8,12},{12,8},{1,5},{5,1},{9,13},{13,9},{2,6},{6,2},{1... | collective-permute-start | bytes 32 | tf_op jit(solution)/shard_map/ppermute | solution.py:57
  115.0 5.8 %collective-permute-start.19 = (f32[2]{0:T(128)S(1)}, f32[2]{0:T(128)S(1)}, u32[]{:S(2)}, u32[]{:S(2)}) collective-permute-start(f32[2]{0:T(128)S(1)} %add.86), channel_id=1, source_target_pairs={{0,8},{4,12},{8,0},{12,4},{1,9},{5,13},{9,1},{13,5},{2,10},{6,14},... | collective-permute-start | bytes 32 | tf_op jit(solution)/shard_map/ppermute | solution.py:57
  120.8 5.8 %collective-permute-start.20 = (f32[2]{0:T(128)S(1)}, f32[2]{0:T(128)S(1)}, u32[]{:S(2)}, u32[]{:S(2)}) collective-permute-start(f32[2]{0:T(128)S(1)} %add.87), channel_id=1, source_target_pairs={{0,1},{1,0},{2,3},{3,2},{4,5},{5,4},{6,7},{7,6},{8,9},{9,8},{10,11... | collective-permute-start | bytes 32 | tf_op jit(solution)/shard_map/ppermute | solution.py:57
  126.6 6.3 %collective-permute-start.21 = (f32[2]{0:T(128)S(1)}, f32[2]{0:T(128)S(1)}, u32[]{:S(2)}, u32[]{:S(2)}) collective-permute-start(f32[2]{0:T(128)S(1)} %add.88), channel_id=1, source_target_pairs={{0,2},{1,3},{2,0},{3,1},{4,6},{5,7},{6,4},{7,5},{8,10},{9,11},{10,... | collective-permute-start | bytes 32 | tf_op jit(solution)/shard_map/ppermute | solution.py:57
  132.9 39.9 %collective-permute-start.7 = (f32[136,1024]{1,0:T(8,128)S(1)}, f32[136,1024]{1,0:T(8,128)S(1)}, u32[]{:S(2)}, u32[]{:S(2)}) collective-permute-start(f32[136,1024]{1,0:T(8,128)S(1)} %get-tuple-element.44), channel_id=1, source_target_pairs={{0,2},{1,3},{2,0},{3,1},{4,6},{5,7},{6,4},{7,5},{8,10},{9,11},{10,... | collective-permute-start | bytes 1671176 | tf_op jit(solution)/shard_map/ppermute | solution.py:12
  137.2 35.7 %collective-permute-start.8 = (f32[136,1024]{1,0:T(8,128)S(1)}, f32[136,1024]{1,0:T(8,128)S(1)}, u32[]{:S(2)}, u32[]{:S(2)}) collective-permute-start(f32[136,1024]{1,0:T(8,128)S(1)} %get-tuple-element.43), channel_id=1, source_target_pairs={{0,1},{1,2},{2,3},{3,0},{4,5},{5,6},{6,7},{7,4},{8,9},{9,10},{10,1... | collective-permute-start | bytes 1671176 | tf_op jit(solution)/shard_map/ppermute | solution.py:12

commit v4 on v3

--- a/solution.py
+++ b/solution.py
@@ -54,8 +54,13 @@
         count = lax.axis_size(axis)
         step = 1
         while step < count:
-            sums = sums + lax.ppermute(sums, axis, [(i, i ^ step) for i in range(count)])
-            step *= 2
+            if step * 4 <= count:
+                got = [lax.ppermute(sums, axis, [(i, i ^ (a * step)) for i in range(count)]) for a in (1, 2, 3)]
+                sums = (sums + got[0]) + (got[1] + got[2])
+                step *= 4
+            else:
+                sums = sums + lax.ppermute(sums, axis, [(i, i ^ step) for i in range(count)])
+                step *= 2
     return sums
 
 

time: 178 us -> 217 us (1.22)
  the two profiles are of different devices: /device:TPU:1 before, /device:TPU:32 now
where the time goes in v4:
time: 217 us; the launch traced here: 215 us
  starting transfers between devices  103 us (47%)
  waiting for transfers between devices  90.9 us (42%)
  other arithmetic  8 us (4%)
  between operations  5.95 us (3%)
  local copies, waits for them, and re-layouts  5.23 us (2%)
  matrix products  2.44 us (1%)
    ppermute x15, waiting for transfers between devices, total_sums(): lax.ppermute(sums, axis, [(i, i ^ a * step) for i in range(count)])  72.8 us
    ppermute x15, starting transfers between devices, total_sums(): lax.ppermute(sums, axis, [(i, i ^ a * step) for i in range(count)])  56.2 us
    ppermute x12, starting transfers between devices, shifted(): lax.ppermute(value, axis, [(i, (i + by) % count) for i in range(count)])  46.8 us
    ppermute x12, waiting for transfers between devices, shifted(): lax.ppermute(value, axis, [(i, (i + by) % count) for i in range(count)])  18 us
  transfers between devices with their start and end apart: 27, of which 16 were waited for; matrix products, arithmetic and copies ran while one was open for 4% of the time, Pallas kernels for 0%

profile of v4, /device:TPU:32, one launch (start us, length us, event | category | flops | bytes accessed | tf_op | source)
XLA Modules:
  0.0 215.5 jit_solution(9858915622223470293)
XLA Ops:
  0.7 1.1 constant_dynamic-update-slice_fusion.3
  1.8 0.7 and_convert_fusion
  2.6 4.3 %collective-permute-start = (bf16[144,1024]{1,0:T(8,128)(2,1)S(1)}, bf16[144,1024]{1,0:T(8,128)(2,1)}, u32[]{:S(2)}, u32[]{:S(2)}) collective-permute-start(bf16[144,1024]{1,0:T(8,128)(2,1)S(1)} %get-tuple-element.49), channel_id=1, source_target_pairs={{0,1},{1,2},{2,3},{3,0},{4,5},{5,6},{6,7},{7,4},{8,9},{9,10},{10,1... | collective-permute-start | bytes 884744 | tf_op jit(solution)/shard_map/ppermute | solution.py:12
  6.9 6.1 %collective-permute-start.1 = (bf16[144,1024]{1,0:T(8,128)(2,1)S(1)}, bf16[144,1024]{1,0:T(8,128)(2,1)}, u32[]{:S(2)}, u32[]{:S(2)}) collective-permute-start(bf16[144,1024]{1,0:T(8,128)(2,1)S(1)} %get-tuple-element.49), channel_id=1, source_target_pairs={{0,2},{1,3},{2,0},{3,1},{4,6},{5,7},{6,4},{7,5},{8,10},{9,11},{10,... | collective-permute-start | bytes 884744 | tf_op jit(solution)/shard_map/ppermute | solution.py:12
  13.0 2.5 %collective-permute-start.2 = (bf16[144,1024]{1,0:T(8,128)(2,1)S(1)}, bf16[144,1024]{1,0:T(8,128)(2,1)}, u32[]{:S(2)}, u32[]{:S(2)}) collective-permute-start(bf16[144,1024]{1,0:T(8,128)(2,1)S(1)} %get-tuple-element.49), channel_id=1, source_target_pairs={{0,3},{1,0},{2,1},{3,2},{4,7},{5,4},{6,5},{7,6},{8,11},{9,8},{10,9... | collective-permute-start | bytes 884744 | tf_op jit(solution)/shard_map/ppermute | solution.py:12
  15.5 3.4 %collective-permute-start.3 = (bf16[144,1024]{1,0:T(8,128)(2,1)S(1)}, bf16[144,1024]{1,0:T(8,128)(2,1)S(1)}, u32[]{:S(2)}, u32[]{:S(2)}) collective-permute-start(bf16[144,1024]{1,0:T(8,128)(2,1)S(1)} %get-tuple-element.48), channel_id=1, source_target_pairs={{0,4},{4,8},{8,12},{12,0},{1,5},{5,9},{9,13},{13,1},{2,6},{6,10},{... | collective-permute-start | bytes 884744 | tf_op jit(solution)/shard_map/ppermute | solution.py:12
  18.9 4.6 %collective-permute-start.4 = (bf16[144,1024]{1,0:T(8,128)(2,1)S(1)}, bf16[144,1024]{1,0:T(8,128)(2,1)S(1)}, u32[]{:S(2)}, u32[]{:S(2)}) collective-permute-start(bf16[144,1024]{1,0:T(8,128)(2,1)S(1)} %get-tuple-element.48), channel_id=1, source_target_pairs={{0,8},{4,12},{8,0},{12,4},{1,9},{5,13},{9,1},{13,5},{2,10},{6,14},... | collective-permute-start | bytes 884744 | tf_op jit(solution)/shard_map/ppermute | solution.py:12
  24.8 3.3 %collective-permute-start.5 = (bf16[144,1024]{1,0:T(8,128)(2,1)S(1)}, bf16[144,1024]{1,0:T(8,128)(2,1)S(1)}, u32[]{:S(2)}, u32[]{:S(2)}) collective-permute-start(bf16[144,1024]{1,0:T(8,128)(2,1)S(1)} %get-tuple-element.48), channel_id=1, source_target_pairs={{0,12},{4,0},{8,4},{12,8},{1,13},{5,1},{9,5},{13,9},{2,14},{6,2},{... | collective-permute-start | bytes 884744 | tf_op jit(solution)/shard_map/ppermute | solution.py:12
  28.2 1.0 constant_dynamic-update-slice_fusion.2
  29.1 1.2 collective-permute-done.1
  30.3 1.0 constant_dynamic-update-slice_fusion.1
  31.3 1.0 constant_dynamic-update-slice_fusion
  32.3 0.1 slice.164
  32.5 1.3 collective-permute-done.4
  33.8 1.5 collective-permute-done.5
  35.3 0.1 slice.165
  35.5 1.0 fusion.14
  36.5 1.6 multiply_reduce_fusion
  38.1 1.4 pad_maximum_fusion.2
  39.5 1.9 collective-permute-start.12
  41.4 10.9 %collective-permute-start.13 = (f32[2]{0:T(128)S(1)}, f32[2]{0:T(128)S(1)}, u32[]{:S(2)}, u32[]{:S(2)}) collective-permute-start(f32[2]{0:T(128)S(1)} %pad_maximum_fusion.2), channel_id=1, source_target_pairs={{0,32},{16,48},{32,0},{48,16},{64,96},{80,112},{96,64},{112,80},{1... | collective-permute-start | bytes 32 | tf_op jit(solution)/shard_map/ppermute | solution.py:58
  52.3 2.0 collective-permute-start.14
  54.3 0.7 fusion.18
  55.1 0.2 fusion.15
  55.2 4.9 %collective-permute-start.10 = (f32[128,1024]{1,0:T(8,128)S(1)}, f32[128,1024]{1,0:T(8,128)S(1)}, u32[]{:S(2)}, u32[]{:S(2)}) collective-permute-start(f32[128,1024]{1,0:T(8,128)S(1)} %get-tuple-element.47), channel_id=1, source_target_pairs={{0,8},{4,12},{8,0},{12,4},{1,9},{5,13},{9,1},{13,5},{2,10},{6,14},... | collective-permute-start | bytes 1572872 | tf_op jit(solution)/shard_map/ppermute | solution.py:12
  60.2 2.4 %collective-permute-start.11 = (f32[128,1024]{1,0:T(8,128)S(1)}, f32[128,1024]{1,0:T(8,128)S(1)}, u32[]{:S(2)}, u32[]{:S(2)}) collective-permute-start(f32[128,1024]{1,0:T(8,128)S(1)} %get-tuple-element.46), channel_id=1, source_target_pairs={{0,4},{4,8},{8,12},{12,0},{1,5},{5,9},{9,13},{13,1},{2,6},{6,10},{... | collective-permute-start | bytes 1572872 | tf_op jit(solution)/shard_map/ppermute | solution.py:12
  62.6 0.7 fusion.17
  63.3 0.3 select_maximum_fusion
  63.6 0.1 slice_bitcast_fusion.2
  63.8 4.6 %collective-permute-start.9 = (f32[128,1024]{1,0:T(8,128)S(1)}, f32[128,1024]{1,0:T(8,128)S(1)}, u32[]{:S(2)}, u32[]{:S(2)}) collective-permute-start(f32[128,1024]{1,0:T(8,128)S(1)} %get-tuple-element.45), channel_id=1, source_target_pairs={{0,12},{4,0},{8,4},{12,8},{1,13},{5,1},{9,5},{13,9},{2,14},{6,2},{... | collective-permute-start | bytes 1572872 | tf_op jit(solution)/shard_map/ppermute | solution.py:12
  68.4 6.2 %collective-permute-start.6 = (f32[136,1024]{1,0:T(8,128)S(1)}, f32[136,1024]{1,0:T(8,128)S(1)}, u32[]{:S(2)}, u32[]{:S(2)}) collective-permute-start(f32[136,1024]{1,0:T(8,128)S(1)} %get-tuple-element.42), channel_id=1, source_target_pairs={{0,3},{1,0},{2,1},{3,2},{4,7},{5,4},{6,5},{7,6},{8,11},{9,8},{10,9... | collective-permute-start | bytes 1671176 | tf_op jit(solution)/shard_map/ppermute | solution.py:12
  74.6 1.4 add_add_fusion.4
  76.0 14.2 %collective-permute-start.15 = (f32[2]{0:T(128)S(1)}, f32[2]{0:T(128)S(1)}, u32[]{:S(2)}, u32[]{:S(2)}) collective-permute-start(f32[2]{0:T(128)S(1)} %add_add_fusion.4), channel_id=1, source_target_pairs={{0,64},{16,80},{32,96},{48,112},{64,0},{80,16},{96,32},{112,48},{1... | collective-permute-start | bytes 32 | tf_op jit(solution)/shard_map/ppermute | solution.py:58
  90.2 8.7 %collective-permute-done.15 = f32[2]{0:T(128)S(1)} collective-permute-done((f32[2]{0:T(128)S(1)}, f32[2]{0:T(128)S(1)}, u32[]{:S(2)}, u32[]{:S(2)}) %collective-permute-start.15) | collective-permute-done | bytes 40 | tf_op jit(solution)/shard_map/ppermute | solution.py:58
  98.9 2.6 %collective-permute-start.16 = (f32[2]{0:T(128)S(1)}, f32[2]{0:T(128)S(1)}, u32[]{:S(2)}, u32[]{:S(2)}) collective-permute-start(f32[2]{0:T(128)S(1)} %add_add_fusion.4), channel_id=1, source_target_pairs={{0,128},{16,144},{32,160},{48,176},{64,192},{80,208},{96,224},{112... | collective-permute-start | bytes 32 | tf_op jit(solution)/shard_map/ppermute | solution.py:58
  101.5 2.9 %collective-permute-done.16 = f32[2]{0:T(128)S(1)} collective-permute-done((f32[2]{0:T(128)S(1)}, f32[2]{0:T(128)S(1)}, u32[]{:S(2)}, u32[]{:S(2)}) %collective-permute-start.16) | collective-permute-done | bytes 40 | tf_op jit(solution)/shard_map/ppermute | solution.py:58
  104.3 5.6 %collective-permute-start.17 = (f32[2]{0:T(128)S(1)}, f32[2]{0:T(128)S(1)}, u32[]{:S(2)}, u32[]{:S(2)}) collective-permute-start(f32[2]{0:T(128)S(1)} %add_add_fusion.4), channel_id=1, source_target_pairs={{0,192},{16,208},{32,224},{48,240},{64,128},{80,144},{96,160},{112... | collective-permute-start | bytes 32 | tf_op jit(solution)/shard_map/ppermute | solution.py:58
  109.9 9.5 %collective-permute-done.17 = f32[2]{0:T(128)S(1)} collective-permute-done((f32[2]{0:T(128)S(1)}, f32[2]{0:T(128)S(1)}, u32[]{:S(2)}, u32[]{:S(2)}) %collective-permute-start.17) | collective-permute-done | bytes 40 | tf_op jit(solution)/shard_map/ppermute | solution.py:58
  119.4 2.7 %collective-permute-start.18 = (f32[2]{0:T(128)S(1)}, f32[2]{0:T(128)S(1)}, u32[]{:S(2)}, u32[]{:S(2)}) collective-permute-start(f32[2]{0:T(128)S(1)} %add_add_fusion.3), channel_id=1, source_target_pairs={{0,256},{16,272},{32,288},{48,304},{64,320},{80,336},{96,352},{112... | collective-permute-start | bytes 32 | tf_op jit(solution)/shard_map/ppermute | solution.py:58
  122.1 3.7 %collective-permute-done.18 = f32[2]{0:T(128)S(1)} collective-permute-done((f32[2]{0:T(128)S(1)}, f32[2]{0:T(128)S(1)}, u32[]{:S(2)}, u32[]{:S(2)}) %collective-permute-start.18) | collective-permute-done | bytes 40 | tf_op jit(solution)/shard_map/ppermute | solution.py:58
  125.8 2.0 collective-permute-start.19
  127.8 7.3 %collective-permute-done.19 = f32[2]{0:T(128)S(1)} collective-permute-done((f32[2]{0:T(128)S(1)}, f32[2]{0:T(128)S(1)}, u32[]{:S(2)}, u32[]{:S(2)}) %collective-permute-start.19) | collective-permute-done | bytes 40 | tf_op jit(solution)/shard_map/ppermute | solution.py:58
  135.1 2.2 %collective-permute-start.20 = (f32[2]{0:T(128)S(1)}, f32[2]{0:T(128)S(1)}, u32[]{:S(2)}, u32[]{:S(2)}) collective-permute-start(f32[2]{0:T(128)S(1)} %add_add_fusion.3), channel_id=1, source_target_pairs={{0,768},{16,784},{32,800},{48,816},{64,832},{80,848},{96,864},{112... | collective-permute-start | bytes 32 | tf_op jit(solution)/shard_map/ppermute | solution.py:58
  137.4 5.3 %collective-permute-done.20 = f32[2]{0:T(128)S(1)} collective-permute-done((f32[2]{0:T(128)S(1)}, f32[2]{0:T(128)S(1)}, u32[]{:S(2)}, u32[]{:S(2)}) %collective-permute-start.20) | collective-permute-done | bytes 40 | tf_op jit(solution)/shard_map/ppermute | solution.py:58
  142.7 1.9 collective-permute-start.21
  144.6 3.5 %collective-permute-done.21 = f32[2]{0:T(128)S(1)} collective-permute-done((f32[2]{0:T(128)S(1)}, f32[2]{0:T(128)S(1)}, u32[]{:S(2)}, u32[]{:S(2)}) %collective-permute-start.21) | collective-permute-done | bytes 40 | tf_op jit(solution)/shard_map/ppermute | solution.py:58
  148.1 1.9 collective-permute-start.22
  150.1 5.0 %collective-permute-done.22 = f32[2]{0:T(128)S(1)} collective-permute-done((f32[2]{0:T(128)S(1)}, f32[2]{0:T(128)S(1)}, u32[]{:S(2)}, u32[]{:S(2)}) %collective-permute-start.22) | collective-permute-done | bytes 40 | tf_op jit(solution)/shard_map/ppermute | solution.py:58
  155.1 2.2 %collective-permute-start.23 = (f32[2]{0:T(128)S(1)}, f32[2]{0:T(128)S(1)}, u32[]{:S(2)}, u32[]{:S(2)}) collective-permute-start(f32[2]{0:T(128)S(1)} %add_add_fusion.2), channel_id=1, source_target_pairs={{0,12},{4,8},{8,4},{12,0},{1,13},{5,9},{9,5},{13,1},{2,14},{6,10},... | collective-permute-start | bytes 32 | tf_op jit(solution)/shard_map/ppermute | solution.py:58
  157.3 4.5 %collective-permute-done.23 = f32[2]{0:T(128)S(1)} collective-permute-done((f32[2]{0:T(128)S(1)}, f32[2]{0:T(128)S(1)}, u32[]{:S(2)}, u32[]{:S(2)}) %collective-permute-start.23) | collective-permute-done | bytes 40 | tf_op jit(solution)/shard_map/ppermute | solution.py:58
  161.8 1.9 collective-permute-start.24
  163.7 3.5 %collective-permute-done.24 = f32[2]{0:T(128)S(1)} collective-permute-done((f32[2]{0:T(128)S(1)}, f32[2]{0:T(128)S(1)}, u32[]{:S(2)}, u32[]{:S(2)}) %collective-permute-start.24) | collective-permute-done | bytes 40 | tf_op jit(solution)/shard_map/ppermute | solution.py:58
  167.2 2.2 %collective-permute-start.25 = (f32[2]{0:T(128)S(1)}, f32[2]{0:T(128)S(1)}, u32[]{:S(2)}, u32[]{:S(2)}) collective-permute-start(f32[2]{0:T(128)S(1)} %add_add_fusion.1), channel_id=1, source_target_pairs={{0,2},{1,3},{2,0},{3,1},{4,6},{5,7},{6,4},{7,5},{8,10},{9,11},{10,... | collective-permute-start | bytes 32 | tf_op jit(solution)/shard_map/ppermute | solution.py:58
  169.5 13.6 %collective-permute-done.25 = f32[2]{0:T(128)S(1)} collective-permute-done((f32[2]{0:T(128)S(1)}, f32[2]{0:T(128)S(1)}, u32[]{:S(2)}, u32[]{:S(2)}) %collective-permute-start.25) | collective-permute-done | bytes 40 | tf_op jit(solution)/shard_map/ppermute | solution.py:58
  183.0 1.9 collective-permute-start.26
  185.0 5.3 %collective-permute-done.26 = f32[2]{0:T(128)S(1)} collective-permute-done((f32[2]{0:T(128)S(1)}, f32[2]{0:T(128)S(1)}, u32[]{:S(2)}, u32[]{:S(2)}) %collective-permute-start.26) | collective-permute-done | bytes 40 | tf_op jit(solution)/shard_map/ppermute | solution.py:58
  190.3 1.9 collective-permute-start.7
  192.2 2.5 %collective-permute-start.8 = (f32[136,1024]{1,0:T(8,128)S(1)}, f32[136,1024]{1,0:T(8,128)S(1)}, u32[]{:S(2)}, u32[]{:S(2)}) collective-permute-start(f32[136,1024]{1,0:T(8,128)S(1)} %get-tuple-element.43), channel_id=1, source_target_pairs={{0,1},{1,2},{2,3},{3,0},{4,5},{5,6},{6,7},{7,4},{8,9},{9,10},{10,1... | collective-permute-start | bytes 1671176 | tf_op jit(solution)/shard_map/ppermute | solution.py:12
  194.7 0.6 fusion.16
  196.6 1.0 fusion.6
  197.6 14.0 %collective-permute-done.7 = f32[136,1024]{1,0:T(8,128)S(1)} collective-permute-done((f32[136,1024]{1,0:T(8,128)S(1)}, f32[136,1024]{1,0:T(8,128)S(1)}, u32[]{:S(2)}, u32[]{:S(2)}) %collective-permute-start.7) | collective-permute-done | bytes 557088 | tf_op jit(solution)/shard_map/ppermute | solution.py:12
  211.6 0.2 fusion.3
  211.8 0.8 slice_multiply_fusion
  212.7 0.5 fusion.13
  (29 shorter events, 0.2 us)
Async XLA Ops:
  0.6 1.9 copy-start
  0.6 1.9 copy-start.1
  2.6 22.2 %collective-permute-start = (bf16[144,1024]{1,0:T(8,128)(2,1)S(1)}, bf16[144,1024]{1,0:T(8,128)(2,1)}, u32[]{:S(2)}, u32[]{:S(2)}) collective-permute-start(bf16[144,1024]{1,0:T(8,128)(2,1)S(1)} %get-tuple-element.49), channel_id=1, source_target_pairs={{0,1},{1,2},{2,3},{3,0},{4,5},{5,6},{6,7},{7,4},{8,9},{9,10},{10,1... | collective-permute-start | bytes 884744 | tf_op jit(solution)/shard_map/ppermute | solution.py:12
  6.9 23.4 %collective-permute-start.1 = (bf16[144,1024]{1,0:T(8,128)(2,1)S(1)}, bf16[144,1024]{1,0:T(8,128)(2,1)}, u32[]{:S(2)}, u32[]{:S(2)}) collective-permute-start(bf16[144,1024]{1,0:T(8,128)(2,1)S(1)} %get-tuple-element.49), channel_id=1, source_target_pairs={{0,2},{1,3},{2,0},{3,1},{4,6},{5,7},{6,4},{7,5},{8,10},{9,11},{10,... | collective-permute-start | bytes 884744 | tf_op jit(solution)/shard_map/ppermute | solution.py:12
  13.0 18.3 %collective-permute-start.2 = (bf16[144,1024]{1,0:T(8,128)(2,1)S(1)}, bf16[144,1024]{1,0:T(8,128)(2,1)}, u32[]{:S(2)}, u32[]{:S(2)}) collective-permute-start(bf16[144,1024]{1,0:T(8,128)(2,1)S(1)} %get-tuple-element.49), channel_id=1, source_target_pairs={{0,3},{1,0},{2,1},{3,2},{4,7},{5,4},{6,5},{7,6},{8,11},{9,8},{10,9... | collective-permute-start | bytes 884744 | tf_op jit(solution)/shard_map/ppermute | solution.py:12
  15.5 17.0 %collective-permute-start.3 = (bf16[144,1024]{1,0:T(8,128)(2,1)S(1)}, bf16[144,1024]{1,0:T(8,128)(2,1)S(1)}, u32[]{:S(2)}, u32[]{:S(2)}) collective-permute-start(bf16[144,1024]{1,0:T(8,128)(2,1)S(1)} %get-tuple-element.48), channel_id=1, source_target_pairs={{0,4},{4,8},{8,12},{12,0},{1,5},{5,9},{9,13},{13,1},{2,6},{6,10},{... | collective-permute-start | bytes 884744 | tf_op jit(solution)/shard_map/ppermute | solution.py:12
  18.9 14.9 %collective-permute-start.4 = (bf16[144,1024]{1,0:T(8,128)(2,1)S(1)}, bf16[144,1024]{1,0:T(8,128)(2,1)S(1)}, u32[]{:S(2)}, u32[]{:S(2)}) collective-permute-start(bf16[144,1024]{1,0:T(8,128)(2,1)S(1)} %get-tuple-element.48), channel_id=1, source_target_pairs={{0,8},{4,12},{8,0},{12,4},{1,9},{5,13},{9,1},{13,5},{2,10},{6,14},... | collective-permute-start | bytes 884744 | tf_op jit(solution)/shard_map/ppermute | solution.py:12
  24.8 10.5 %collective-permute-start.5 = (bf16[144,1024]{1,0:T(8,128)(2,1)S(1)}, bf16[144,1024]{1,0:T(8,128)(2,1)S(1)}, u32[]{:S(2)}, u32[]{:S(2)}) collective-permute-start(bf16[144,1024]{1,0:T(8,128)(2,1)S(1)} %get-tuple-element.48), channel_id=1, source_target_pairs={{0,12},{4,0},{8,4},{12,8},{1,13},{5,1},{9,5},{13,9},{2,14},{6,2},{... | collective-permute-start | bytes 884744 | tf_op jit(solution)/shard_map/ppermute | solution.py:12
  39.5 24.3 %collective-permute-start.12 = (f32[2]{0:T(128)S(1)}, f32[2]{0:T(128)S(1)}, u32[]{:S(2)}, u32[]{:S(2)}) collective-permute-start(f32[2]{0:T(128)S(1)} %pad_maximum_fusion.2), channel_id=1, source_target_pairs={{0,16},{16,0},{32,48},{48,32},{64,80},{80,64},{96,112},{112,96},{1... | collective-permute-start | bytes 32 | tf_op jit(solution)/shard_map/ppermute | solution.py:58
  41.4 27.0 %collective-permute-start.13 = (f32[2]{0:T(128)S(1)}, f32[2]{0:T(128)S(1)}, u32[]{:S(2)}, u32[]{:S(2)}) collective-permute-start(f32[2]{0:T(128)S(1)} %pad_maximum_fusion.2), channel_id=1, source_target_pairs={{0,32},{16,48},{32,0},{48,16},{64,96},{80,112},{96,64},{112,80},{1... | collective-permute-start | bytes 32 | tf_op jit(solution)/shard_map/ppermute | solution.py:58
  52.3 22.3 %collective-permute-start.14 = (f32[2]{0:T(128)S(1)}, f32[2]{0:T(128)S(1)}, u32[]{:S(2)}, u32[]{:S(2)}) collective-permute-start(f32[2]{0:T(128)S(1)} %pad_maximum_fusion.2), channel_id=1, source_target_pairs={{0,48},{16,32},{32,16},{48,0},{64,112},{80,96},{96,80},{112,64},{1... | collective-permute-start | bytes 32 | tf_op jit(solution)/shard_map/ppermute | solution.py:58
  55.2 137.0 %collective-permute-start.10 = (f32[128,1024]{1,0:T(8,128)S(1)}, f32[128,1024]{1,0:T(8,128)S(1)}, u32[]{:S(2)}, u32[]{:S(2)}) collective-permute-start(f32[128,1024]{1,0:T(8,128)S(1)} %get-tuple-element.47), channel_id=1, source_target_pairs={{0,8},{4,12},{8,0},{12,4},{1,9},{5,13},{9,1},{13,5},{2,10},{6,14},... | collective-permute-start | bytes 1572872 | tf_op jit(solution)/shard_map/ppermute | solution.py:12
  60.2 136.4 %collective-permute-start.11 = (f32[128,1024]{1,0:T(8,128)S(1)}, f32[128,1024]{1,0:T(8,128)S(1)}, u32[]{:S(2)}, u32[]{:S(2)}) collective-permute-start(f32[128,1024]{1,0:T(8,128)S(1)} %get-tuple-element.46), channel_id=1, source_target_pairs={{0,4},{4,8},{8,12},{12,0},{1,5},{5,9},{9,13},{13,1},{2,6},{6,10},{... | collective-permute-start | bytes 1572872 | tf_op jit(solution)/shard_map/ppermute | solution.py:12
  63.8 132.8 %collective-permute-start.9 = (f32[128,1024]{1,0:T(8,128)S(1)}, f32[128,1024]{1,0:T(8,128)S(1)}, u32[]{:S(2)}, u32[]{:S(2)}) collective-permute-start(f32[128,1024]{1,0:T(8,128)S(1)} %get-tuple-element.45), channel_id=1, source_target_pairs={{0,12},{4,0},{8,4},{12,8},{1,13},{5,1},{9,5},{13,9},{2,14},{6,2},{... | collective-permute-start | bytes 1572872 | tf_op jit(solution)/shard_map/ppermute | solution.py:12
  68.4 129.2 %collective-permute-start.6 = (f32[136,1024]{1,0:T(8,128)S(1)}, f32[136,1024]{1,0:T(8,128)S(1)}, u32[]{:S(2)}, u32[]{:S(2)}) collective-permute-start(f32[136,1024]{1,0:T(8,128)S(1)} %get-tuple-element.42), channel_id=1, source_target_pairs={{0,3},{1,0},{2,1},{3,2},{4,7},{5,4},{6,5},{7,6},{8,11},{9,8},{10,9... | collective-permute-start | bytes 1671176 | tf_op jit(solution)/shard_map/ppermute | solution.py:12
  76.0 22.9 %collective-permute-start.15 = (f32[2]{0:T(128)S(1)}, f32[2]{0:T(128)S(1)}, u32[]{:S(2)}, u32[]{:S(2)}) collective-permute-start(f32[2]{0:T(128)S(1)} %add_add_fusion.4), channel_id=1, source_target_pairs={{0,64},{16,80},{32,96},{48,112},{64,0},{80,16},{96,32},{112,48},{1... | collective-permute-start | bytes 32 | tf_op jit(solution)/shard_map/ppermute | solution.py:58
  98.9 5.5 %collective-permute-start.16 = (f32[2]{0:T(128)S(1)}, f32[2]{0:T(128)S(1)}, u32[]{:S(2)}, u32[]{:S(2)}) collective-permute-start(f32[2]{0:T(128)S(1)} %add_add_fusion.4), channel_id=1, source_target_pairs={{0,128},{16,144},{32,160},{48,176},{64,192},{80,208},{96,224},{112... | collective-permute-start | bytes 32 | tf_op jit(solution)/shard_map/ppermute | solution.py:58
  104.3 15.1 %collective-permute-start.17 = (f32[2]{0:T(128)S(1)}, f32[2]{0:T(128)S(1)}, u32[]{:S(2)}, u32[]{:S(2)}) collective-permute-start(f32[2]{0:T(128)S(1)} %add_add_fusion.4), channel_id=1, source_target_pairs={{0,192},{16,208},{32,224},{48,240},{64,128},{80,144},{96,160},{112... | collective-permute-start | bytes 32 | tf_op jit(solution)/shard_map/ppermute | solution.py:58
  119.4 6.3 %collective-permute-start.18 = (f32[2]{0:T(128)S(1)}, f32[2]{0:T(128)S(1)}, u32[]{:S(2)}, u32[]{:S(2)}) collective-permute-start(f32[2]{0:T(128)S(1)} %add_add_fusion.3), channel_id=1, source_target_pairs={{0,256},{16,272},{32,288},{48,304},{64,320},{80,336},{96,352},{112... | collective-permute-start | bytes 32 | tf_op jit(solution)/shard_map/ppermute | solution.py:58
  125.8 9.4 %collective-permute-start.19 = (f32[2]{0:T(128)S(1)}, f32[2]{0:T(128)S(1)}, u32[]{:S(2)}, u32[]{:S(2)}) collective-permute-start(f32[2]{0:T(128)S(1)} %add_add_fusion.3), channel_id=1, source_target_pairs={{0,512},{16,528},{32,544},{48,560},{64,576},{80,592},{96,608},{112... | collective-permute-start | bytes 32 | tf_op jit(solution)/shard_map/ppermute | solution.py:58
  135.1 7.6 %collective-permute-start.20 = (f32[2]{0:T(128)S(1)}, f32[2]{0:T(128)S(1)}, u32[]{:S(2)}, u32[]{:S(2)}) collective-permute-start(f32[2]{0:T(128)S(1)} %add_add_fusion.3), channel_id=1, source_target_pairs={{0,768},{16,784},{32,800},{48,816},{64,832},{80,848},{96,864},{112... | collective-permute-start | bytes 32 | tf_op jit(solution)/shard_map/ppermute | solution.py:58
  142.7 5.5 %collective-permute-start.21 = (f32[2]{0:T(128)S(1)}, f32[2]{0:T(128)S(1)}, u32[]{:S(2)}, u32[]{:S(2)}) collective-permute-start(f32[2]{0:T(128)S(1)} %add_add_fusion.2), channel_id=1, source_target_pairs={{0,4},{4,0},{8,12},{12,8},{1,5},{5,1},{9,13},{13,9},{2,6},{6,2},{1... | collective-permute-start | bytes 32 | tf_op jit(solution)/shard_map/ppermute | solution.py:58
  148.1 7.0 %collective-permute-start.22 = (f32[2]{0:T(128)S(1)}, f32[2]{0:T(128)S(1)}, u32[]{:S(2)}, u32[]{:S(2)}) collective-permute-start(f32[2]{0:T(128)S(1)} %add_add_fusion.2), channel_id=1, source_target_pairs={{0,8},{4,12},{8,0},{12,4},{1,9},{5,13},{9,1},{13,5},{2,10},{6,14},... | collective-permute-start | bytes 32 | tf_op jit(solution)/shard_map/ppermute | solution.py:58
  155.1 6.7 %collective-permute-start.23 = (f32[2]{0:T(128)S(1)}, f32[2]{0:T(128)S(1)}, u32[]{:S(2)}, u32[]{:S(2)}) collective-permute-start(f32[2]{0:T(128)S(1)} %add_add_fusion.2), channel_id=1, source_target_pairs={{0,12},{4,8},{8,4},{12,0},{1,13},{5,9},{9,5},{13,1},{2,14},{6,10},... | collective-permute-start | bytes 32 | tf_op jit(solution)/shard_map/ppermute | solution.py:58
  161.8 5.5 %collective-permute-start.24 = (f32[2]{0:T(128)S(1)}, f32[2]{0:T(128)S(1)}, u32[]{:S(2)}, u32[]{:S(2)}) collective-permute-start(f32[2]{0:T(128)S(1)} %add_add_fusion.1), channel_id=1, source_target_pairs={{0,1},{1,0},{2,3},{3,2},{4,5},{5,4},{6,7},{7,6},{8,9},{9,8},{10,11... | collective-permute-start | bytes 32 | tf_op jit(solution)/shard_map/ppermute | solution.py:58
  167.2 15.8 %collective-permute-start.25 = (f32[2]{0:T(128)S(1)}, f32[2]{0:T(128)S(1)}, u32[]{:S(2)}, u32[]{:S(2)}) collective-permute-start(f32[2]{0:T(128)S(1)} %add_add_fusion.1), channel_id=1, source_target_pairs={{0,2},{1,3},{2,0},{3,1},{4,6},{5,7},{6,4},{7,5},{8,10},{9,11},{10,... | collective-permute-start | bytes 32 | tf_op jit(solution)/shard_map/ppermute | solution.py:58
  183.0 7.2 %collective-permute-start.26 = (f32[2]{0:T(128)S(1)}, f32[2]{0:T(128)S(1)}, u32[]{:S(2)}, u32[]{:S(2)}) collective-permute-start(f32[2]{0:T(128)S(1)} %add_add_fusion.1), channel_id=1, source_target_pairs={{0,3},{1,2},{2,1},{3,0},{4,7},{5,6},{6,5},{7,4},{8,11},{9,10},{10,... | collective-permute-start | bytes 32 | tf_op jit(solution)/shard_map/ppermute | solution.py:58
  190.3 21.4 %collective-permute-start.7 = (f32[136,1024]{1,0:T(8,128)S(1)}, f32[136,1024]{1,0:T(8,128)S(1)}, u32[]{:S(2)}, u32[]{:S(2)}) collective-permute-start(f32[136,1024]{1,0:T(8,128)S(1)} %get-tuple-element.44), channel_id=1, source_target_pairs={{0,2},{1,3},{2,0},{3,1},{4,6},{5,7},{6,4},{7,5},{8,10},{9,11},{10,... | collective-permute-start | bytes 1671176 | tf_op jit(solution)/shard_map/ppermute | solution.py:12
  192.2 19.4 %collective-permute-start.8 = (f32[136,1024]{1,0:T(8,128)S(1)}, f32[136,1024]{1,0:T(8,128)S(1)}, u32[]{:S(2)}, u32[]{:S(2)}) collective-permute-start(f32[136,1024]{1,0:T(8,128)S(1)} %get-tuple-element.43), channel_id=1, source_target_pairs={{0,1},{1,2},{2,3},{3,0},{4,5},{5,6},{6,7},{7,4},{8,9},{9,10},{10,1... | collective-permute-start | bytes 1671176 | tf_op jit(solution)/shard_map/ppermute | solution.py:12

commit v5 on v3

--- a/solution.py
+++ b/solution.py
@@ -7,21 +7,17 @@
 from jax.sharding import PartitionSpec as P
 
 
-def shifted(value, axis, by):
+def gather_all(value, axis):
     count = lax.axis_size(axis)
-    return lax.ppermute(value, axis, [(i, (i + by) % count) for i in range(count)])
+    return lax.all_to_all(jnp.tile(value, (count, 1)), axis, 0, 0, tiled=True)
 
 
-def gather_by_shift(value, axis):
+def reduce_all(parts, axis):
     count = lax.axis_size(axis)
-    return jnp.concatenate([value] + [shifted(value, axis, k) for k in range(1, count)], axis=0)
-
-
-def reduce_by_shift(parts, axis):
-    count = lax.axis_size(axis)
-    total = parts[0]
+    got = lax.all_to_all(parts, axis, 0, 0, tiled=True)
+    total = got[0]
     for k in range(1, count):
-        total = total + shifted(parts[k], axis, -k)
+        total = total + got[k]
     return total
 
 
@@ -66,8 +62,8 @@
     ncol = lax.axis_size("bx")
     root = math.sqrt(width)
     scale = temp / root
-    row_informal, row_labels = split_labels(gather_by_shift(with_labels(informal, labels), "bz"), rows)
-    col_formal, col_labels = split_labels(gather_by_shift(with_labels(formal, labels), "bx"), rows)
+    row_informal, row_labels = split_labels(gather_all(with_labels(informal, labels), "bz"), rows)
+    col_formal, col_labels = split_labels(gather_all(with_labels(formal, labels), "bx"), rows)
     raw = lax.dot_general(row_informal, col_formal, (((1,), (1,)), ((), ())), preferred_element_type=jnp.float32) / root
     logits = temp * raw + bias
     sign = jnp.where(row_labels[:, None] == col_labels[None, :], 1.0, -1.0).astype(jnp.float32)
@@ -76,10 +72,10 @@
     weights = slope.astype(jnp.bfloat16)
     grad_x_part = jnp.dot(weights, col_formal, preferred_element_type=jnp.float32)
     grad_y_part = lax.dot_general(weights, row_informal, (((0,), (0,)), ((), ())), preferred_element_type=jnp.float32)
-    packed = reduce_by_shift(with_loss(grad_x_part.reshape(nrow, rows, width), loss_part.reshape(nrow, rows)), "bz")
+    packed = reduce_all(with_loss(grad_x_part.reshape(nrow, rows, width), loss_part.reshape(nrow, rows)), "bz")
     loss_sum = packed[rows, :rows]
     grad_x = scale * packed[:rows]
-    grad_y = scale * reduce_by_shift(grad_y_part.reshape(ncol, rows, width), "bx")
+    grad_y = scale * reduce_all(grad_y_part.reshape(ncol, rows, width), "bx")
     sums = total_sums(jnp.stack([jnp.sum(slope * raw), jnp.sum(slope)]), ("group", "bx", "bz"))
     set_size = rows * nrow * ncol
     total = jnp.float32(set_size * ngroup) * jnp.float32(set_size)

time: 178 us -> 231 us (1.30)
  the two profiles are of different devices: /device:TPU:1 before, /device:TPU:40 now
where the time goes in v5:
time: 231 us; the launch traced here: 230 us
  starting transfers between devices  83.5 us (36%)
  waiting for transfers between devices  82.3 us (36%)
  blocking collectives  20.6 us (9%)
  other arithmetic  19 us (8%)
  local copies, waits for them, and re-layouts  13.7 us (6%)
  between operations  5.72 us (2%)
  matrix products  5.52 us (2%)
    ppermute x10, starting transfers between devices, total_sums(): lax.ppermute(sums, axis, [(i, i ^ step) for i in range(count)])  69 us
    ppermute x10, waiting for transfers between devices, total_sums(): lax.ppermute(sums, axis, [(i, i ^ step) for i in range(count)])  43.5 us
    all_to_all x1, waiting for transfers between devices, gather_all(): return lax.all_to_all(jnp.tile(value, (count, 1)), axis, 0, 0, tiled=True)  26 us
    all_to_all x1, blocking collectives, gather_all(): return lax.all_to_all(jnp.tile(value, (count, 1)), axis, 0, 0, tiled=True)  20.6 us
    all_to_all x2, waiting for transfers between devices, reduce_all(): got = lax.all_to_all(parts, axis, 0, 0, tiled=True)  12.8 us
    all_to_all x1, starting transfers between devices, gather_all(): return lax.all_to_all(jnp.tile(value, (count, 1)), axis, 0, 0, tiled=True)  7.26 us
    all_to_all x2, starting transfers between devices, reduce_all(): got = lax.all_to_all(parts, axis, 0, 0, tiled=True)  7.23 us
  transfers between devices with their start and end apart: 13, of which 12 were waited for; matrix products, arithmetic and copies ran while one was open for 9% of the time, Pallas kernels for 0%

profile of v5, /device:TPU:40, one launch (start us, length us, event | category | flops | bytes accessed | tf_op | source)
XLA Modules:
  0.0 230.3 jit_solution(2266592330779957981)
XLA Ops:
  0.6 0.7 and_convert_fusion
  1.4 1.1 fusion.13
  2.5 0.1 tile.5
  2.6 20.6 %all_to_all.22 = bf16[4,144,1024]{2,1,0:T(8,128)(2,1)S(1)} all-to-all(bf16[4,144,1024]{2,1,0:T(8,128)(2,1)S(1)} %tile.5), channel_id=1, replica_groups=mesh['group'=64,'bx'=4,'bz'=4] {'bx'}, dimensions={0} | all-to-all | bytes 2359296 | tf_op jit(solution)/shard_map/all_to_all | solution.py:12
  23.2 1.2 tile.4
  24.4 7.3 %all-to-all-start = ((bf16[4,144,1024]{2,1,0:T(8,128)(2,1)}), bf16[4,144,1024]{2,1,0:T(8,128)(2,1)S(1)}, u32[]{:S(2)}, u32[]{:S(2)}) async-start(bf16[4,144,1024]{2,1,0:T(8,128)(2,1)} %tile.4), calls=%async_computation | async-start | bytes 2359296 | tf_op jit(solution)/shard_map/all_to_all | solution.py:12
  32.9 0.1 slice.162
  33.0 0.0 copy-start.1
  33.1 26.0 %all-to-all-done = bf16[4,144,1024]{2,1,0:T(8,128)(2,1)S(1)} async-done(((bf16[4,144,1024]{2,1,0:T(8,128)(2,1)}), bf16[4,144,1024]{2,1,0:T(8,128)(2,1)S(1)}, u32[]{:S(2)}, u32[]{:S(2)}) %all-to-all-start) | async-done | bytes 1179680 | tf_op jit(solution)/shard_map/all_to_all | solution.py:12
  59.0 0.1 slice.161
  59.1 0.0 copy-done.1
  59.1 1.7 fusion.22
  60.9 1.6 copy.11
  62.5 2.4 %negate_exponential_fusion = (f32[512,512]{1,0:T(8,128)}, f32[512]{0:T(512)S(1)}, f32[512,512]{1,0:T(8,128)}, f32[512,512]{1,0:T(8,128)}) fusion(f32[]{:T(128)S(6)} %copy.21, f32[512,512]{1,0:T(8,128)S(1)} %copy.11, f32[]{:T(128)S(6)} %mul.51, s32[512]{0:T(512)S(1)} %bitcast.49, s32[512]{0:T(512)S(1)} %bitcast.50), kind=kLoop, calls=%fused_computation.12 | loop fusion | flops 4193792 | bytes 4200456 | tf_op jit(solution)/shard_map/exp | solution.py:71
  64.8 1.6 copy.16
  66.4 1.2 fusion.6
  67.5 1.3 copy.19
  68.8 2.0 fusion.24
  70.8 3.6 %all-to-all-start.3 = ((f32[4,128,1024]{2,1,0:T(8,128)}), f32[4,128,1024]{2,1,0:T(8,128)S(1)}, u32[]{:S(2)}, u32[]{:S(2)}) async-start(f32[4,128,1024]{2,1,0:T(8,128)} %fusion.24), calls=%async_computation.3 | async-start | bytes 4194304 | tf_op jit(solution)/shard_map/all_to_all | solution.py:17
  74.4 0.0 copy-start.3
  74.4 2.7 %copy.12 = f32[512,512]{0,1:T(8,128)} copy(f32[512,512]{1,0:T(8,128)} %get-tuple-element.40) | data formatting | bytes 2097152 | tf_op jit(solution)/shard_map/exp | solution.py:71
  77.1 0.0 copy-done.3
  77.1 1.3 copy.13
  78.4 0.0 copy-start.2
  78.4 3.7 %multiply_reduce_fusion = (f32[]{:T(128)}, f32[]{:T(128)}, bf16[512,512]{0,1:T(8,128)(2,1)}) fusion(f32[512,512]{0,1:T(8,128)} %fusion.22, f32[512,512]{0,1:T(8,128)} %copy.13, f32[512,512]{0,1:T(8,128)} %copy.12), kind=kLoop, calls=%fused_computation.10 | loop fusion | flops 2097150 | bytes 3670024 | tf_op jit(solution)/shard_map/reduce_sum | solution.py:79
  82.1 2.0 copy.18
  84.2 0.0 copy-done.2
  84.2 1.8 fusion.23
  85.9 1.6 select_maximum_fusion
  87.5 12.8 %all-to-all-done.3 = f32[4,128,1024]{2,1,0:T(8,128)S(1)} async-done(((f32[4,128,1024]{2,1,0:T(8,128)}), f32[4,128,1024]{2,1,0:T(8,128)S(1)}, u32[]{:S(2)}, u32[]{:S(2)}) %all-to-all-start.3) | async-done | bytes 2097184 | tf_op jit(solution)/shard_map/all_to_all | solution.py:17
  100.3 0.0 copy-start
  100.3 1.3 copy-done
  101.6 3.6 %all-to-all-start.2 = ((f32[4,136,1024]{2,1,0:T(8,128)}), f32[4,136,1024]{2,1,0:T(8,128)S(1)}, u32[]{:S(2)}, u32[]{:S(2)}) async-start(f32[4,136,1024]{2,1,0:T(8,128)} %select_maximum_fusion), calls=%async_computation.2 | async-start | bytes 4456448 | tf_op jit(solution)/shard_map/all_to_all | solution.py:17
  105.3 1.4 pad_maximum_fusion
  106.6 1.9 collective-permute-start
  108.5 1.1 collective-permute-done
  109.7 1.4 fusion.31
  111.0 10.9 %collective-permute-start.1 = (f32[2]{0:T(128)S(1)}, f32[2]{0:T(128)S(1)}, u32[]{:S(2)}, u32[]{:S(2)}) collective-permute-start(f32[2]{0:T(128)S(1)} %fusion.31), channel_id=1, source_target_pairs={{0,32},{16,48},{32,0},{48,16},{64,96},{80,112},{96,64},{112,80},{1... | collective-permute-start | bytes 32 | tf_op jit(solution)/shard_map/ppermute | solution.py:53
  122.0 18.1 %collective-permute-done.1 = f32[2]{0:T(128)S(1)} collective-permute-done((f32[2]{0:T(128)S(1)}, f32[2]{0:T(128)S(1)}, u32[]{:S(2)}, u32[]{:S(2)}) %collective-permute-start.1) | collective-permute-done | bytes 40 | tf_op jit(solution)/shard_map/ppermute | solution.py:53
  140.1 1.4 fusion.33
  141.4 16.7 %collective-permute-start.2 = (f32[2]{0:T(128)S(1)}, f32[2]{0:T(128)S(1)}, u32[]{:S(2)}, u32[]{:S(2)}) collective-permute-start(f32[2]{0:T(128)S(1)} %fusion.33), channel_id=1, source_target_pairs={{0,64},{16,80},{32,96},{48,112},{64,0},{80,16},{96,32},{112,48},{1... | collective-permute-start | bytes 32 | tf_op jit(solution)/shard_map/ppermute | solution.py:53
  158.1 1.5 collective-permute-done.2
  159.6 3.3 %collective-permute-start.3 = (f32[2]{0:T(128)S(1)}, f32[2]{0:T(128)S(1)}, u32[]{:S(2)}, u32[]{:S(2)}) collective-permute-start(f32[2]{0:T(128)S(1)} %add.100), channel_id=1, source_target_pairs={{0,128},{16,144},{32,160},{48,176},{64,192},{80,208},{96,224},{112... | collective-permute-start | bytes 32 | tf_op jit(solution)/shard_map/ppermute | solution.py:53
  162.9 2.2 collective-permute-done.3
  165.1 2.7 %collective-permute-start.4 = (f32[2]{0:T(128)S(1)}, f32[2]{0:T(128)S(1)}, u32[]{:S(2)}, u32[]{:S(2)}) collective-permute-start(f32[2]{0:T(128)S(1)} %add.101), channel_id=1, source_target_pairs={{0,256},{16,272},{32,288},{48,304},{64,320},{80,336},{96,352},{112... | collective-permute-start | bytes 32 | tf_op jit(solution)/shard_map/ppermute | solution.py:53
  167.8 3.7 %collective-permute-done.4 = f32[2]{0:T(128)S(1)} collective-permute-done((f32[2]{0:T(128)S(1)}, f32[2]{0:T(128)S(1)}, u32[]{:S(2)}, u32[]{:S(2)}) %collective-permute-start.4) | collective-permute-done | bytes 40 | tf_op jit(solution)/shard_map/ppermute | solution.py:53
  171.4 2.9 %collective-permute-start.5 = (f32[2]{0:T(128)S(1)}, f32[2]{0:T(128)S(1)}, u32[]{:S(2)}, u32[]{:S(2)}) collective-permute-start(f32[2]{0:T(128)S(1)} %add.102), channel_id=1, source_target_pairs={{0,512},{16,528},{32,544},{48,560},{64,576},{80,592},{96,608},{112... | collective-permute-start | bytes 32 | tf_op jit(solution)/shard_map/ppermute | solution.py:53
  174.4 6.5 %collective-permute-done.5 = f32[2]{0:T(128)S(1)} collective-permute-done((f32[2]{0:T(128)S(1)}, f32[2]{0:T(128)S(1)}, u32[]{:S(2)}, u32[]{:S(2)}) %collective-permute-start.5) | collective-permute-done | bytes 40 | tf_op jit(solution)/shard_map/ppermute | solution.py:53
  180.8 2.5 %collective-permute-start.6 = (f32[2]{0:T(128)S(1)}, f32[2]{0:T(128)S(1)}, u32[]{:S(2)}, u32[]{:S(2)}) collective-permute-start(f32[2]{0:T(128)S(1)} %add.103), channel_id=1, source_target_pairs={{0,4},{4,0},{8,12},{12,8},{1,5},{5,1},{9,13},{13,9},{2,6},{6,2},{1... | collective-permute-start | bytes 32 | tf_op jit(solution)/shard_map/ppermute | solution.py:53
  183.3 3.0 %collective-permute-done.6 = f32[2]{0:T(128)S(1)} collective-permute-done((f32[2]{0:T(128)S(1)}, f32[2]{0:T(128)S(1)}, u32[]{:S(2)}, u32[]{:S(2)}) %collective-permute-start.6) | collective-permute-done | bytes 40 | tf_op jit(solution)/shard_map/ppermute | solution.py:53
  186.3 2.5 %collective-permute-start.7 = (f32[2]{0:T(128)S(1)}, f32[2]{0:T(128)S(1)}, u32[]{:S(2)}, u32[]{:S(2)}) collective-permute-start(f32[2]{0:T(128)S(1)} %add.104), channel_id=1, source_target_pairs={{0,8},{4,12},{8,0},{12,4},{1,9},{5,13},{9,1},{13,5},{2,10},{6,14},... | collective-permute-start | bytes 32 | tf_op jit(solution)/shard_map/ppermute | solution.py:53
  188.8 4.4 %collective-permute-done.7 = f32[2]{0:T(128)S(1)} collective-permute-done((f32[2]{0:T(128)S(1)}, f32[2]{0:T(128)S(1)}, u32[]{:S(2)}, u32[]{:S(2)}) %collective-permute-start.7) | collective-permute-done | bytes 40 | tf_op jit(solution)/shard_map/ppermute | solution.py:53
  193.2 15.6 %collective-permute-start.8 = (f32[2]{0:T(128)S(1)}, f32[2]{0:T(128)S(1)}, u32[]{:S(2)}, u32[]{:S(2)}) collective-permute-start(f32[2]{0:T(128)S(1)} %add.105), channel_id=1, source_target_pairs={{0,1},{1,0},{2,3},{3,2},{4,5},{5,4},{6,7},{7,6},{8,9},{9,8},{10,11... | collective-permute-start | bytes 32 | tf_op jit(solution)/shard_map/ppermute | solution.py:53
  208.8 1.5 collective-permute-done.8
  210.3 10.1 %collective-permute-start.9 = (f32[2]{0:T(128)S(1)}, f32[2]{0:T(128)S(1)}, u32[]{:S(2)}, u32[]{:S(2)}) collective-permute-start(f32[2]{0:T(128)S(1)} %add.106), channel_id=1, source_target_pairs={{0,2},{1,3},{2,0},{3,1},{4,6},{5,7},{6,4},{7,5},{8,10},{9,11},{10,... | collective-permute-start | bytes 32 | tf_op jit(solution)/shard_map/ppermute | solution.py:53
  220.5 1.5 collective-permute-done.9
  222.0 0.6 fusion.21
  223.9 2.5 %fusion.10 = f32[128,1024]{1,0:T(8,128)} fusion(f32[4,128,1024]{2,1,0:T(8,128)} %copy-done, f32[]{:T(128)S(6)} %mul.51), kind=kLoop, calls=%fused_computation.25 | loop fusion | flops 524288 | bytes 2621444 | tf_op jit(solution)/shard_map/mul | solution.py:78
  226.4 0.0 all-to-all-done.2
  226.4 0.2 slice_add_fusion
  226.5 0.8 fusion.11
  227.4 0.2 fusion.32
  227.5 0.5 fusion.20
  (13 shorter events, 0.1 us)
Async XLA Ops:
  24.4 34.7 %all-to-all-start = ((bf16[4,144,1024]{2,1,0:T(8,128)(2,1)}), bf16[4,144,1024]{2,1,0:T(8,128)(2,1)S(1)}, u32[]{:S(2)}, u32[]{:S(2)}) async-start(bf16[4,144,1024]{2,1,0:T(8,128)(2,1)} %tile.4), calls=%async_computation | async-start | bytes 2359296 | tf_op jit(solution)/shard_map/all_to_all | solution.py:12
  33.0 26.1 %copy-start.1 = (bf16[4,128,1024]{2,1,0:T(8,128)(2,1)}, bf16[4,128,1024]{2,1,0:T(8,128)(2,1)S(1)}, u32[]{:S(2)}) copy-start(bf16[4,128,1024]{2,1,0:T(8,128)(2,1)S(1)} %slice.162) | copy-start | bytes 3145732
  70.8 29.5 %all-to-all-start.3 = ((f32[4,128,1024]{2,1,0:T(8,128)}), f32[4,128,1024]{2,1,0:T(8,128)S(1)}, u32[]{:S(2)}, u32[]{:S(2)}) async-start(f32[4,128,1024]{2,1,0:T(8,128)} %fusion.24), calls=%async_computation.3 | async-start | bytes 4194304 | tf_op jit(solution)/shard_map/all_to_all | solution.py:17
  74.4 2.7 %copy-start.3 = (f32[512,512]{1,0:T(8,128)S(1)}, f32[512,512]{1,0:T(8,128)}, u32[]{:S(2)}) copy-start(f32[512,512]{1,0:T(8,128)} %get-tuple-element.43) | copy-start | bytes 3145732
  78.4 5.7 %copy-start.2 = (bf16[4,128,1024]{2,1,0:T(8,128)(2,1)S(1)}, bf16[4,128,1024]{2,1,0:T(8,128)(2,1)}, u32[]{:S(2)}) copy-start(bf16[4,128,1024]{2,1,0:T(8,128)(2,1)} %copy-done.1) | copy-start | bytes 3145732
  100.3 1.3 copy-start
  101.6 124.7 %all-to-all-start.2 = ((f32[4,136,1024]{2,1,0:T(8,128)}), f32[4,136,1024]{2,1,0:T(8,128)S(1)}, u32[]{:S(2)}, u32[]{:S(2)}) async-start(f32[4,136,1024]{2,1,0:T(8,128)} %select_maximum_fusion), calls=%async_computation.2 | async-start | bytes 4456448 | tf_op jit(solution)/shard_map/all_to_all | solution.py:17
  106.6 3.0 %collective-permute-start = (f32[2]{0:T(128)S(1)}, f32[2]{0:T(128)S(1)}, u32[]{:S(2)}, u32[]{:S(2)}) collective-permute-start(f32[2]{0:T(128)S(1)} %pad_maximum_fusion), channel_id=1, source_target_pairs={{0,16},{16,0},{32,48},{48,32},{64,80},{80,64},{96,112},{112,96},{1... | collective-permute-start | bytes 32 | tf_op jit(solution)/shard_map/ppermute | solution.py:53
  111.0 29.0 %collective-permute-start.1 = (f32[2]{0:T(128)S(1)}, f32[2]{0:T(128)S(1)}, u32[]{:S(2)}, u32[]{:S(2)}) collective-permute-start(f32[2]{0:T(128)S(1)} %fusion.31), channel_id=1, source_target_pairs={{0,32},{16,48},{32,0},{48,16},{64,96},{80,112},{96,64},{112,80},{1... | collective-permute-start | bytes 32 | tf_op jit(solution)/shard_map/ppermute | solution.py:53
  141.4 18.2 %collective-permute-start.2 = (f32[2]{0:T(128)S(1)}, f32[2]{0:T(128)S(1)}, u32[]{:S(2)}, u32[]{:S(2)}) collective-permute-start(f32[2]{0:T(128)S(1)} %fusion.33), channel_id=1, source_target_pairs={{0,64},{16,80},{32,96},{48,112},{64,0},{80,16},{96,32},{112,48},{1... | collective-permute-start | bytes 32 | tf_op jit(solution)/shard_map/ppermute | solution.py:53
  159.6 5.5 %collective-permute-start.3 = (f32[2]{0:T(128)S(1)}, f32[2]{0:T(128)S(1)}, u32[]{:S(2)}, u32[]{:S(2)}) collective-permute-start(f32[2]{0:T(128)S(1)} %add.100), channel_id=1, source_target_pairs={{0,128},{16,144},{32,160},{48,176},{64,192},{80,208},{96,224},{112... | collective-permute-start | bytes 32 | tf_op jit(solution)/shard_map/ppermute | solution.py:53
  165.1 6.3 %collective-permute-start.4 = (f32[2]{0:T(128)S(1)}, f32[2]{0:T(128)S(1)}, u32[]{:S(2)}, u32[]{:S(2)}) collective-permute-start(f32[2]{0:T(128)S(1)} %add.101), channel_id=1, source_target_pairs={{0,256},{16,272},{32,288},{48,304},{64,320},{80,336},{96,352},{112... | collective-permute-start | bytes 32 | tf_op jit(solution)/shard_map/ppermute | solution.py:53
  171.4 9.4 %collective-permute-start.5 = (f32[2]{0:T(128)S(1)}, f32[2]{0:T(128)S(1)}, u32[]{:S(2)}, u32[]{:S(2)}) collective-permute-start(f32[2]{0:T(128)S(1)} %add.102), channel_id=1, source_target_pairs={{0,512},{16,528},{32,544},{48,560},{64,576},{80,592},{96,608},{112... | collective-permute-start | bytes 32 | tf_op jit(solution)/shard_map/ppermute | solution.py:53
  180.8 5.5 %collective-permute-start.6 = (f32[2]{0:T(128)S(1)}, f32[2]{0:T(128)S(1)}, u32[]{:S(2)}, u32[]{:S(2)}) collective-permute-start(f32[2]{0:T(128)S(1)} %add.103), channel_id=1, source_target_pairs={{0,4},{4,0},{8,12},{12,8},{1,5},{5,1},{9,13},{13,9},{2,6},{6,2},{1... | collective-permute-start | bytes 32 | tf_op jit(solution)/shard_map/ppermute | solution.py:53
  186.3 7.0 %collective-permute-start.7 = (f32[2]{0:T(128)S(1)}, f32[2]{0:T(128)S(1)}, u32[]{:S(2)}, u32[]{:S(2)}) collective-permute-start(f32[2]{0:T(128)S(1)} %add.104), channel_id=1, source_target_pairs={{0,8},{4,12},{8,0},{12,4},{1,9},{5,13},{9,1},{13,5},{2,10},{6,14},... | collective-permute-start | bytes 32 | tf_op jit(solution)/shard_map/ppermute | solution.py:53
  193.2 17.1 %collective-permute-start.8 = (f32[2]{0:T(128)S(1)}, f32[2]{0:T(128)S(1)}, u32[]{:S(2)}, u32[]{:S(2)}) collective-permute-start(f32[2]{0:T(128)S(1)} %add.105), channel_id=1, source_target_pairs={{0,1},{1,0},{2,3},{3,2},{4,5},{5,4},{6,7},{7,6},{8,9},{9,8},{10,11... | collective-permute-start | bytes 32 | tf_op jit(solution)/shard_map/ppermute | solution.py:53
  210.3 11.6 %collective-permute-start.9 = (f32[2]{0:T(128)S(1)}, f32[2]{0:T(128)S(1)}, u32[]{:S(2)}, u32[]{:S(2)}) collective-permute-start(f32[2]{0:T(128)S(1)} %add.106), channel_id=1, source_target_pairs={{0,2},{1,3},{2,0},{3,1},{4,6},{5,7},{6,4},{7,5},{8,10},{9,11},{10,... | collective-permute-start | bytes 32 | tf_op jit(solution)/shard_map/ppermute | solution.py:53

commit v6 on v3

--- a/solution.py
+++ b/solution.py
@@ -49,13 +49,26 @@
     return jnp.concatenate([grad_part, tail], axis=1)
 
 
+def pairings(digits):
+    count = math.prod(size for size, _, _ in digits)
+    steps = []
+    for size, stride, ring in digits:
+        bit = 1
+        while bit < size:
+            top = bit * 2 == size
+            def partner(i, size=size, stride=stride, bit=bit, mirror=ring and top and size > 2):
+                d = (i // stride) % size
+                e = size - 1 - d if mirror else d ^ bit
+                return i + (e - d) * stride
+            steps.append([(i, partner(i)) for i in range(count)])
+            bit *= 2
+    return steps
+
+
 def total_sums(sums, axes):
-    for axis in axes:
-        count = lax.axis_size(axis)
-        step = 1
-        while step < count:
-            sums = sums + lax.ppermute(sums, axis, [(i, i ^ step) for i in range(count)])
-            step *= 2
+    for axis, digits in axes:
+        for perm in pairings(digits):
+            sums = sums + lax.ppermute(sums, axis, perm)
     return sums
 
 
@@ -80,16 +93,35 @@
     loss_sum = packed[rows, :rows]
     grad_x = scale * packed[:rows]
     grad_y = scale * reduce_by_shift(grad_y_part.reshape(ncol, rows, width), "bx")
-    sums = total_sums(jnp.stack([jnp.sum(slope * raw), jnp.sum(slope)]), ("group", "bx", "bz"))
+    sums = total_sums(jnp.stack([jnp.sum(slope * raw), jnp.sum(slope)]), AXIS_DIGITS)
     set_size = rows * nrow * ncol
     total = jnp.float32(set_size * ngroup) * jnp.float32(set_size)
     loss = loss_sum / set_size
     return (loss, grad_x, grad_y, sums[0] / total, sums[1] / total)
 
 
+AXIS_DIGITS = ()
+
+
+def group_digits(mesh):
+    column = mesh.devices[:, 0]
+    ncore = len({d.core_on_chip for d in column})
+    ny = len({d.coords[1] for d in column})
+    nzh = column.size // (ny * ncore)
+    if ny * nzh * ncore != column.size:
+        return ((column.size, 1, False),)
+    return ((ny, nzh * ncore, True), (nzh, ncore, True), (ncore, 1, False))
+
+
 def split_blk(mesh):
     blk = mesh.devices[0]
     nx = len({d.coords[0] for d in blk})
+    global AXIS_DIGITS
+    AXIS_DIGITS = (
+        ("group", group_digits(mesh)),
+        ("bx", ((nx, 1, True),)),
+        ("bz", ((blk.size // nx, 1, False),)),
+    )
     grid = mesh.devices.reshape(mesh.shape["group"], nx, blk.size // nx)
     return Mesh(grid, ("group", "bx", "bz"))
 

time: 178 us -> 176 us (0.989)
  starting transfers between devices: 109 us -> 101 us
  waiting for transfers between devices: 44.4 us -> 50.3 us
    ppermute x10, starting transfers between devices: 66.5 us -> 55.1 us  [total_sums(): sums = sums + lax.ppermute(sums, axis, perm)]
    ppermute x12, starting transfers between devices: 42.7 us -> 46.2 us  [shifted(): lax.ppermute(value, axis, [(i, (i + by) % count) for i in range(count)])]
    ppermute x10, waiting for transfers between devices: 13.1 us -> 16.2 us  [total_sums(): sums = sums + lax.ppermute(sums, axis, perm)]
    ppermute x12, waiting for transfers between devices: 31.4 us -> 34.1 us  [shifted(): lax.ppermute(value, axis, [(i, (i + by) % count) for i in range(count)])]
where the time goes in v6:
time: 176 us; the launch traced here: 175 us
  starting transfers between devices  101 us (57%)
  waiting for transfers between devices  50.3 us (29%)
  other arithmetic  9.35 us (5%)
  between operations  5.9 us (3%)
  local copies, waits for them, and re-layouts  5.23 us (3%)
  matrix products  2.44 us (1%)
    ppermute x10, starting transfers between devices, total_sums(): sums = sums + lax.ppermute(sums, axis, perm)  55.1 us
    ppermute x12, starting transfers between devices, shifted(): lax.ppermute(value, axis, [(i, (i + by) % count) for i in range(count)])  46.2 us
    ppermute x12, waiting for transfers between devices, shifted(): lax.ppermute(value, axis, [(i, (i + by) % count) for i in range(count)])  34.1 us
    ppermute x10, waiting for transfers between devices, total_sums(): sums = sums + lax.ppermute(sums, axis, perm)  16.2 us
  transfers between devices with their start and end apart: 22, of which 12 were waited for; matrix products, arithmetic and copies ran while one was open for 5% of the time, Pallas kernels for 0%

profile of v6, /device:TPU:1, one launch (start us, length us, event | category | flops | bytes accessed | tf_op | source)
XLA Modules:
  0.0 174.6 jit_solution(14270980407605556722)
XLA Ops:
  0.6 0.0 copy-start
  0.6 0.0 copy-start.1
  0.7 1.1 constant_dynamic-update-slice_fusion.3
  1.8 0.7 and_convert_fusion
  2.6 4.8 %collective-permute-start = (bf16[144,1024]{1,0:T(8,128)(2,1)S(1)}, bf16[144,1024]{1,0:T(8,128)(2,1)}, u32[]{:S(2)}, u32[]{:S(2)}) collective-permute-start(bf16[144,1024]{1,0:T(8,128)(2,1)S(1)} %get-tuple-element.49), channel_id=1, source_target_pairs={{0,1},{1,2},{2,3},{3,0},{4,5},{5,6},{6,7},{7,4},{8,9},{9,10},{10,1... | collective-permute-start | bytes 884744 | tf_op jit(solution)/shard_map/ppermute | solution.py:12
  7.4 5.8 %collective-permute-start.1 = (bf16[144,1024]{1,0:T(8,128)(2,1)S(1)}, bf16[144,1024]{1,0:T(8,128)(2,1)}, u32[]{:S(2)}, u32[]{:S(2)}) collective-permute-start(bf16[144,1024]{1,0:T(8,128)(2,1)S(1)} %get-tuple-element.49), channel_id=1, source_target_pairs={{0,2},{1,3},{2,0},{3,1},{4,6},{5,7},{6,4},{7,5},{8,10},{9,11},{10,... | collective-permute-start | bytes 884744 | tf_op jit(solution)/shard_map/ppermute | solution.py:12
  13.2 2.2 %collective-permute-start.2 = (bf16[144,1024]{1,0:T(8,128)(2,1)S(1)}, bf16[144,1024]{1,0:T(8,128)(2,1)}, u32[]{:S(2)}, u32[]{:S(2)}) collective-permute-start(bf16[144,1024]{1,0:T(8,128)(2,1)S(1)} %get-tuple-element.49), channel_id=1, source_target_pairs={{0,3},{1,0},{2,1},{3,2},{4,7},{5,4},{6,5},{7,6},{8,11},{9,8},{10,9... | collective-permute-start | bytes 884744 | tf_op jit(solution)/shard_map/ppermute | solution.py:12
  15.4 3.1 %collective-permute-start.3 = (bf16[144,1024]{1,0:T(8,128)(2,1)S(1)}, bf16[144,1024]{1,0:T(8,128)(2,1)S(1)}, u32[]{:S(2)}, u32[]{:S(2)}) collective-permute-start(bf16[144,1024]{1,0:T(8,128)(2,1)S(1)} %get-tuple-element.48), channel_id=1, source_target_pairs={{0,4},{4,8},{8,12},{12,0},{1,5},{5,9},{9,13},{13,1},{2,6},{6,10},{... | collective-permute-start | bytes 884744 | tf_op jit(solution)/shard_map/ppermute | solution.py:12
  18.6 4.4 %collective-permute-start.4 = (bf16[144,1024]{1,0:T(8,128)(2,1)S(1)}, bf16[144,1024]{1,0:T(8,128)(2,1)S(1)}, u32[]{:S(2)}, u32[]{:S(2)}) collective-permute-start(bf16[144,1024]{1,0:T(8,128)(2,1)S(1)} %get-tuple-element.48), channel_id=1, source_target_pairs={{0,8},{4,12},{8,0},{12,4},{1,9},{5,13},{9,1},{13,5},{2,10},{6,14},... | collective-permute-start | bytes 884744 | tf_op jit(solution)/shard_map/ppermute | solution.py:12
  24.2 0.0 collective-permute-done
  24.2 3.1 %collective-permute-start.5 = (bf16[144,1024]{1,0:T(8,128)(2,1)S(1)}, bf16[144,1024]{1,0:T(8,128)(2,1)S(1)}, u32[]{:S(2)}, u32[]{:S(2)}) collective-permute-start(bf16[144,1024]{1,0:T(8,128)(2,1)S(1)} %get-tuple-element.48), channel_id=1, source_target_pairs={{0,12},{4,0},{8,4},{12,8},{1,13},{5,1},{9,5},{13,9},{2,14},{6,2},{... | collective-permute-start | bytes 884744 | tf_op jit(solution)/shard_map/ppermute | solution.py:12
  27.3 1.0 constant_dynamic-update-slice_fusion.2
  28.3 0.0 collective-permute-done.1
  28.3 1.0 constant_dynamic-update-slice_fusion.1
  29.3 0.0 collective-permute-done.2
  29.3 1.0 constant_dynamic-update-slice_fusion
  30.3 0.1 slice.164
  30.4 0.0 collective-permute-done.3
  30.4 1.0 collective-permute-done.4
  31.5 0.6 collective-permute-done.5
  32.1 0.1 slice.165
  32.3 1.0 fusion.14
  33.3 1.6 multiply_reduce_fusion
  34.9 1.4 pad_maximum_fusion.2
  36.3 6.2 %collective-permute-start.12 = (f32[2]{0:T(128)S(1)}, f32[2]{0:T(128)S(1)}, u32[]{:S(2)}, u32[]{:S(2)}) collective-permute-start(f32[2]{0:T(128)S(1)} %pad_maximum_fusion.2), channel_id=1, source_target_pairs={{0,128},{16,144},{32,160},{48,176},{64,192},{80,208},{96,224},{112... | collective-permute-start | bytes 32 | tf_op jit(solution)/shard_map/ppermute | solution.py:71
  42.4 0.7 fusion.18
  43.2 0.2 fusion.15
  43.4 4.4 %collective-permute-start.10 = (f32[128,1024]{1,0:T(8,128)S(1)}, f32[128,1024]{1,0:T(8,128)S(1)}, u32[]{:S(2)}, u32[]{:S(2)}) collective-permute-start(f32[128,1024]{1,0:T(8,128)S(1)} %get-tuple-element.47), channel_id=1, source_target_pairs={{0,8},{4,12},{8,0},{12,4},{1,9},{5,13},{9,1},{13,5},{2,10},{6,14},... | collective-permute-start | bytes 1572872 | tf_op jit(solution)/shard_map/ppermute | solution.py:12
  47.8 2.4 %collective-permute-start.11 = (f32[128,1024]{1,0:T(8,128)S(1)}, f32[128,1024]{1,0:T(8,128)S(1)}, u32[]{:S(2)}, u32[]{:S(2)}) collective-permute-start(f32[128,1024]{1,0:T(8,128)S(1)} %get-tuple-element.46), channel_id=1, source_target_pairs={{0,4},{4,8},{8,12},{12,0},{1,5},{5,9},{9,13},{13,1},{2,6},{6,10},{... | collective-permute-start | bytes 1572872 | tf_op jit(solution)/shard_map/ppermute | solution.py:12
  50.2 4.2 %collective-permute-start.9 = (f32[128,1024]{1,0:T(8,128)S(1)}, f32[128,1024]{1,0:T(8,128)S(1)}, u32[]{:S(2)}, u32[]{:S(2)}) collective-permute-start(f32[128,1024]{1,0:T(8,128)S(1)} %get-tuple-element.45), channel_id=1, source_target_pairs={{0,12},{4,0},{8,4},{12,8},{1,13},{5,1},{9,5},{13,9},{2,14},{6,2},{... | collective-permute-start | bytes 1572872 | tf_op jit(solution)/shard_map/ppermute | solution.py:12
  54.4 0.7 fusion.17
  55.2 0.3 select_maximum_fusion
  55.4 0.1 slice_bitcast_fusion.2
  55.6 6.2 %collective-permute-start.6 = (f32[136,1024]{1,0:T(8,128)S(1)}, f32[136,1024]{1,0:T(8,128)S(1)}, u32[]{:S(2)}, u32[]{:S(2)}) collective-permute-start(f32[136,1024]{1,0:T(8,128)S(1)} %get-tuple-element.42), channel_id=1, source_target_pairs={{0,3},{1,0},{2,1},{3,2},{4,7},{5,4},{6,5},{7,6},{8,11},{9,8},{10,9... | collective-permute-start | bytes 1671176 | tf_op jit(solution)/shard_map/ppermute | solution.py:12
  61.8 0.0 collective-permute-done.12
  61.8 1.4 fusion.25
  63.2 4.2 %collective-permute-start.13 = (f32[2]{0:T(128)S(1)}, f32[2]{0:T(128)S(1)}, u32[]{:S(2)}, u32[]{:S(2)}) collective-permute-start(f32[2]{0:T(128)S(1)} %fusion.25), channel_id=1, source_target_pairs={{0,256},{16,272},{32,288},{48,304},{64,320},{80,336},{96,352},{112... | collective-permute-start | bytes 32 | tf_op jit(solution)/shard_map/ppermute | solution.py:71
  67.4 1.3 collective-permute-done.13
  68.7 1.4 fusion.26
  70.0 4.9 %collective-permute-start.14 = (f32[2]{0:T(128)S(1)}, f32[2]{0:T(128)S(1)}, u32[]{:S(2)}, u32[]{:S(2)}) collective-permute-start(f32[2]{0:T(128)S(1)} %fusion.26), channel_id=1, source_target_pairs={{0,896},{16,912},{32,928},{48,944},{64,960},{80,976},{96,992},{112... | collective-permute-start | bytes 32 | tf_op jit(solution)/shard_map/ppermute | solution.py:71
  74.9 0.9 collective-permute-done.14
  75.8 10.6 %collective-permute-start.15 = (f32[2]{0:T(128)S(1)}, f32[2]{0:T(128)S(1)}, u32[]{:S(2)}, u32[]{:S(2)}) collective-permute-start(f32[2]{0:T(128)S(1)} %add.82), channel_id=1, source_target_pairs={{0,32},{16,48},{32,0},{48,16},{64,96},{80,112},{96,64},{112,80},{1... | collective-permute-start | bytes 32 | tf_op jit(solution)/shard_map/ppermute | solution.py:71
  86.5 0.9 collective-permute-done.15
  87.4 12.7 %collective-permute-start.16 = (f32[2]{0:T(128)S(1)}, f32[2]{0:T(128)S(1)}, u32[]{:S(2)}, u32[]{:S(2)}) collective-permute-start(f32[2]{0:T(128)S(1)} %add.83), channel_id=1, source_target_pairs={{0,96},{16,112},{32,64},{48,80},{64,32},{80,48},{96,0},{112,16},{1... | collective-permute-start | bytes 32 | tf_op jit(solution)/shard_map/ppermute | solution.py:71
  100.2 0.9 collective-permute-done.16
  101.1 8.6 %collective-permute-start.17 = (f32[2]{0:T(128)S(1)}, f32[2]{0:T(128)S(1)}, u32[]{:S(2)}, u32[]{:S(2)}) collective-permute-start(f32[2]{0:T(128)S(1)} %add.84), channel_id=1, source_target_pairs={{0,16},{16,0},{32,48},{48,32},{64,80},{80,64},{96,112},{112,96},{1... | collective-permute-start | bytes 32 | tf_op jit(solution)/shard_map/ppermute | solution.py:71
  109.7 0.8 collective-permute-done.17
  110.5 1.9 %collective-permute-start.18 = (f32[2]{0:T(128)S(1)}, f32[2]{0:T(128)S(1)}, u32[]{:S(2)}, u32[]{:S(2)}) collective-permute-start(f32[2]{0:T(128)S(1)} %add.85), channel_id=1, source_target_pairs={{0,4},{4,0},{8,12},{12,8},{1,5},{5,1},{9,13},{13,9},{2,6},{6,2},{1... | collective-permute-start | bytes 32 | tf_op jit(solution)/shard_map/ppermute | solution.py:71
  112.4 2.4 %collective-permute-done.18 = f32[2]{0:T(128)S(1)} collective-permute-done((f32[2]{0:T(128)S(1)}, f32[2]{0:T(128)S(1)}, u32[]{:S(2)}, u32[]{:S(2)}) %collective-permute-start.18) | collective-permute-done | bytes 40 | tf_op jit(solution)/shard_map/ppermute | solution.py:71
  114.8 1.9 %collective-permute-start.19 = (f32[2]{0:T(128)S(1)}, f32[2]{0:T(128)S(1)}, u32[]{:S(2)}, u32[]{:S(2)}) collective-permute-start(f32[2]{0:T(128)S(1)} %add.86), channel_id=1, source_target_pairs={{0,12},{4,8},{8,4},{12,0},{1,13},{5,9},{9,5},{13,1},{2,14},{6,10},... | collective-permute-start | bytes 32 | tf_op jit(solution)/shard_map/ppermute | solution.py:71
  116.7 3.6 %collective-permute-done.19 = f32[2]{0:T(128)S(1)} collective-permute-done((f32[2]{0:T(128)S(1)}, f32[2]{0:T(128)S(1)}, u32[]{:S(2)}, u32[]{:S(2)}) %collective-permute-start.19) | collective-permute-done | bytes 40 | tf_op jit(solution)/shard_map/ppermute | solution.py:71
  120.3 1.9 %collective-permute-start.20 = (f32[2]{0:T(128)S(1)}, f32[2]{0:T(128)S(1)}, u32[]{:S(2)}, u32[]{:S(2)}) collective-permute-start(f32[2]{0:T(128)S(1)} %add.87), channel_id=1, source_target_pairs={{0,1},{1,0},{2,3},{3,2},{4,5},{5,4},{6,7},{7,6},{8,9},{9,8},{10,11... | collective-permute-start | bytes 32 | tf_op jit(solution)/shard_map/ppermute | solution.py:71
  122.2 2.4 %collective-permute-done.20 = f32[2]{0:T(128)S(1)} collective-permute-done((f32[2]{0:T(128)S(1)}, f32[2]{0:T(128)S(1)}, u32[]{:S(2)}, u32[]{:S(2)}) %collective-permute-start.20) | collective-permute-done | bytes 40 | tf_op jit(solution)/shard_map/ppermute | solution.py:71
  124.6 2.2 %collective-permute-start.21 = (f32[2]{0:T(128)S(1)}, f32[2]{0:T(128)S(1)}, u32[]{:S(2)}, u32[]{:S(2)}) collective-permute-start(f32[2]{0:T(128)S(1)} %add.88), channel_id=1, source_target_pairs={{0,2},{1,3},{2,0},{3,1},{4,6},{5,7},{6,4},{7,5},{8,10},{9,11},{10,... | collective-permute-start | bytes 32 | tf_op jit(solution)/shard_map/ppermute | solution.py:71
  126.9 3.0 %collective-permute-done.21 = f32[2]{0:T(128)S(1)} collective-permute-done((f32[2]{0:T(128)S(1)}, f32[2]{0:T(128)S(1)}, u32[]{:S(2)}, u32[]{:S(2)}) %collective-permute-start.21) | collective-permute-done | bytes 40 | tf_op jit(solution)/shard_map/ppermute | solution.py:71
  129.8 2.2 %collective-permute-start.7 = (f32[136,1024]{1,0:T(8,128)S(1)}, f32[136,1024]{1,0:T(8,128)S(1)}, u32[]{:S(2)}, u32[]{:S(2)}) collective-permute-start(f32[136,1024]{1,0:T(8,128)S(1)} %get-tuple-element.44), channel_id=1, source_target_pairs={{0,2},{1,3},{2,0},{3,1},{4,6},{5,7},{6,4},{7,5},{8,10},{9,11},{10,... | collective-permute-start | bytes 1671176 | tf_op jit(solution)/shard_map/ppermute | solution.py:12
  132.1 3.4 %collective-permute-start.8 = (f32[136,1024]{1,0:T(8,128)S(1)}, f32[136,1024]{1,0:T(8,128)S(1)}, u32[]{:S(2)}, u32[]{:S(2)}) collective-permute-start(f32[136,1024]{1,0:T(8,128)S(1)} %get-tuple-element.43), channel_id=1, source_target_pairs={{0,1},{1,2},{2,3},{3,0},{4,5},{5,6},{6,7},{7,4},{8,9},{9,10},{10,1... | collective-permute-start | bytes 1671176 | tf_op jit(solution)/shard_map/ppermute | solution.py:12
  135.5 0.6 fusion.16
  137.3 0.0 collective-permute-done.11
  137.4 1.0 fusion.6
  138.3 32.4 %collective-permute-done.7 = f32[136,1024]{1,0:T(8,128)S(1)} collective-permute-done((f32[136,1024]{1,0:T(8,128)S(1)}, f32[136,1024]{1,0:T(8,128)S(1)}, u32[]{:S(2)}, u32[]{:S(2)}) %collective-permute-start.7) | collective-permute-done | bytes 557088 | tf_op jit(solution)/shard_map/ppermute | solution.py:12
  170.8 0.2 fusion.3
  170.9 0.8 slice_multiply_fusion
  171.8 0.5 fusion.13
  (24 shorter events, 0.2 us)
Async XLA Ops:
  0.6 1.9 %copy-start = (bf16[128,1024]{1,0:T(8,128)(2,1)S(1)}, bf16[128,1024]{1,0:T(8,128)(2,1)}, u32[]{:S(2)}) copy-start(bf16[128,1024]{1,0:T(8,128)(2,1)} %param.11) | copy-start | bytes 786436
  0.6 1.9 %copy-start.1 = (bf16[128,1024]{1,0:T(8,128)(2,1)S(1)}, bf16[128,1024]{1,0:T(8,128)(2,1)}, u32[]{:S(2)}) copy-start(bf16[128,1024]{1,0:T(8,128)(2,1)} %param.12) | copy-start | bytes 786436
  2.6 21.6 %collective-permute-start = (bf16[144,1024]{1,0:T(8,128)(2,1)S(1)}, bf16[144,1024]{1,0:T(8,128)(2,1)}, u32[]{:S(2)}, u32[]{:S(2)}) collective-permute-start(bf16[144,1024]{1,0:T(8,128)(2,1)S(1)} %get-tuple-element.49), channel_id=1, source_target_pairs={{0,1},{1,2},{2,3},{3,0},{4,5},{5,6},{6,7},{7,4},{8,9},{9,10},{10,1... | collective-permute-start | bytes 884744 | tf_op jit(solution)/shard_map/ppermute | solution.py:12
  7.4 20.9 %collective-permute-start.1 = (bf16[144,1024]{1,0:T(8,128)(2,1)S(1)}, bf16[144,1024]{1,0:T(8,128)(2,1)}, u32[]{:S(2)}, u32[]{:S(2)}) collective-permute-start(bf16[144,1024]{1,0:T(8,128)(2,1)S(1)} %get-tuple-element.49), channel_id=1, source_target_pairs={{0,2},{1,3},{2,0},{3,1},{4,6},{5,7},{6,4},{7,5},{8,10},{9,11},{10,... | collective-permute-start | bytes 884744 | tf_op jit(solution)/shard_map/ppermute | solution.py:12
  13.2 16.0 %collective-permute-start.2 = (bf16[144,1024]{1,0:T(8,128)(2,1)S(1)}, bf16[144,1024]{1,0:T(8,128)(2,1)}, u32[]{:S(2)}, u32[]{:S(2)}) collective-permute-start(bf16[144,1024]{1,0:T(8,128)(2,1)S(1)} %get-tuple-element.49), channel_id=1, source_target_pairs={{0,3},{1,0},{2,1},{3,2},{4,7},{5,4},{6,5},{7,6},{8,11},{9,8},{10,9... | collective-permute-start | bytes 884744 | tf_op jit(solution)/shard_map/ppermute | solution.py:12
  15.4 15.0 %collective-permute-start.3 = (bf16[144,1024]{1,0:T(8,128)(2,1)S(1)}, bf16[144,1024]{1,0:T(8,128)(2,1)S(1)}, u32[]{:S(2)}, u32[]{:S(2)}) collective-permute-start(bf16[144,1024]{1,0:T(8,128)(2,1)S(1)} %get-tuple-element.48), channel_id=1, source_target_pairs={{0,4},{4,8},{8,12},{12,0},{1,5},{5,9},{9,13},{13,1},{2,6},{6,10},{... | collective-permute-start | bytes 884744 | tf_op jit(solution)/shard_map/ppermute | solution.py:12
  18.6 12.9 %collective-permute-start.4 = (bf16[144,1024]{1,0:T(8,128)(2,1)S(1)}, bf16[144,1024]{1,0:T(8,128)(2,1)S(1)}, u32[]{:S(2)}, u32[]{:S(2)}) collective-permute-start(bf16[144,1024]{1,0:T(8,128)(2,1)S(1)} %get-tuple-element.48), channel_id=1, source_target_pairs={{0,8},{4,12},{8,0},{12,4},{1,9},{5,13},{9,1},{13,5},{2,10},{6,14},... | collective-permute-start | bytes 884744 | tf_op jit(solution)/shard_map/ppermute | solution.py:12
  24.2 7.9 %collective-permute-start.5 = (bf16[144,1024]{1,0:T(8,128)(2,1)S(1)}, bf16[144,1024]{1,0:T(8,128)(2,1)S(1)}, u32[]{:S(2)}, u32[]{:S(2)}) collective-permute-start(bf16[144,1024]{1,0:T(8,128)(2,1)S(1)} %get-tuple-element.48), channel_id=1, source_target_pairs={{0,12},{4,0},{8,4},{12,8},{1,13},{5,1},{9,5},{13,9},{2,14},{6,2},{... | collective-permute-start | bytes 884744 | tf_op jit(solution)/shard_map/ppermute | solution.py:12
  36.3 25.5 %collective-permute-start.12 = (f32[2]{0:T(128)S(1)}, f32[2]{0:T(128)S(1)}, u32[]{:S(2)}, u32[]{:S(2)}) collective-permute-start(f32[2]{0:T(128)S(1)} %pad_maximum_fusion.2), channel_id=1, source_target_pairs={{0,128},{16,144},{32,160},{48,176},{64,192},{80,208},{96,224},{112... | collective-permute-start | bytes 32 | tf_op jit(solution)/shard_map/ppermute | solution.py:71
  43.4 88.7 %collective-permute-start.10 = (f32[128,1024]{1,0:T(8,128)S(1)}, f32[128,1024]{1,0:T(8,128)S(1)}, u32[]{:S(2)}, u32[]{:S(2)}) collective-permute-start(f32[128,1024]{1,0:T(8,128)S(1)} %get-tuple-element.47), channel_id=1, source_target_pairs={{0,8},{4,12},{8,0},{12,4},{1,9},{5,13},{9,1},{13,5},{2,10},{6,14},... | collective-permute-start | bytes 1572872 | tf_op jit(solution)/shard_map/ppermute | solution.py:12
  47.8 89.5 %collective-permute-start.11 = (f32[128,1024]{1,0:T(8,128)S(1)}, f32[128,1024]{1,0:T(8,128)S(1)}, u32[]{:S(2)}, u32[]{:S(2)}) collective-permute-start(f32[128,1024]{1,0:T(8,128)S(1)} %get-tuple-element.46), channel_id=1, source_target_pairs={{0,4},{4,8},{8,12},{12,0},{1,5},{5,9},{9,13},{13,1},{2,6},{6,10},{... | collective-permute-start | bytes 1572872 | tf_op jit(solution)/shard_map/ppermute | solution.py:12
  50.2 87.2 %collective-permute-start.9 = (f32[128,1024]{1,0:T(8,128)S(1)}, f32[128,1024]{1,0:T(8,128)S(1)}, u32[]{:S(2)}, u32[]{:S(2)}) collective-permute-start(f32[128,1024]{1,0:T(8,128)S(1)} %get-tuple-element.45), channel_id=1, source_target_pairs={{0,12},{4,0},{8,4},{12,8},{1,13},{5,1},{9,5},{13,9},{2,14},{6,2},{... | collective-permute-start | bytes 1572872 | tf_op jit(solution)/shard_map/ppermute | solution.py:12
  55.6 82.7 %collective-permute-start.6 = (f32[136,1024]{1,0:T(8,128)S(1)}, f32[136,1024]{1,0:T(8,128)S(1)}, u32[]{:S(2)}, u32[]{:S(2)}) collective-permute-start(f32[136,1024]{1,0:T(8,128)S(1)} %get-tuple-element.42), channel_id=1, source_target_pairs={{0,3},{1,0},{2,1},{3,2},{4,7},{5,4},{6,5},{7,6},{8,11},{9,8},{10,9... | collective-permute-start | bytes 1671176 | tf_op jit(solution)/shard_map/ppermute | solution.py:12
  63.2 5.5 %collective-permute-start.13 = (f32[2]{0:T(128)S(1)}, f32[2]{0:T(128)S(1)}, u32[]{:S(2)}, u32[]{:S(2)}) collective-permute-start(f32[2]{0:T(128)S(1)} %fusion.25), channel_id=1, source_target_pairs={{0,256},{16,272},{32,288},{48,304},{64,320},{80,336},{96,352},{112... | collective-permute-start | bytes 32 | tf_op jit(solution)/shard_map/ppermute | solution.py:71
  70.0 5.8 %collective-permute-start.14 = (f32[2]{0:T(128)S(1)}, f32[2]{0:T(128)S(1)}, u32[]{:S(2)}, u32[]{:S(2)}) collective-permute-start(f32[2]{0:T(128)S(1)} %fusion.26), channel_id=1, source_target_pairs={{0,896},{16,912},{32,928},{48,944},{64,960},{80,976},{96,992},{112... | collective-permute-start | bytes 32 | tf_op jit(solution)/shard_map/ppermute | solution.py:71
  75.8 11.6 %collective-permute-start.15 = (f32[2]{0:T(128)S(1)}, f32[2]{0:T(128)S(1)}, u32[]{:S(2)}, u32[]{:S(2)}) collective-permute-start(f32[2]{0:T(128)S(1)} %add.82), channel_id=1, source_target_pairs={{0,32},{16,48},{32,0},{48,16},{64,96},{80,112},{96,64},{112,80},{1... | collective-permute-start | bytes 32 | tf_op jit(solution)/shard_map/ppermute | solution.py:71
  87.4 13.7 %collective-permute-start.16 = (f32[2]{0:T(128)S(1)}, f32[2]{0:T(128)S(1)}, u32[]{:S(2)}, u32[]{:S(2)}) collective-permute-start(f32[2]{0:T(128)S(1)} %add.83), channel_id=1, source_target_pairs={{0,96},{16,112},{32,64},{48,80},{64,32},{80,48},{96,0},{112,16},{1... | collective-permute-start | bytes 32 | tf_op jit(solution)/shard_map/ppermute | solution.py:71
  101.1 9.4 %collective-permute-start.17 = (f32[2]{0:T(128)S(1)}, f32[2]{0:T(128)S(1)}, u32[]{:S(2)}, u32[]{:S(2)}) collective-permute-start(f32[2]{0:T(128)S(1)} %add.84), channel_id=1, source_target_pairs={{0,16},{16,0},{32,48},{48,32},{64,80},{80,64},{96,112},{112,96},{1... | collective-permute-start | bytes 32 | tf_op jit(solution)/shard_map/ppermute | solution.py:71
  110.5 4.3 %collective-permute-start.18 = (f32[2]{0:T(128)S(1)}, f32[2]{0:T(128)S(1)}, u32[]{:S(2)}, u32[]{:S(2)}) collective-permute-start(f32[2]{0:T(128)S(1)} %add.85), channel_id=1, source_target_pairs={{0,4},{4,0},{8,12},{12,8},{1,5},{5,1},{9,13},{13,9},{2,6},{6,2},{1... | collective-permute-start | bytes 32 | tf_op jit(solution)/shard_map/ppermute | solution.py:71
  114.8 5.5 %collective-permute-start.19 = (f32[2]{0:T(128)S(1)}, f32[2]{0:T(128)S(1)}, u32[]{:S(2)}, u32[]{:S(2)}) collective-permute-start(f32[2]{0:T(128)S(1)} %add.86), channel_id=1, source_target_pairs={{0,12},{4,8},{8,4},{12,0},{1,13},{5,9},{9,5},{13,1},{2,14},{6,10},... | collective-permute-start | bytes 32 | tf_op jit(solution)/shard_map/ppermute | solution.py:71
  120.3 4.3 %collective-permute-start.20 = (f32[2]{0:T(128)S(1)}, f32[2]{0:T(128)S(1)}, u32[]{:S(2)}, u32[]{:S(2)}) collective-permute-start(f32[2]{0:T(128)S(1)} %add.87), channel_id=1, source_target_pairs={{0,1},{1,0},{2,3},{3,2},{4,5},{5,4},{6,7},{7,6},{8,9},{9,8},{10,11... | collective-permute-start | bytes 32 | tf_op jit(solution)/shard_map/ppermute | solution.py:71
  124.6 5.2 %collective-permute-start.21 = (f32[2]{0:T(128)S(1)}, f32[2]{0:T(128)S(1)}, u32[]{:S(2)}, u32[]{:S(2)}) collective-permute-start(f32[2]{0:T(128)S(1)} %add.88), channel_id=1, source_target_pairs={{0,2},{1,3},{2,0},{3,1},{4,6},{5,7},{6,4},{7,5},{8,10},{9,11},{10,... | collective-permute-start | bytes 32 | tf_op jit(solution)/shard_map/ppermute | solution.py:71
  129.8 40.9 %collective-permute-start.7 = (f32[136,1024]{1,0:T(8,128)S(1)}, f32[136,1024]{1,0:T(8,128)S(1)}, u32[]{:S(2)}, u32[]{:S(2)}) collective-permute-start(f32[136,1024]{1,0:T(8,128)S(1)} %get-tuple-element.44), channel_id=1, source_target_pairs={{0,2},{1,3},{2,0},{3,1},{4,6},{5,7},{6,4},{7,5},{8,10},{9,11},{10,... | collective-permute-start | bytes 1671176 | tf_op jit(solution)/shard_map/ppermute | solution.py:12
  132.1 38.7 %collective-permute-start.8 = (f32[136,1024]{1,0:T(8,128)S(1)}, f32[136,1024]{1,0:T(8,128)S(1)}, u32[]{:S(2)}, u32[]{:S(2)}) collective-permute-start(f32[136,1024]{1,0:T(8,128)S(1)} %get-tuple-element.43), channel_id=1, source_target_pairs={{0,1},{1,2},{2,3},{3,0},{4,5},{5,6},{6,7},{7,4},{8,9},{9,10},{10,1... | collective-permute-start | bytes 1671176 | tf_op jit(solution)/shard_map/ppermute | solution.py:12

commit v7 on v6

--- a/solution.py
+++ b/solution.py
@@ -49,8 +49,7 @@
     return jnp.concatenate([grad_part, tail], axis=1)
 
 
-def pairings(digits):
-    count = math.prod(size for size, _, _ in digits)
+def pairings(digits, count):
     steps = []
     for size, stride, ring in digits:
         bit = 1
@@ -67,7 +66,7 @@
 
 def total_sums(sums, axes):
     for axis, digits in axes:
-        for perm in pairings(digits):
+        for perm in pairings(digits, lax.axis_size(axis)):
             sums = sums + lax.ppermute(sums, axis, perm)
     return sums
 
@@ -109,17 +108,19 @@
     ny = len({d.coords[1] for d in column})
     nzh = column.size // (ny * ncore)
     if ny * nzh * ncore != column.size:
-        return ((column.size, 1, False),)
-    return ((ny, nzh * ncore, True), (nzh, ncore, True), (ncore, 1, False))
+        return ((column.size, 1, False),), ()
+    return ((ncore, 1, False), (ny, nzh * ncore, True)), ((nzh, ncore, True),)
 
 
 def split_blk(mesh):
     blk = mesh.devices[0]
     nx = len({d.coords[0] for d in blk})
     global AXIS_DIGITS
+    early, late = group_digits(mesh)
     AXIS_DIGITS = (
-        ("group", group_digits(mesh)),
+        ("group", early),
         ("bx", ((nx, 1, True),)),
+        ("group", late),
         ("bz", ((blk.size // nx, 1, False),)),
     )
     grid = mesh.devices.reshape(mesh.shape["group"], nx, blk.size // nx)

time: 176 us -> 172 us (0.977)
  the two profiles are of different devices: /device:TPU:1 before, /device:TPU:8 now
where the time goes in v7:
time: 172 us; the launch traced here: 171 us
  starting transfers between devices  93.9 us (55%)
  waiting for transfers between devices  53.9 us (31%)
  other arithmetic  9.35 us (5%)
  between operations  5.9 us (3%)
  local copies, waits for them, and re-layouts  5.23 us (3%)
  matrix products  2.44 us (1%)
    ppermute x10, starting transfers between devices, total_sums(): sums = sums + lax.ppermute(sums, axis, perm)  47.7 us
    ppermute x12, starting transfers between devices, shifted(): lax.ppermute(value, axis, [(i, (i + by) % count) for i in range(count)])  46.2 us
    ppermute x10, waiting for transfers between devices, total_sums(): sums = sums + lax.ppermute(sums, axis, perm)  38.4 us
    ppermute x12, waiting for transfers between devices, shifted(): lax.ppermute(value, axis, [(i, (i + by) % count) for i in range(count)])  15.5 us
  transfers between devices with their start and end apart: 22, of which 13 were waited for; matrix products, arithmetic and copies ran while one was open for 6% of the time, Pallas kernels for 0%

profile of v7, /device:TPU:8, one launch (start us, length us, event | category | flops | bytes accessed | tf_op | source)
XLA Modules:
  0.0 170.7 jit_solution(14035242708206758557)
XLA Ops:
  0.6 0.0 copy-start
  0.6 0.0 copy-start.1
  0.7 1.1 constant_dynamic-update-slice_fusion.3
  1.8 0.7 and_convert_fusion
  2.6 4.3 %collective-permute-start = (bf16[144,1024]{1,0:T(8,128)(2,1)S(1)}, bf16[144,1024]{1,0:T(8,128)(2,1)}, u32[]{:S(2)}, u32[]{:S(2)}) collective-permute-start(bf16[144,1024]{1,0:T(8,128)(2,1)S(1)} %get-tuple-element.49), channel_id=1, source_target_pairs={{0,1},{1,2},{2,3},{3,0},{4,5},{5,6},{6,7},{7,4},{8,9},{9,10},{10,1... | collective-permute-start | bytes 884744 | tf_op jit(solution)/shard_map/ppermute | solution.py:12
  6.9 6.1 %collective-permute-start.1 = (bf16[144,1024]{1,0:T(8,128)(2,1)S(1)}, bf16[144,1024]{1,0:T(8,128)(2,1)}, u32[]{:S(2)}, u32[]{:S(2)}) collective-permute-start(bf16[144,1024]{1,0:T(8,128)(2,1)S(1)} %get-tuple-element.49), channel_id=1, source_target_pairs={{0,2},{1,3},{2,0},{3,1},{4,6},{5,7},{6,4},{7,5},{8,10},{9,11},{10,... | collective-permute-start | bytes 884744 | tf_op jit(solution)/shard_map/ppermute | solution.py:12
  13.0 2.5 %collective-permute-start.2 = (bf16[144,1024]{1,0:T(8,128)(2,1)S(1)}, bf16[144,1024]{1,0:T(8,128)(2,1)}, u32[]{:S(2)}, u32[]{:S(2)}) collective-permute-start(bf16[144,1024]{1,0:T(8,128)(2,1)S(1)} %get-tuple-element.49), channel_id=1, source_target_pairs={{0,3},{1,0},{2,1},{3,2},{4,7},{5,4},{6,5},{7,6},{8,11},{9,8},{10,9... | collective-permute-start | bytes 884744 | tf_op jit(solution)/shard_map/ppermute | solution.py:12
  15.5 3.4 %collective-permute-start.3 = (bf16[144,1024]{1,0:T(8,128)(2,1)S(1)}, bf16[144,1024]{1,0:T(8,128)(2,1)S(1)}, u32[]{:S(2)}, u32[]{:S(2)}) collective-permute-start(bf16[144,1024]{1,0:T(8,128)(2,1)S(1)} %get-tuple-element.48), channel_id=1, source_target_pairs={{0,4},{4,8},{8,12},{12,0},{1,5},{5,9},{9,13},{13,1},{2,6},{6,10},{... | collective-permute-start | bytes 884744 | tf_op jit(solution)/shard_map/ppermute | solution.py:12
  18.9 4.6 %collective-permute-start.4 = (bf16[144,1024]{1,0:T(8,128)(2,1)S(1)}, bf16[144,1024]{1,0:T(8,128)(2,1)S(1)}, u32[]{:S(2)}, u32[]{:S(2)}) collective-permute-start(bf16[144,1024]{1,0:T(8,128)(2,1)S(1)} %get-tuple-element.48), channel_id=1, source_target_pairs={{0,8},{4,12},{8,0},{12,4},{1,9},{5,13},{9,1},{13,5},{2,10},{6,14},... | collective-permute-start | bytes 884744 | tf_op jit(solution)/shard_map/ppermute | solution.py:12
  24.8 0.0 collective-permute-done
  24.8 3.3 %collective-permute-start.5 = (bf16[144,1024]{1,0:T(8,128)(2,1)S(1)}, bf16[144,1024]{1,0:T(8,128)(2,1)S(1)}, u32[]{:S(2)}, u32[]{:S(2)}) collective-permute-start(bf16[144,1024]{1,0:T(8,128)(2,1)S(1)} %get-tuple-element.48), channel_id=1, source_target_pairs={{0,12},{4,0},{8,4},{12,8},{1,13},{5,1},{9,5},{13,9},{2,14},{6,2},{... | collective-permute-start | bytes 884744 | tf_op jit(solution)/shard_map/ppermute | solution.py:12
  28.2 1.0 constant_dynamic-update-slice_fusion.2
  29.1 1.2 collective-permute-done.1
  30.3 1.0 constant_dynamic-update-slice_fusion.1
  31.3 1.0 constant_dynamic-update-slice_fusion
  32.3 0.1 slice.164
  32.5 1.3 collective-permute-done.4
  33.8 1.5 collective-permute-done.5
  35.3 0.1 slice.165
  35.5 1.0 fusion.14
  36.5 1.6 multiply_reduce_fusion
  38.1 1.4 pad_maximum_fusion.2
  39.5 1.9 %collective-permute-start.12 = (f32[2]{0:T(128)S(1)}, f32[2]{0:T(128)S(1)}, u32[]{:S(2)}, u32[]{:S(2)}) collective-permute-start(f32[2]{0:T(128)S(1)} %pad_maximum_fusion.2), channel_id=1, source_target_pairs={{0,16},{16,0},{32,48},{48,32},{64,80},{80,64},{96,112},{112,96},{1... | collective-permute-start | bytes 32 | tf_op jit(solution)/shard_map/ppermute | solution.py:70
  41.4 0.7 fusion.18
  42.1 0.2 fusion.15
  42.3 4.9 %collective-permute-start.10 = (f32[128,1024]{1,0:T(8,128)S(1)}, f32[128,1024]{1,0:T(8,128)S(1)}, u32[]{:S(2)}, u32[]{:S(2)}) collective-permute-start(f32[128,1024]{1,0:T(8,128)S(1)} %get-tuple-element.47), channel_id=1, source_target_pairs={{0,8},{4,12},{8,0},{12,4},{1,9},{5,13},{9,1},{13,5},{2,10},{6,14},... | collective-permute-start | bytes 1572872 | tf_op jit(solution)/shard_map/ppermute | solution.py:12
  47.2 2.4 %collective-permute-start.11 = (f32[128,1024]{1,0:T(8,128)S(1)}, f32[128,1024]{1,0:T(8,128)S(1)}, u32[]{:S(2)}, u32[]{:S(2)}) collective-permute-start(f32[128,1024]{1,0:T(8,128)S(1)} %get-tuple-element.46), channel_id=1, source_target_pairs={{0,4},{4,8},{8,12},{12,0},{1,5},{5,9},{9,13},{13,1},{2,6},{6,10},{... | collective-permute-start | bytes 1572872 | tf_op jit(solution)/shard_map/ppermute | solution.py:12
  49.6 4.6 %collective-permute-start.9 = (f32[128,1024]{1,0:T(8,128)S(1)}, f32[128,1024]{1,0:T(8,128)S(1)}, u32[]{:S(2)}, u32[]{:S(2)}) collective-permute-start(f32[128,1024]{1,0:T(8,128)S(1)} %get-tuple-element.45), channel_id=1, source_target_pairs={{0,12},{4,0},{8,4},{12,8},{1,13},{5,1},{9,5},{13,9},{2,14},{6,2},{... | collective-permute-start | bytes 1572872 | tf_op jit(solution)/shard_map/ppermute | solution.py:12
  54.3 0.7 fusion.17
  55.0 0.3 select_maximum_fusion
  55.3 0.1 slice_bitcast_fusion.2
  55.4 6.2 %collective-permute-start.6 = (f32[136,1024]{1,0:T(8,128)S(1)}, f32[136,1024]{1,0:T(8,128)S(1)}, u32[]{:S(2)}, u32[]{:S(2)}) collective-permute-start(f32[136,1024]{1,0:T(8,128)S(1)} %get-tuple-element.42), channel_id=1, source_target_pairs={{0,3},{1,0},{2,1},{3,2},{4,7},{5,4},{6,5},{7,6},{8,11},{9,8},{10,9... | collective-permute-start | bytes 1671176 | tf_op jit(solution)/shard_map/ppermute | solution.py:12
  61.7 0.0 collective-permute-done.12
  61.7 1.4 fusion.25
  63.0 2.5 %collective-permute-start.13 = (f32[2]{0:T(128)S(1)}, f32[2]{0:T(128)S(1)}, u32[]{:S(2)}, u32[]{:S(2)}) collective-permute-start(f32[2]{0:T(128)S(1)} %fusion.25), channel_id=1, source_target_pairs={{0,128},{16,144},{32,160},{48,176},{64,192},{80,208},{96,224},{112... | collective-permute-start | bytes 32 | tf_op jit(solution)/shard_map/ppermute | solution.py:70
  65.6 2.9 %collective-permute-done.13 = f32[2]{0:T(128)S(1)} collective-permute-done((f32[2]{0:T(128)S(1)}, f32[2]{0:T(128)S(1)}, u32[]{:S(2)}, u32[]{:S(2)}) %collective-permute-start.13) | collective-permute-done | bytes 40 | tf_op jit(solution)/shard_map/ppermute | solution.py:70
  68.5 1.4 fusion.26
  69.9 4.5 %collective-permute-start.14 = (f32[2]{0:T(128)S(1)}, f32[2]{0:T(128)S(1)}, u32[]{:S(2)}, u32[]{:S(2)}) collective-permute-start(f32[2]{0:T(128)S(1)} %fusion.26), channel_id=1, source_target_pairs={{0,256},{16,272},{32,288},{48,304},{64,320},{80,336},{96,352},{112... | collective-permute-start | bytes 32 | tf_op jit(solution)/shard_map/ppermute | solution.py:70
  74.4 1.9 %collective-permute-done.14 = f32[2]{0:T(128)S(1)} collective-permute-done((f32[2]{0:T(128)S(1)}, f32[2]{0:T(128)S(1)}, u32[]{:S(2)}, u32[]{:S(2)}) %collective-permute-start.14) | collective-permute-done | bytes 40 | tf_op jit(solution)/shard_map/ppermute | solution.py:70
  76.2 6.0 %collective-permute-start.15 = (f32[2]{0:T(128)S(1)}, f32[2]{0:T(128)S(1)}, u32[]{:S(2)}, u32[]{:S(2)}) collective-permute-start(f32[2]{0:T(128)S(1)} %add.82), channel_id=1, source_target_pairs={{0,896},{16,912},{32,928},{48,944},{64,960},{80,976},{96,992},{112... | collective-permute-start | bytes 32 | tf_op jit(solution)/shard_map/ppermute | solution.py:70
  82.3 2.4 %collective-permute-done.15 = f32[2]{0:T(128)S(1)} collective-permute-done((f32[2]{0:T(128)S(1)}, f32[2]{0:T(128)S(1)}, u32[]{:S(2)}, u32[]{:S(2)}) %collective-permute-start.15) | collective-permute-done | bytes 40 | tf_op jit(solution)/shard_map/ppermute | solution.py:70
  84.7 1.9 %collective-permute-start.16 = (f32[2]{0:T(128)S(1)}, f32[2]{0:T(128)S(1)}, u32[]{:S(2)}, u32[]{:S(2)}) collective-permute-start(f32[2]{0:T(128)S(1)} %add.83), channel_id=1, source_target_pairs={{0,4},{4,0},{8,12},{12,8},{1,5},{5,1},{9,13},{13,9},{2,6},{6,2},{1... | collective-permute-start | bytes 32 | tf_op jit(solution)/shard_map/ppermute | solution.py:70
  86.6 3.5 %collective-permute-done.16 = f32[2]{0:T(128)S(1)} collective-permute-done((f32[2]{0:T(128)S(1)}, f32[2]{0:T(128)S(1)}, u32[]{:S(2)}, u32[]{:S(2)}) %collective-permute-start.16) | collective-permute-done | bytes 40 | tf_op jit(solution)/shard_map/ppermute | solution.py:70
  90.1 2.4 %collective-permute-start.17 = (f32[2]{0:T(128)S(1)}, f32[2]{0:T(128)S(1)}, u32[]{:S(2)}, u32[]{:S(2)}) collective-permute-start(f32[2]{0:T(128)S(1)} %add.84), channel_id=1, source_target_pairs={{0,12},{4,8},{8,4},{12,0},{1,13},{5,9},{9,5},{13,1},{2,14},{6,10},... | collective-permute-start | bytes 32 | tf_op jit(solution)/shard_map/ppermute | solution.py:70
  92.6 4.2 %collective-permute-done.17 = f32[2]{0:T(128)S(1)} collective-permute-done((f32[2]{0:T(128)S(1)}, f32[2]{0:T(128)S(1)}, u32[]{:S(2)}, u32[]{:S(2)}) %collective-permute-start.17) | collective-permute-done | bytes 40 | tf_op jit(solution)/shard_map/ppermute | solution.py:70
  96.8 10.9 %collective-permute-start.18 = (f32[2]{0:T(128)S(1)}, f32[2]{0:T(128)S(1)}, u32[]{:S(2)}, u32[]{:S(2)}) collective-permute-start(f32[2]{0:T(128)S(1)} %add.85), channel_id=1, source_target_pairs={{0,32},{16,48},{32,0},{48,16},{64,96},{80,112},{96,64},{112,80},{1... | collective-permute-start | bytes 32 | tf_op jit(solution)/shard_map/ppermute | solution.py:70
  107.7 1.5 collective-permute-done.18
  109.2 13.3 %collective-permute-start.19 = (f32[2]{0:T(128)S(1)}, f32[2]{0:T(128)S(1)}, u32[]{:S(2)}, u32[]{:S(2)}) collective-permute-start(f32[2]{0:T(128)S(1)} %add.86), channel_id=1, source_target_pairs={{0,96},{16,112},{32,64},{48,80},{64,32},{80,48},{96,0},{112,16},{1... | collective-permute-start | bytes 32 | tf_op jit(solution)/shard_map/ppermute | solution.py:70
  122.6 1.5 collective-permute-done.19
  124.1 1.9 %collective-permute-start.20 = (f32[2]{0:T(128)S(1)}, f32[2]{0:T(128)S(1)}, u32[]{:S(2)}, u32[]{:S(2)}) collective-permute-start(f32[2]{0:T(128)S(1)} %add.87), channel_id=1, source_target_pairs={{0,1},{1,0},{2,3},{3,2},{4,5},{5,4},{6,7},{7,6},{8,9},{9,8},{10,11... | collective-permute-start | bytes 32 | tf_op jit(solution)/shard_map/ppermute | solution.py:70
  126.0 3.5 %collective-permute-done.20 = f32[2]{0:T(128)S(1)} collective-permute-done((f32[2]{0:T(128)S(1)}, f32[2]{0:T(128)S(1)}, u32[]{:S(2)}, u32[]{:S(2)}) %collective-permute-start.20) | collective-permute-done | bytes 40 | tf_op jit(solution)/shard_map/ppermute | solution.py:70
  129.5 2.2 %collective-permute-start.21 = (f32[2]{0:T(128)S(1)}, f32[2]{0:T(128)S(1)}, u32[]{:S(2)}, u32[]{:S(2)}) collective-permute-start(f32[2]{0:T(128)S(1)} %add.88), channel_id=1, source_target_pairs={{0,2},{1,3},{2,0},{3,1},{4,6},{5,7},{6,4},{7,5},{8,10},{9,11},{10,... | collective-permute-start | bytes 32 | tf_op jit(solution)/shard_map/ppermute | solution.py:70
  131.8 16.8 %collective-permute-done.21 = f32[2]{0:T(128)S(1)} collective-permute-done((f32[2]{0:T(128)S(1)}, f32[2]{0:T(128)S(1)}, u32[]{:S(2)}, u32[]{:S(2)}) %collective-permute-start.21) | collective-permute-done | bytes 40 | tf_op jit(solution)/shard_map/ppermute | solution.py:70
  148.6 1.9 %collective-permute-start.7 = (f32[136,1024]{1,0:T(8,128)S(1)}, f32[136,1024]{1,0:T(8,128)S(1)}, u32[]{:S(2)}, u32[]{:S(2)}) collective-permute-start(f32[136,1024]{1,0:T(8,128)S(1)} %get-tuple-element.44), channel_id=1, source_target_pairs={{0,2},{1,3},{2,0},{3,1},{4,6},{5,7},{6,4},{7,5},{8,10},{9,11},{10,... | collective-permute-start | bytes 1671176 | tf_op jit(solution)/shard_map/ppermute | solution.py:12
  150.5 0.0 collective-permute-done.10
  150.6 1.9 %collective-permute-start.8 = (f32[136,1024]{1,0:T(8,128)S(1)}, f32[136,1024]{1,0:T(8,128)S(1)}, u32[]{:S(2)}, u32[]{:S(2)}) collective-permute-start(f32[136,1024]{1,0:T(8,128)S(1)} %get-tuple-element.43), channel_id=1, source_target_pairs={{0,1},{1,2},{2,3},{3,0},{4,5},{5,6},{6,7},{7,4},{8,9},{9,10},{10,1... | collective-permute-start | bytes 1671176 | tf_op jit(solution)/shard_map/ppermute | solution.py:12
  152.5 0.6 fusion.16
  154.4 0.0 collective-permute-done.11
  154.4 0.0 collective-permute-done.9
  154.4 1.0 fusion.6
  155.4 11.6 %collective-permute-done.7 = f32[136,1024]{1,0:T(8,128)S(1)} collective-permute-done((f32[136,1024]{1,0:T(8,128)S(1)}, f32[136,1024]{1,0:T(8,128)S(1)}, u32[]{:S(2)}, u32[]{:S(2)}) %collective-permute-start.7) | collective-permute-done | bytes 557088 | tf_op jit(solution)/shard_map/ppermute | solution.py:12
  166.9 0.2 fusion.3
  167.1 0.8 slice_multiply_fusion
  167.9 0.5 fusion.13
  (24 shorter events, 0.2 us)
Async XLA Ops:
  0.6 1.9 %copy-start = (bf16[128,1024]{1,0:T(8,128)(2,1)S(1)}, bf16[128,1024]{1,0:T(8,128)(2,1)}, u32[]{:S(2)}) copy-start(bf16[128,1024]{1,0:T(8,128)(2,1)} %param.11) | copy-start | bytes 786436
  0.6 1.9 %copy-start.1 = (bf16[128,1024]{1,0:T(8,128)(2,1)S(1)}, bf16[128,1024]{1,0:T(8,128)(2,1)}, u32[]{:S(2)}) copy-start(bf16[128,1024]{1,0:T(8,128)(2,1)} %param.12) | copy-start | bytes 786436
  2.6 22.2 %collective-permute-start = (bf16[144,1024]{1,0:T(8,128)(2,1)S(1)}, bf16[144,1024]{1,0:T(8,128)(2,1)}, u32[]{:S(2)}, u32[]{:S(2)}) collective-permute-start(bf16[144,1024]{1,0:T(8,128)(2,1)S(1)} %get-tuple-element.49), channel_id=1, source_target_pairs={{0,1},{1,2},{2,3},{3,0},{4,5},{5,6},{6,7},{7,4},{8,9},{9,10},{10,1... | collective-permute-start | bytes 884744 | tf_op jit(solution)/shard_map/ppermute | solution.py:12
  6.9 23.4 %collective-permute-start.1 = (bf16[144,1024]{1,0:T(8,128)(2,1)S(1)}, bf16[144,1024]{1,0:T(8,128)(2,1)}, u32[]{:S(2)}, u32[]{:S(2)}) collective-permute-start(bf16[144,1024]{1,0:T(8,128)(2,1)S(1)} %get-tuple-element.49), channel_id=1, source_target_pairs={{0,2},{1,3},{2,0},{3,1},{4,6},{5,7},{6,4},{7,5},{8,10},{9,11},{10,... | collective-permute-start | bytes 884744 | tf_op jit(solution)/shard_map/ppermute | solution.py:12
  13.0 18.3 %collective-permute-start.2 = (bf16[144,1024]{1,0:T(8,128)(2,1)S(1)}, bf16[144,1024]{1,0:T(8,128)(2,1)}, u32[]{:S(2)}, u32[]{:S(2)}) collective-permute-start(bf16[144,1024]{1,0:T(8,128)(2,1)S(1)} %get-tuple-element.49), channel_id=1, source_target_pairs={{0,3},{1,0},{2,1},{3,2},{4,7},{5,4},{6,5},{7,6},{8,11},{9,8},{10,9... | collective-permute-start | bytes 884744 | tf_op jit(solution)/shard_map/ppermute | solution.py:12
  15.5 17.0 %collective-permute-start.3 = (bf16[144,1024]{1,0:T(8,128)(2,1)S(1)}, bf16[144,1024]{1,0:T(8,128)(2,1)S(1)}, u32[]{:S(2)}, u32[]{:S(2)}) collective-permute-start(bf16[144,1024]{1,0:T(8,128)(2,1)S(1)} %get-tuple-element.48), channel_id=1, source_target_pairs={{0,4},{4,8},{8,12},{12,0},{1,5},{5,9},{9,13},{13,1},{2,6},{6,10},{... | collective-permute-start | bytes 884744 | tf_op jit(solution)/shard_map/ppermute | solution.py:12
  18.9 14.9 %collective-permute-start.4 = (bf16[144,1024]{1,0:T(8,128)(2,1)S(1)}, bf16[144,1024]{1,0:T(8,128)(2,1)S(1)}, u32[]{:S(2)}, u32[]{:S(2)}) collective-permute-start(bf16[144,1024]{1,0:T(8,128)(2,1)S(1)} %get-tuple-element.48), channel_id=1, source_target_pairs={{0,8},{4,12},{8,0},{12,4},{1,9},{5,13},{9,1},{13,5},{2,10},{6,14},... | collective-permute-start | bytes 884744 | tf_op jit(solution)/shard_map/ppermute | solution.py:12
  24.8 10.5 %collective-permute-start.5 = (bf16[144,1024]{1,0:T(8,128)(2,1)S(1)}, bf16[144,1024]{1,0:T(8,128)(2,1)S(1)}, u32[]{:S(2)}, u32[]{:S(2)}) collective-permute-start(bf16[144,1024]{1,0:T(8,128)(2,1)S(1)} %get-tuple-element.48), channel_id=1, source_target_pairs={{0,12},{4,0},{8,4},{12,8},{1,13},{5,1},{9,5},{13,9},{2,14},{6,2},{... | collective-permute-start | bytes 884744 | tf_op jit(solution)/shard_map/ppermute | solution.py:12
  39.5 22.2 %collective-permute-start.12 = (f32[2]{0:T(128)S(1)}, f32[2]{0:T(128)S(1)}, u32[]{:S(2)}, u32[]{:S(2)}) collective-permute-start(f32[2]{0:T(128)S(1)} %pad_maximum_fusion.2), channel_id=1, source_target_pairs={{0,16},{16,0},{32,48},{48,32},{64,80},{80,64},{96,112},{112,96},{1... | collective-permute-start | bytes 32 | tf_op jit(solution)/shard_map/ppermute | solution.py:70
  42.3 108.3 %collective-permute-start.10 = (f32[128,1024]{1,0:T(8,128)S(1)}, f32[128,1024]{1,0:T(8,128)S(1)}, u32[]{:S(2)}, u32[]{:S(2)}) collective-permute-start(f32[128,1024]{1,0:T(8,128)S(1)} %get-tuple-element.47), channel_id=1, source_target_pairs={{0,8},{4,12},{8,0},{12,4},{1,9},{5,13},{9,1},{13,5},{2,10},{6,14},... | collective-permute-start | bytes 1572872 | tf_op jit(solution)/shard_map/ppermute | solution.py:12
  47.2 107.2 %collective-permute-start.11 = (f32[128,1024]{1,0:T(8,128)S(1)}, f32[128,1024]{1,0:T(8,128)S(1)}, u32[]{:S(2)}, u32[]{:S(2)}) collective-permute-start(f32[128,1024]{1,0:T(8,128)S(1)} %get-tuple-element.46), channel_id=1, source_target_pairs={{0,4},{4,8},{8,12},{12,0},{1,5},{5,9},{9,13},{13,1},{2,6},{6,10},{... | collective-permute-start | bytes 1572872 | tf_op jit(solution)/shard_map/ppermute | solution.py:12
  49.6 104.7 %collective-permute-start.9 = (f32[128,1024]{1,0:T(8,128)S(1)}, f32[128,1024]{1,0:T(8,128)S(1)}, u32[]{:S(2)}, u32[]{:S(2)}) collective-permute-start(f32[128,1024]{1,0:T(8,128)S(1)} %get-tuple-element.45), channel_id=1, source_target_pairs={{0,12},{4,0},{8,4},{12,8},{1,13},{5,1},{9,5},{13,9},{2,14},{6,2},{... | collective-permute-start | bytes 1572872 | tf_op jit(solution)/shard_map/ppermute | solution.py:12
  55.4 99.9 %collective-permute-start.6 = (f32[136,1024]{1,0:T(8,128)S(1)}, f32[136,1024]{1,0:T(8,128)S(1)}, u32[]{:S(2)}, u32[]{:S(2)}) collective-permute-start(f32[136,1024]{1,0:T(8,128)S(1)} %get-tuple-element.42), channel_id=1, source_target_pairs={{0,3},{1,0},{2,1},{3,2},{4,7},{5,4},{6,5},{7,6},{8,11},{9,8},{10,9... | collective-permute-start | bytes 1671176 | tf_op jit(solution)/shard_map/ppermute | solution.py:12
  63.0 5.5 %collective-permute-start.13 = (f32[2]{0:T(128)S(1)}, f32[2]{0:T(128)S(1)}, u32[]{:S(2)}, u32[]{:S(2)}) collective-permute-start(f32[2]{0:T(128)S(1)} %fusion.25), channel_id=1, source_target_pairs={{0,128},{16,144},{32,160},{48,176},{64,192},{80,208},{96,224},{112... | collective-permute-start | bytes 32 | tf_op jit(solution)/shard_map/ppermute | solution.py:70
  69.9 6.3 %collective-permute-start.14 = (f32[2]{0:T(128)S(1)}, f32[2]{0:T(128)S(1)}, u32[]{:S(2)}, u32[]{:S(2)}) collective-permute-start(f32[2]{0:T(128)S(1)} %fusion.26), channel_id=1, source_target_pairs={{0,256},{16,272},{32,288},{48,304},{64,320},{80,336},{96,352},{112... | collective-permute-start | bytes 32 | tf_op jit(solution)/shard_map/ppermute | solution.py:70
  76.2 8.5 %collective-permute-start.15 = (f32[2]{0:T(128)S(1)}, f32[2]{0:T(128)S(1)}, u32[]{:S(2)}, u32[]{:S(2)}) collective-permute-start(f32[2]{0:T(128)S(1)} %add.82), channel_id=1, source_target_pairs={{0,896},{16,912},{32,928},{48,944},{64,960},{80,976},{96,992},{112... | collective-permute-start | bytes 32 | tf_op jit(solution)/shard_map/ppermute | solution.py:70
  84.7 5.5 %collective-permute-start.16 = (f32[2]{0:T(128)S(1)}, f32[2]{0:T(128)S(1)}, u32[]{:S(2)}, u32[]{:S(2)}) collective-permute-start(f32[2]{0:T(128)S(1)} %add.83), channel_id=1, source_target_pairs={{0,4},{4,0},{8,12},{12,8},{1,5},{5,1},{9,13},{13,9},{2,6},{6,2},{1... | collective-permute-start | bytes 32 | tf_op jit(solution)/shard_map/ppermute | solution.py:70
  90.1 6.7 %collective-permute-start.17 = (f32[2]{0:T(128)S(1)}, f32[2]{0:T(128)S(1)}, u32[]{:S(2)}, u32[]{:S(2)}) collective-permute-start(f32[2]{0:T(128)S(1)} %add.84), channel_id=1, source_target_pairs={{0,12},{4,8},{8,4},{12,0},{1,13},{5,9},{9,5},{13,1},{2,14},{6,10},... | collective-permute-start | bytes 32 | tf_op jit(solution)/shard_map/ppermute | solution.py:70
  96.8 12.4 %collective-permute-start.18 = (f32[2]{0:T(128)S(1)}, f32[2]{0:T(128)S(1)}, u32[]{:S(2)}, u32[]{:S(2)}) collective-permute-start(f32[2]{0:T(128)S(1)} %add.85), channel_id=1, source_target_pairs={{0,32},{16,48},{32,0},{48,16},{64,96},{80,112},{96,64},{112,80},{1... | collective-permute-start | bytes 32 | tf_op jit(solution)/shard_map/ppermute | solution.py:70
  109.2 14.8 %collective-permute-start.19 = (f32[2]{0:T(128)S(1)}, f32[2]{0:T(128)S(1)}, u32[]{:S(2)}, u32[]{:S(2)}) collective-permute-start(f32[2]{0:T(128)S(1)} %add.86), channel_id=1, source_target_pairs={{0,96},{16,112},{32,64},{48,80},{64,32},{80,48},{96,0},{112,16},{1... | collective-permute-start | bytes 32 | tf_op jit(solution)/shard_map/ppermute | solution.py:70
  124.1 5.5 %collective-permute-start.20 = (f32[2]{0:T(128)S(1)}, f32[2]{0:T(128)S(1)}, u32[]{:S(2)}, u32[]{:S(2)}) collective-permute-start(f32[2]{0:T(128)S(1)} %add.87), channel_id=1, source_target_pairs={{0,1},{1,0},{2,3},{3,2},{4,5},{5,4},{6,7},{7,6},{8,9},{9,8},{10,11... | collective-permute-start | bytes 32 | tf_op jit(solution)/shard_map/ppermute | solution.py:70
  129.5 19.1 %collective-permute-start.21 = (f32[2]{0:T(128)S(1)}, f32[2]{0:T(128)S(1)}, u32[]{:S(2)}, u32[]{:S(2)}) collective-permute-start(f32[2]{0:T(128)S(1)} %add.88), channel_id=1, source_target_pairs={{0,2},{1,3},{2,0},{3,1},{4,6},{5,7},{6,4},{7,5},{8,10},{9,11},{10,... | collective-permute-start | bytes 32 | tf_op jit(solution)/shard_map/ppermute | solution.py:70
  148.6 18.3 %collective-permute-start.7 = (f32[136,1024]{1,0:T(8,128)S(1)}, f32[136,1024]{1,0:T(8,128)S(1)}, u32[]{:S(2)}, u32[]{:S(2)}) collective-permute-start(f32[136,1024]{1,0:T(8,128)S(1)} %get-tuple-element.44), channel_id=1, source_target_pairs={{0,2},{1,3},{2,0},{3,1},{4,6},{5,7},{6,4},{7,5},{8,10},{9,11},{10,... | collective-permute-start | bytes 1671176 | tf_op jit(solution)/shard_map/ppermute | solution.py:12
  150.6 16.4 %collective-permute-start.8 = (f32[136,1024]{1,0:T(8,128)S(1)}, f32[136,1024]{1,0:T(8,128)S(1)}, u32[]{:S(2)}, u32[]{:S(2)}) collective-permute-start(f32[136,1024]{1,0:T(8,128)S(1)} %get-tuple-element.43), channel_id=1, source_target_pairs={{0,1},{1,2},{2,3},{3,0},{4,5},{5,6},{6,7},{7,4},{8,9},{9,10},{10,1... | collective-permute-start | bytes 1671176 | tf_op jit(solution)/shard_map/ppermute | solution.py:12
